TPU v7x, 256 devices: a whole 4x4x8 slice. The times are simulated.
256 devices in a mesh: ctx: 64 (over z, y_hi, x), head: 4 (over y_lo, core).
Axes of the slice: x: 4, y: 4 (y_hi: 2, y_lo: 2; y = y_hi * 2 + y_lo), z: 8, core: 2. Of those that a mesh axis runs over, the one named last changes fastest.
Arguments:
- query_rows: bfloat16 [32768, 5120], P(('ctx', 'head')), may hold values from -6 to 6
- key_rows: bfloat16 [32768, 1024], P(('ctx', 'head')), may hold values from -6 to 6
- value_rows: bfloat16 [32768, 1024], P(('ctx', 'head')), may hold values from -6 to 6
- attn_output: bfloat16 [32768, 5120], P(('ctx', 'head')), may hold values from -3 to 3
- out_grad: bfloat16 [32768, 5120], P(('ctx', 'head')), may hold values from -24 to 24
- log_norm: float32 [40, 32768], P('head', 'ctx'), may hold values from 5 to 7
- prefix_keys: bfloat16 [1024, 1024], P('ctx', 'head'), may hold values from -6 to 6
- prefix_values: bfloat16 [1024, 1024], P('ctx', 'head'), may hold values from -6 to 6
- response_blocks: int32 [128], replicated, may hold values from 1 to 16, as said below
- prompt_members: int32 [8, 16], replicated, may hold values from 0 to 127, as said below
Outputs:
- query_grad: bfloat16 [32768, 5120], P('ctx', 'head')
- key_grad: bfloat16 [32768, 1024], P('ctx', 'head')
- value_grad: bfloat16 [32768, 1024], P('ctx', 'head')
- prefix_keygrads: bfloat16 [1024, 1024], P('ctx', 'head')
- prefix_valuegrads: bfloat16 [1024, 1024], P('ctx', 'head')
Inputs may be any that keep to these rules, and one draw needn't show every extreme that they name: `response_blocks`: the lengths fill all 1024 blocks of the row. Every index of ctx from 1 on begins inside a response that started on the index before it. `prompt_members`: every response, numbered 0 to 127 in order along the row, is listed exactly once.
All inputs are finite; a program needn't handle non-finite values.
Results may differ from a plain program's by a relative error of at most 0.008.
Values may be sent and summed in bfloat16 or wider, within the bound.
No kernel may reach another device: no remote copies, remote signals or barrier semaphores. Data moves between devices by JAX's collectives and lax.ppermute only.
A program may use at most 64 MiB of HBM per device.

v0:
```python
import math

import jax
import jax.numpy as jnp
from jax import lax
from jax.sharding import PartitionSpec as P

HD = 128
BLK = 32
PL = 128


def shifted(array, axis, by):
    devices = lax.axis_size(axis)
    pairs = [(i, i + by) for i in range(devices) if 0 <= i + by < devices]
    return lax.ppermute(array, axis, pairs)


def token_tables(response_blocks, prompt_members, first_block, count):
    starts = jnp.cumsum(response_blocks) - response_blocks
    responses = response_blocks.shape[0]
    group = prompt_members.shape[1]
    listed = prompt_members.reshape(-1)
    owner = jnp.arange(listed.shape[0], dtype=jnp.int32) // group
    numbers = jnp.arange(responses, dtype=jnp.int32)
    hits = listed[:, None] == numbers[None, :]
    prompt_of = jnp.sum(jnp.where(hits, owner[:, None], 0), axis=0)
    blocks = first_block + jnp.arange(count, dtype=jnp.int32)
    before = starts[None, :] <= blocks[:, None]
    first = jnp.max(jnp.where(before, starts[None, :], 0), axis=1)
    current = jnp.sum(before.astype(jnp.int32), axis=1) - 1
    chosen = numbers[None, :] == current[:, None]
    prompt_block = jnp.sum(jnp.where(chosen, prompt_of[None, :], 0), axis=1)
    return (jnp.repeat(first * BLK, BLK), jnp.repeat(prompt_block, BLK))


def tile_terms(queries, grads, norms, deltas, keys, values, allowed):
    rows = queries.shape[0]
    cols = keys.shape[0]
    heads = norms.shape[1]
    group = heads // (keys.shape[1] // HD)
    scale = 1.0 / math.sqrt(HD)

    def one_head(head, carry):
        query_acc, key_acc, value_acc = carry
        kv_head = head // group
        query_h = lax.dynamic_slice_in_dim(queries, head * HD, HD, 1)
        grad_h = lax.dynamic_slice_in_dim(grads, head * HD, HD, 1)
        key_h = lax.dynamic_slice_in_dim(keys, kv_head * HD, HD, 1)
        value_h = lax.dynamic_slice_in_dim(values, kv_head * HD, HD, 1)
        norm_h = lax.dynamic_slice_in_dim(norms, head, 1, 1)
        delta_h = lax.dynamic_slice_in_dim(deltas, head, 1, 1)
        logits = jnp.dot(query_h, key_h.T, preferred_element_type=jnp.float32)
        weights = jnp.where(allowed, jnp.exp(logits * scale - norm_h), 0.0)
        weights_b = weights.astype(jnp.bfloat16)
        value_term = jnp.dot(weights_b.T, grad_h, preferred_element_type=jnp.float32)
        dweights = jnp.dot(grad_h, value_h.T, preferred_element_type=jnp.float32)
        dlogits = (weights * (dweights - delta_h)).astype(jnp.bfloat16)
        query_term = jnp.dot(dlogits, key_h, preferred_element_type=jnp.float32)
        key_term = jnp.dot(dlogits.T, query_h, preferred_element_type=jnp.float32)
        query_acc = lax.dynamic_update_slice_in_dim(query_acc, query_term, head * HD, 1)
        old_key = lax.dynamic_slice_in_dim(key_acc, kv_head * HD, HD, 1)
        key_acc = lax.dynamic_update_slice_in_dim(key_acc, old_key + key_term, kv_head * HD, 1)
        old_value = lax.dynamic_slice_in_dim(value_acc, kv_head * HD, HD, 1)
        value_acc = lax.dynamic_update_slice_in_dim(
            value_acc, old_value + value_term, kv_head * HD, 1
        )
        return (query_acc, key_acc, value_acc)

    start = (
        jnp.zeros((rows, queries.shape[1]), jnp.float32),
        jnp.zeros((cols, keys.shape[1]), jnp.float32),
        jnp.zeros((cols, keys.shape[1]), jnp.float32),
    )
    return lax.fori_loop(0, heads, one_head, start)


def add_rows(total, term, offset):
    old = lax.dynamic_slice_in_dim(total, offset, term.shape[0], 0)
    return lax.dynamic_update_slice_in_dim(total, old + term, offset, 0)


def shards(
    query_rows,
    key_rows,
    value_rows,
    attn_output,
    out_grad,
    log_norm,
    prefix_keys,
    prefix_values,
    response_blocks,
    prompt_members,
):
    queries, keys, values, outputs, grads = (
        lax.all_to_all(query_rows, "head", split_axis=1, concat_axis=0, tiled=True),
        lax.all_to_all(key_rows, "head", split_axis=1, concat_axis=0, tiled=True),
        lax.all_to_all(value_rows, "head", split_axis=1, concat_axis=0, tiled=True),
        lax.all_to_all(attn_output, "head", split_axis=1, concat_axis=0, tiled=True),
        lax.all_to_all(out_grad, "head", split_axis=1, concat_axis=0, tiled=True),
    )
    own_heads = queries.shape[1] // HD
    deltas = jnp.einsum(
        "thd,thd->th",
        grads.reshape(-1, own_heads, HD),
        outputs.reshape(-1, own_heads, HD),
        preferred_element_type=jnp.float32,
    )
    tokens = queries.shape[0]
    scale = 1.0 / math.sqrt(HD)
    norms = log_norm.T
    position = lax.axis_index("ctx")
    base = position * tokens
    starts, prompts = token_tables(
        response_blocks, prompt_members, position * (tokens // BLK), tokens // BLK
    )
    local_start = starts - base
    positions = jnp.arange(tokens, dtype=jnp.int32)
    allowed_here = (positions[None, :] >= local_start[:, None]) & (
        positions[None, :] <= positions[:, None]
    )
    allowed_prior = positions[None, :] - tokens >= local_start[:, None]
    query_one, key_one, value_one = tile_terms(
        queries, grads, norms, deltas, keys, values, allowed_here
    )
    keys_prior, values_prior = shifted((keys, values), "ctx", 1)
    query_two, key_two, value_two = tile_terms(
        queries, grads, norms, deltas, keys_prior, values_prior, allowed_prior
    )
    back_keys, back_values = (
        shifted(key_two.astype(jnp.bfloat16), "ctx", -1).astype(key_two.dtype),
        shifted(value_two.astype(jnp.bfloat16), "ctx", -1).astype(value_two.dtype),
    )
    whole_keys, whole_values = (
        lax.all_gather(prefix_keys, "ctx", axis=0, tiled=True),
        lax.all_gather(prefix_values, "ctx", axis=0, tiled=True),
    )
    prompt_total = whole_keys.shape[0]
    prompt_count = prompt_total // PL
    width = prefix_keys.shape[1]
    init = (
        query_one + query_two,
        jnp.zeros((prompt_total, width), jnp.float32),
        jnp.zeros((prompt_total, width), jnp.float32),
    )

    def prompt_step(number, state):
        seen = prompts == number

        def compute(inner):
            total, pkeys, pvalues = inner
            keys_p = lax.dynamic_slice_in_dim(whole_keys, number * PL, PL, 0)
            values_p = lax.dynamic_slice_in_dim(whole_values, number * PL, PL, 0)
            allowed = jnp.broadcast_to(seen[:, None], (tokens, PL))
            query_p, key_p, value_p = tile_terms(
                queries, grads, norms, deltas, keys_p, values_p, allowed
            )
            return (
                total + query_p,
                add_rows(pkeys, key_p, number * PL),
                add_rows(pvalues, value_p, number * PL),
            )

        return lax.cond(jnp.any(seen), compute, lambda inner: inner, state)

    query_total, pkey_acc, pvalue_acc = lax.fori_loop(0, prompt_count, prompt_step, init)
    pkey_sum, pvalue_sum = (
        lax.psum_scatter(pkey_acc, "ctx", scatter_dimension=0, tiled=True),
        lax.psum_scatter(pvalue_acc, "ctx", scatter_dimension=0, tiled=True),
    )
    return (
        (query_total * scale).astype(jnp.bfloat16),
        ((key_one + back_keys) * scale).astype(jnp.bfloat16),
        (value_one + back_values).astype(jnp.bfloat16),
        (pkey_sum * scale).astype(jnp.bfloat16),
        pvalue_sum.astype(jnp.bfloat16),
    )


def solution(mesh):
    placed = (
        P(("ctx", "head"), None),
        P(("ctx", "head"), None),
        P(("ctx", "head"), None),
        P(("ctx", "head"), None),
        P(("ctx", "head"), None),
        P("head", "ctx"),
        P("ctx", "head"),
        P("ctx", "head"),
        P(),
        P(),
    )
    return jax.shard_map(
        shards,
        mesh=mesh,
        in_specs=placed,
        out_specs=(
            P("ctx", "head"),
            P("ctx", "head"),
            P("ctx", "head"),
            P("ctx", "head"),
            P("ctx", "head"),
        ),
        check_vma=False,
    )
```

profile of v0, /device:TPU:8, one launch (start us, length us, event | category | flops | bytes accessed | tf_op | source)
XLA Modules:
  0.0 1574.4 jit_solution(12429472949831046137)
XLA Ops:
  7.2 1.8 copy.67
  8.9 5.5 all-to-all-start.1
  14.5 1.7 copy.66
  16.2 2.7 all-to-all-done.1
  18.9 5.0 all-to-all-start.3
  23.9 1.4 copy.46
  25.3 2.9 all-to-all-done.3
  28.2 5.3 all-to-all-start.2
  33.5 1.5 copy.50
  35.0 14.1 all-to-all-done.2
  49.1 5.3 all-to-all-start.4
  54.8 2.5 copy.65
  57.7 12.3 all-to-all-done.4
  70.0 6.1 all-to-all-start
  76.3 195.1 %all_gather.6 = bf16[1024,256]{1,0:T(8,128)(2,1)} all-gather(bf16[16,256]{1,0:T(8,128)(2,1)S(1)} %copy-done.9), channel_id=1, replica_groups=mesh['ctx'=64,'head'=4] {'ctx'}, dimensions={0}, use_global_device_ids=true | all-gather | bytes 532480 | tf_op jit(solution)/shard_map/all_gather | solution.py:135
  271.4 186.6 %all_gather.7 = bf16[1024,256]{1,0:T(8,128)(2,1)} all-gather(bf16[16,256]{1,0:T(8,128)(2,1)S(1)} %copy-done.10), channel_id=1, replica_groups=mesh['ctx'=64,'head'=4] {'ctx'}, dimensions={0}, use_global_device_ids=true | all-gather | bytes 532480 | tf_op jit(solution)/shard_map/all_gather | solution.py:136
  458.1 3.9 collective-permute-start
  462.0 2.6 collective-permute-start.1
  464.7 6.9 copy.49
  471.7 3.5 reshape.101
  475.2 6.9 copy.51
  482.1 3.5 reshape.102
  485.6 1.5 copy.47
  487.0 2.3 fusion.69
  489.4 1.6 broadcast.110.clone.1
  491.1 69.6 %while.79 = (s32[]{:T(128)}, f32[512,1280]{1,0:T(8,128)}, f32[512,256]{1,0:T(8,128)S(1)}, f32[512,256]{1,0:T(8,128)S(1)}, bf16[512,1280]{1,0:T(8,128)(2,1)}, /*i...) while((s32[]{:T(128)}, f32[512,1280]{1,0:T(8,128)}, ...), condition=%wide.region_5.6_spmd.clone, body=%wide.region_4.5_spmd.clone.sunk | while | flops 337772544 | bytes 6963587 | solution.py:75
  491.9 1.3 fusion.146
  498.8 1.3 fusion.146
  505.7 1.3 fusion.146
  512.7 1.3 fusion.146
  519.7 1.3 fusion.146
  533.6 1.3 fusion.146
  540.5 1.3 fusion.146
  560.7 1.7 broadcast.110.clone
  562.5 69.3 %while.78 = (s32[]{:T(128)}, f32[512,1280]{1,0:T(8,128)}, f32[512,256]{1,0:T(8,128)S(1)}, f32[512,256]{1,0:T(8,128)S(1)}, bf16[512,1280]{1,0:T(8,128)(2,1)}, /*i...) while((s32[]{:T(128)}, f32[512,1280]{1,0:T(8,128)}, ...), condition=%wide.region_3.4_spmd.clone, body=%wide.region_2.3_spmd.clone.sunk | while | flops 338296832 | bytes 6961531 | solution.py:75
  563.2 1.3 fusion.132
  570.1 1.3 fusion.132
  577.0 1.3 fusion.132
  583.9 1.3 fusion.132
  590.9 1.3 fusion.132
  597.7 1.3 fusion.132
  604.6 1.3 fusion.132
  611.6 1.3 fusion.132
  618.5 1.3 fusion.132
  625.4 1.3 fusion.132
  631.8 4.7 add.320
  638.6 136.6 %while.80 = (s32[]{:T(128)}, f32[512,1280]{1,0:T(8,128)}, f32[1024,256]{1,0:T(8,128)}, f32[1024,256]{1,0:T(8,128)}, bf16[1024,256]{1,0:T(8,128)(2,1)}, /*index=5...) while((s32[]{:T(128)}, f32[512,1280]{1,0:T(8,128)}, ...), condition=%wide.region_15.16_spmd.clone, body=%wide.region_9.15_spmd.clone.sunk | while | flops 85099536 | bytes 14145448 | solution.py:166
  643.0 62.4 %conditional.3 = ((f32[512,1280]{1,0:T(8,128)}, f32[1024,256]{1,0:T(8,128)}, f32[1024,256]{1,0:T(8,128)})) conditional(s32[]{:T(128)} %convert_element_type.143, (f32[512,1280]{1,0:T(8,128)}, f32[1024,256]{1,0:T(8,128)}, f32[1024,256]{1,0:T(8,128)}) %tuple.159, (s32[]{:T(128)}, bf16[1024,256]{1,0:T(8,128)(2,1)}, bf16[1024,256]{1,0:T(8,128)(2,1)}, ...), branch_computations={%region_11.11_spmd, %region_12.14_spmd} | conditional | flops 85098512 | bytes 14136441 | solution.py:164
  644.9 55.2 %while.77 = (s32[]{:T(128)}, f32[512,1280]{1,0:T(8,128)S(1)}, f32[128,256]{1,0:T(8,128)S(1)}, f32[128,256]{1,0:T(8,128)S(1)}, bf16[512,1280]{1,0:T(8,128)(2,1)},...) while((s32[]{:T(128)}, f32[512,1280]{1,0:T(8,128)S(1)}, ...), condition=%wide.region_14.13_spmd.clone, body=%wide.region_13.12_spmd.clone.sunk | while | flops 84377616 | bytes 2339707 | solution.py:75
  700.1 1.7 add_dynamic-update-slice_fusion
  701.8 3.5 add.309
  711.3 62.4 %conditional.3 = ((f32[512,1280]{1,0:T(8,128)}, f32[1024,256]{1,0:T(8,128)}, f32[1024,256]{1,0:T(8,128)})) conditional(s32[]{:T(128)} %convert_element_type.143, (f32[512,1280]{1,0:T(8,128)}, f32[1024,256]{1,0:T(8,128)}, f32[1024,256]{1,0:T(8,128)}) %tuple.159, (s32[]{:T(128)}, bf16[1024,256]{1,0:T(8,128)(2,1)}, bf16[1024,256]{1,0:T(8,128)(2,1)}, ...), branch_computations={%region_11.11_spmd, %region_12.14_spmd} | conditional | flops 85098512 | bytes 14136441 | solution.py:164
  713.2 55.2 %while.77 = (s32[]{:T(128)}, f32[512,1280]{1,0:T(8,128)S(1)}, f32[128,256]{1,0:T(8,128)S(1)}, f32[128,256]{1,0:T(8,128)S(1)}, bf16[512,1280]{1,0:T(8,128)(2,1)},...) while((s32[]{:T(128)}, f32[512,1280]{1,0:T(8,128)S(1)}, ...), condition=%wide.region_14.13_spmd.clone, body=%wide.region_13.12_spmd.clone.sunk | while | flops 84377616 | bytes 2339707 | solution.py:75
  768.4 1.7 add_dynamic-update-slice_fusion
  770.1 3.5 add.309
  776.2 1.3 collective-permute-start.3
  777.6 1.3 collective-permute-start.2
  778.9 3.1 multiply_convert_fusion
  781.9 2.6 collective-permute-done.3
  785.2 2.0 collective-permute-done.2
  788.1 413.7 %reduce-scatter.5.cloned.1.call-done = f32[16,256]{1,0:T(8,128)} async-done(((f32[1024,256]{1,0:T(8,128)}), f32[16,256]{1,0:T(8,128)}) %reduce-scatter.5.cloned.1.call-update) | async-done | bytes 16400 | tf_op jit(solution)/shard_map/reduce_scatter | solution.py:169
  1201.8 1.3 convert_element_type.106
  1203.1 363.2 %reduce-scatter.3.cloned.1.call-done = f32[16,256]{1,0:T(8,128)} async-done(((f32[1024,256]{1,0:T(8,128)}), f32[16,256]{1,0:T(8,128)}) %reduce-scatter.3.cloned.1.call-update) | async-done | bytes 16400 | tf_op jit(solution)/shard_map/reduce_scatter | solution.py:168
  1566.3 1.3 multiply_convert_fusion.2
  (321 shorter events, 240.1 us)
Async XLA Ops:
  7.2 16.7 %copy-start.7 = (bf16[128,5120]{1,0:T(8,128)(2,1)S(1)}, bf16[128,5120]{1,0:T(8,128)(2,1)}, u32[]{:S(2)}) copy-start(bf16[128,5120]{1,0:T(8,128)(2,1)} %param.24) | copy-start | bytes 3932164
  8.9 9.9 all-to-all-start.1
  18.9 9.4 all-to-all-start.3
  28.2 5.3 copy-start.8
  28.2 20.9 %all-to-all-start.2 = ((bf16[128,4,1280]{0,2,1:T(8,128)(2,1)}), bf16[128,4,1280]{0,2,1:T(8,128)(2,1)S(1)}, u32[]{:S(2)}, u32[]{:S(2)}) async-start(bf16[128,4,1280]{0,2,1:T(8,128)(2,1)} %bitcast.5), calls=%async_computation.2 | async-start | bytes 2621440 | tf_op jit(solution)/shard_map/all_to_all | solution.py:100
  49.1 5.3 copy-start.12
  49.1 20.9 %all-to-all-start.4 = ((bf16[128,4,1280]{0,2,1:T(8,128)(2,1)}), bf16[128,4,1280]{0,2,1:T(8,128)(2,1)S(1)}, u32[]{:S(2)}, u32[]{:S(2)}) async-start(bf16[128,4,1280]{0,2,1:T(8,128)(2,1)} %bitcast.73), calls=%async_computation.4 | async-start | bytes 2621440 | tf_op jit(solution)/shard_map/all_to_all | solution.py:99
  54.8 2.5 copy-start.11
  70.0 6.2 copy-start.9
  70.0 201.4 %copy-start.10 = (bf16[16,256]{1,0:T(8,128)(2,1)S(1)}, bf16[16,256]{1,0:T(8,128)(2,1)}, u32[]{:S(2)}) copy-start(bf16[16,256]{1,0:T(8,128)(2,1)} %param.27) | copy-start | bytes 24580
  70.0 419.3 %all-to-all-start = ((bf16[128,4,1280]{2,0,1:T(8,128)(2,1)}), bf16[128,4,1280]{2,0,1:T(8,128)(2,1)}, u32[]{:S(2)}, u32[]{:S(2)}) async-start(bf16[128,4,1280]{2,0,1:T(8,128)(2,1)} %bitcast.72), calls=%async_computation | async-start | bytes 2621440 | tf_op jit(solution)/shard_map/all_to_all | solution.py:96
  76.1 1125.7 %reduce-scatter.5.cloned.1.call-start = ((), (), s32[]{:S(2)}) async-start(), calls=%async_computation.8 | async-start | bytes 1064960 | tf_op jit(solution)/shard_map/reduce_scatter | solution.py:169
  458.1 31.3 %collective-permute-start = (bf16[512,256]{1,0:T(8,128)(2,1)S(1)}, bf16[512,256]{1,0:T(8,128)(2,1)S(1)}, u32[]{:S(2)}, u32[]{:S(2)}) collective-permute-start(bf16[512,256]{1,0:T(8,128)(2,1)S(1)} %bitcast.75), channel_id=1, source_target_pairs={{0,4},{4,8},{8,12},{12,16},{16,20},{20,24},{24,28},{28,32},{32,36}... | collective-permute-start | bytes 786440 | tf_op jit(solution)/shard_map/ppermute | solution.py:16
  462.0 27.4 %collective-permute-start.1 = (bf16[512,256]{1,0:T(8,128)(2,1)S(1)}, bf16[512,256]{1,0:T(8,128)(2,1)}, u32[]{:S(2)}, u32[]{:S(2)}) collective-permute-start(bf16[512,256]{1,0:T(8,128)(2,1)S(1)} %bitcast.77), channel_id=1, source_target_pairs={{0,4},{4,8},{8,12},{12,16},{16,20},{20,24},{24,28},{28,32},{32,36}... | collective-permute-start | bytes 786440 | tf_op jit(solution)/shard_map/ppermute | solution.py:16
  485.6 1.5 copy-start.6
  560.7 1.7 copy-start
  631.8 4.7 copy-start.2
  631.8 4.7 copy-start.4
  775.1 1.0 copy-start.1
  775.2 791.1 %reduce-scatter.3.cloned.1.call-start = ((), (), s32[]{:S(2)}) async-start(), calls=%async_computation.7 | async-start | bytes 1064960 | tf_op jit(solution)/shard_map/reduce_scatter | solution.py:168
  776.2 8.3 collective-permute-start.3
  777.6 9.7 collective-permute-start.2
  778.9 5.6 copy-start.5
  781.9 5.4 copy-start.3
Sparse Core Ops, SparseCore 0:
  775.3 426.4 reduce-scatter.4
  1204.2 361.9 reduce-scatter.2
where the time goes:
time: 1590 us; the launch traced here: 1570 us
  waiting for transfers between devices  814 us (51%)
  blocking collectives  382 us (24%)
  matrix products  216 us (14%)
  local copies, waits for them, and re-layouts  72.1 us (5%)
  starting transfers between devices  36.3 us (2%)
  other arithmetic  30.7 us (2%)
    reduce_scatter x1, waiting for transfers between devices, shards(): lax.psum_scatter(pvalue_acc, 'ctx', scatter_dimension=0, tiled=True)  414 us
    reduce_scatter x1, waiting for transfers between devices, shards(): lax.psum_scatter(pkey_acc, 'ctx', scatter_dimension=0, tiled=True)  363 us
    all_gather x1, blocking collectives, shards(): lax.all_gather(prefix_keys, 'ctx', axis=0, tiled=True)  195 us
    all_gather x1, blocking collectives, shards(): lax.all_gather(prefix_values, 'ctx', axis=0, tiled=True)  187 us
    dot_general x40, matrix products, one_head(): logits = jnp.dot(query_h, key_h.T, preferred_element_type=jnp.float32)  48.4 us
    dot_general x40, matrix products, one_head(): jnp.dot(weights_b.T, grad_h, preferred_element_type=jnp.float32)  48.2 us
    dot_general x40, matrix products, one_head(): key_term = jnp.dot(dlogits.T, query_h, preferred_element_type=jnp.float32)  47.9 us
    dot_general x40, matrix products, one_head(): dweights = jnp.dot(grad_h, value_h.T, preferred_element_type=jnp.float32)  47.1 us
  transfers between devices with their start and end apart: 11, of which 8 were waited for; matrix products, arithmetic and copies ran while one was open for 2% of the time, Pallas kernels for 0%

commit v1 on v0

v1 whole, which is shorter than its diff:
```python
import math

import jax
import jax.numpy as jnp
import numpy as np
from jax import lax
from jax.sharding import Mesh
from jax.sharding import PartitionSpec as P

HD = 128
BLK = 32
PL = 128

CTX_PARTS = (("z", 8), ("yh", 2), ("x", 4))


def ctx_axes(mesh):
    ctx = mesh.shape["ctx"]
    if ctx == math.prod(n for _, n in CTX_PARTS):
        return CTX_PARTS
    return (("c", ctx),)


def shifted(array, axes, sizes, by):
    devices = math.prod(sizes)
    pairs = [(i, i + by) for i in range(devices) if 0 <= i + by < devices]
    return lax.ppermute(array, axes, pairs)


def block_tables(response_blocks, prompt_members, first_block, count):
    starts = jnp.cumsum(response_blocks) - response_blocks
    responses = response_blocks.shape[0]
    group = prompt_members.shape[1]
    listed = prompt_members.reshape(-1)
    owner = jnp.arange(listed.shape[0], dtype=jnp.int32) // group
    numbers = jnp.arange(responses, dtype=jnp.int32)
    hits = listed[:, None] == numbers[None, :]
    prompt_of = jnp.sum(jnp.where(hits, owner[:, None], 0), axis=0)
    blocks = first_block + jnp.arange(count, dtype=jnp.int32)
    before = starts[None, :] <= blocks[:, None]
    first = jnp.max(jnp.where(before, starts[None, :], 0), axis=1)
    current = jnp.sum(before.astype(jnp.int32), axis=1) - 1
    chosen = numbers[None, :] == current[:, None]
    prompt_block = jnp.sum(jnp.where(chosen, prompt_of[None, :], 0), axis=1)
    return first, prompt_block


def make_shards(parts):
    names = tuple(n for n, _ in parts)
    sizes = tuple(s for _, s in parts)

    def shards(
        query_rows,
        key_rows,
        value_rows,
        attn_output,
        out_grad,
        log_norm,
        prefix_keys,
        prefix_values,
        response_blocks,
        prompt_members,
    ):
        f32, bf16 = jnp.float32, jnp.bfloat16
        nh = lax.axis_size("head")
        rows, qw = query_rows.shape
        kw = key_rows.shape[1]
        all_heads = qw // HD
        scale = 1.0 / math.sqrt(HD)

        delta_rows = jnp.einsum(
            "thd,thd->th",
            out_grad.reshape(rows, all_heads, HD),
            attn_output.reshape(rows, all_heads, HD),
            preferred_element_type=f32,
        )
        packed = jnp.concatenate(
            [
                query_rows.reshape(rows, nh, qw // nh),
                out_grad.reshape(rows, nh, qw // nh),
                key_rows.reshape(rows, nh, kw // nh),
                value_rows.reshape(rows, nh, kw // nh),
            ],
            axis=2,
        )
        got = lax.all_to_all(packed, "head", split_axis=1, concat_axis=0, tiled=True)
        deltas = lax.all_to_all(
            delta_rows.reshape(rows, nh, all_heads // nh),
            "head",
            split_axis=1,
            concat_axis=0,
            tiled=True,
        )
        tokens = got.shape[0]
        got = got.reshape(tokens, -1)
        lq, lk = qw // nh, kw // nh
        kvh = lk // HD
        grp = (lq // HD) // kvh
        q = got[:, :lq].reshape(tokens, kvh, grp, HD)
        do = got[:, lq : 2 * lq].reshape(tokens, kvh, grp, HD)
        k = got[:, 2 * lq : 2 * lq + lk].reshape(tokens, kvh, HD)
        v = got[:, 2 * lq + lk :].reshape(tokens, kvh, HD)
        norms = log_norm.reshape(kvh, grp, tokens)
        delta = deltas.reshape(tokens, kvh * grp).T.reshape(kvh, grp, tokens)

        position = lax.axis_index(names)
        base = position * tokens
        nblk = tokens // BLK
        first, prompt_block = block_tables(
            response_blocks, prompt_members, position * nblk, nblk
        )
        local_start = jnp.repeat(first * BLK, BLK) - base

        k_prior, v_prior = shifted((k, v), names, sizes, 1)
        keys = jnp.concatenate([k_prior, k], axis=0)
        values = jnp.concatenate([v_prior, v], axis=0)
        u = jnp.arange(2 * tokens, dtype=jnp.int32) - tokens
        t = jnp.arange(tokens, dtype=jnp.int32)
        allowed = (u[None, :] >= local_start[:, None]) & (u[None, :] <= t[:, None])

        dq_parts, dk_parts, dv_parts = [], [], []
        for g in range(kvh):
            qg, dog, kg, vg = q[:, g], do[:, g], keys[:, g], values[:, g]
            logits = jnp.einsum("trd,sd->rts", qg, kg, preferred_element_type=f32)
            w = jnp.where(
                allowed[None], jnp.exp(logits * scale - norms[g][:, :, None]), 0.0
            )
            wb = w.astype(bf16)
            dv_parts.append(jnp.einsum("rts,trd->sd", wb, dog, preferred_element_type=f32))
            dw = jnp.einsum("trd,sd->rts", dog, vg, preferred_element_type=f32)
            dl = (w * (dw - delta[g][:, :, None])).astype(bf16)
            dq_parts.append(jnp.einsum("rts,sd->trd", dl, kg, preferred_element_type=f32))
            dk_parts.append(jnp.einsum("rts,trd->sd", dl, qg, preferred_element_type=f32))
        dq = jnp.stack(dq_parts, axis=1)
        dk = jnp.stack(dk_parts, axis=1)
        dv = jnp.stack(dv_parts, axis=1)

        pkv = jnp.concatenate([prefix_keys, prefix_values], axis=1)
        for name in reversed(names):
            pkv = lax.all_gather(pkv, name, axis=0, tiled=True)
        nprompt = pkv.shape[0] // PL
        pk_all = pkv[:, :lk].reshape(nprompt, PL, kvh, HD)
        pv_all = pkv[:, lk:].reshape(nprompt, PL, kvh, HD)
        pkb = jnp.take(pk_all, prompt_block, axis=0)
        pvb = jnp.take(pv_all, prompt_block, axis=0)
        qb = q.reshape(nblk, BLK, kvh, grp, HD)
        dob = do.reshape(nblk, BLK, kvh, grp, HD)
        normb = norms.reshape(kvh, grp, nblk, BLK).transpose(2, 0, 1, 3)
        deltab = delta.reshape(kvh, grp, nblk, BLK).transpose(2, 0, 1, 3)
        lp = jnp.einsum("bigrd,bjgd->bgrij", qb, pkb, preferred_element_type=f32)
        wp = jnp.exp(lp * scale - normb[..., None])
        wpb = wp.astype(bf16)
        dv_pb = jnp.einsum("bgrij,bigrd->bjgd", wpb, dob, preferred_element_type=f32)
        dwp = jnp.einsum("bigrd,bjgd->bgrij", dob, pvb, preferred_element_type=f32)
        dlp = (wp * (dwp - deltab[..., None])).astype(bf16)
        dq_p = jnp.einsum("bgrij,bjgd->bigrd", dlp, pkb, preferred_element_type=f32)
        dk_pb = jnp.einsum("bgrij,bigrd->bjgd", dlp, qb, preferred_element_type=f32)
        onehot = (prompt_block[:, None] == jnp.arange(nprompt)[None, :]).astype(f32)
        pgrad = jnp.einsum(
            "bp,bjx->pjx",
            onehot,
            jnp.concatenate(
                [dk_pb.reshape(nblk, PL, lk), dv_pb.reshape(nblk, PL, lk)], axis=2
            ),
            precision=lax.Precision.HIGHEST,
            preferred_element_type=f32,
        ).reshape(nprompt * PL, 2 * lk)
        for name in names:
            pgrad = lax.psum_scatter(pgrad, name, scatter_dimension=0, tiled=True)

        dq = dq + dq_p.reshape(tokens, kvh, grp, HD)
        back_k, back_v = shifted(
            (dk[:tokens].astype(bf16), dv[:tokens].astype(bf16)), names, sizes, -1
        )
        key_grad = (dk[tokens:] + back_k.astype(f32)) * scale
        value_grad = dv[tokens:] + back_v.astype(f32)
        return (
            (dq * scale).astype(bf16).reshape(tokens, lq),
            key_grad.astype(bf16).reshape(tokens, lk),
            value_grad.astype(bf16).reshape(tokens, lk),
            (pgrad[:, :lk] * scale).astype(bf16),
            pgrad[:, lk:].astype(bf16),
        )

    return shards, names


def solution(mesh):
    parts = ctx_axes(mesh)
    devices = np.asarray(mesh.devices).reshape(
        tuple(s for _, s in parts) + (mesh.shape["head"],)
    )
    sub = Mesh(devices, tuple(n for n, _ in parts) + ("head",))
    shards, ctx = make_shards(parts)
    rows = P(ctx + ("head",), None)
    grid = P(ctx, "head")
    placed = (
        rows,
        rows,
        rows,
        rows,
        rows,
        P("head", ctx),
        grid,
        grid,
        P(),
        P(),
    )
    return jax.shard_map(
        shards,
        mesh=sub,
        in_specs=placed,
        out_specs=(grid,) * 5,
        check_vma=False,
    )
```

time: 1590 us -> 246 us (0.15)
  the two profiles are of different devices: /device:TPU:8 before, /device:TPU:22 now
where the time goes in v1:
time: 246 us; the launch traced here: 242 us
  local copies, waits for them, and re-layouts  67.6 us (27%)
  waiting for transfers between devices  56.8 us (23%)
  matrix products  49.9 us (20%)
  starting transfers between devices  19.6 us (8%)
  blocking collectives  18.4 us (7%)
  other arithmetic  15.5 us (6%)
  between operations  14.5 us (6%)
    reduce_scatter x3, waiting for transfers between devices, shards(): pgrad = lax.psum_scatter(pgrad, name, scatter_dimension=0, tiled=True)  35.6 us
    all_gather x1, waiting for transfers between devices, shards(): pkv = lax.all_gather(pkv, name, axis=0, tiled=True)  21.2 us
    all_gather x2, blocking collectives, shards(): pkv = lax.all_gather(pkv, name, axis=0, tiled=True)  18.4 us
    ppermute x4, starting transfers between devices, shifted(): return lax.ppermute(array, axes, pairs)  12.4 us
    dot_general x2, matrix products, shards(): dw = jnp.einsum('trd,sd->rts', dog, vg, preferred_element_type=f32)  10.5 us
    dot_general x2, matrix products, shards(): jnp.einsum('rts,trd->sd', wb, dog, preferred_element_type=f32)  10.3 us
    unnamed x92, local copies, waits for them, and re-layouts  9.95 us
    dot_general x2, matrix products, shards(): jnp.einsum('rts,sd->trd', dl, kg, preferred_element_type=f32)  5.68 us
  transfers between devices with their start and end apart: 10, of which 3 were waited for; matrix products, arithmetic and copies ran while one was open for 45% of the time, Pallas kernels for 0%

profile of v1, /device:TPU:22, one launch (start us, length us, event | category | flops | bytes accessed | tf_op | source)
XLA Modules:
  0.0 242.3 jit_solution(4802524583771293655)
XLA Ops:
  8.0 11.8 %all_gather.9 = bf16[64,512]{1,0:T(8,128)(2,1)S(1)} all-gather(bf16[16,512]{1,0:T(8,128)(2,1)S(1)} %pad_maximum_fusion.6), channel_id=1, replica_groups=mesh['z'=8,'yh'=2,'x'=4,'head'=4] {'x'}, dimensions={0}, use_global_device_ids=true | all-gather | bytes 81920 | tf_op jit(solution)/shard_map/all_gather | solution.py:140
  19.9 6.5 %all_gather.10 = bf16[128,512]{1,0:T(8,128)(2,1)} all-gather(bf16[64,512]{1,0:T(8,128)(2,1)S(1)} %all_gather.9), channel_id=1, replica_groups=mesh['z'=8,'yh'=2,'x'=4,'head'=4] {'yh'}, dimensions={0}, use_global_device_ids=true | all-gather | bytes 196608 | tf_op jit(solution)/shard_map/all_gather | solution.py:140
  26.4 1.6 copy.202
  29.8 3.3 %all-to-all-start.1 = ((f32[128,4,10]{0,2,1:T(8,128)}), f32[128,4,10]{0,2,1:T(8,128)S(1)}, u32[]{:S(2)}, u32[]{:S(2)}) async-start(f32[128,4,10]{0,2,1:T(8,128)} %reshape.222), calls=%async_computation.1 | async-start | bytes 65536 | tf_op jit(solution)/shard_map/all_to_all | solution.py:87
  34.2 1.8 copy.121
  36.0 1.8 pad_maximum_fusion
  37.8 3.8 %all-to-all-start = ((bf16[128,4,3072]{0,2,1:T(8,128)(2,1)}), bf16[128,4,3072]{0,2,1:T(8,128)(2,1)S(1)}, u32[]{:S(2)}, u32[]{:S(2)}) async-start(bf16[128,4,3072]{0,2,1:T(8,128)(2,1)} %pad_maximum_fusion), calls=%async_computation | async-start | bytes 6291456 | tf_op jit(solution)/shard_map/all_to_all | solution.py:86
  43.5 1.3 fusion.25
  46.3 21.2 %all-gather.2.cloned.1.call-done = bf16[1024,512]{1,0:T(8,128)(2,1)} async-done(((bf16[128,512]{1,0:T(8,128)(2,1)}), bf16[1024,512]{1,0:T(8,128)(2,1)}) %all-gather.2.cloned.1.call-update) | async-done | bytes 1048592 | tf_op jit(solution)/shard_map/all_gather | solution.py:140
  67.5 2.2 fusion.93
  69.7 2.0 reshape.273
  71.7 1.9 copy.149
  73.6 2.0 reshape.272
  75.5 1.9 copy.145
  77.5 2.7 %gather_fusion.1 = bf16[16,128,2,128]{3,1,2,0:T(8,128)(2,1)} fusion(bf16[8,128,2,128]{3,1,2,0:T(8,128)(2,1)} %copy.149, s32[1024]{0:T(1024)S(1)} %pad_clamp_fusion), kind=kCustom, calls=%fused_computation.1.clone | custom fusion | bytes 2097216 | tf_op jit(solution)/shard_map/jit(_take)/gather | solution.py:145
  80.2 2.7 %gather_fusion = bf16[16,128,2,128]{3,1,2,0:T(8,128)(2,1)} fusion(bf16[8,128,2,128]{3,1,2,0:T(8,128)(2,1)} %copy.145, s32[1024]{0:T(1024)S(1)} %pad_clamp_fusion), kind=kCustom, calls=%fused_computation.clone | custom fusion | bytes 2097216 | tf_op jit(solution)/shard_map/jit(_take)/gather | solution.py:144
  82.9 2.8 %copy.125 = bf16[4,128,1,3072]{3,1,0,2:T(8,128)(2,1)} copy(bf16[4,128,1,3072]{1,3,0,2:T(8,128)(2,1)S(1)} %bitcast.196) | data formatting | bytes 6291456 | tf_op jit(solution)/shard_map/all_to_all | solution.py:86
  85.7 1.9 fusion.91
  87.5 1.9 fusion.92
  89.4 1.5 copy.135
  90.9 2.4 %reshape_reshape.14 = bf16[16,32,2,5,128]{4,3,2,1,0:T(8,128)(2,1)} reshape(bf16[512,1280]{1,0:T(8,128)(2,1)S(1)} %get-tuple-element.30) | data formatting | bytes 2621440 | tf_op jit(solution)/shard_map/reshape;reshape | solution.py:147
  93.3 1.5 copy.130
  94.8 1.5 reshape_reshape.12
  96.3 1.2 copy.132
  97.5 0.8 copy.133
  98.3 1.1 copy.126
  99.4 0.8 copy.127
  100.3 3.0 %collective-permute-start = (bf16[512,2,128]{2,0,1:T(8,128)(2,1)}, bf16[512,2,128]{2,0,1:T(8,128)(2,1)}, u32[]{:S(2)}, u32[]{:S(2)}) collective-permute-start(bf16[512,2,128]{2,0,1:T(8,128)(2,1)} %copy.127), channel_id=1, source_target_pairs={{0,4},{4,8},{8,12},{12,16},{16,20},{20,24},{24,28},{28,32},{32,36}... | collective-permute-start | bytes 786440 | tf_op jit(solution)/shard_map/ppermute | solution.py:27
  103.3 3.5 %collective-permute-start.1 = (bf16[512,2,128]{2,0,1:T(8,128)(2,1)}, bf16[512,2,128]{2,0,1:T(8,128)(2,1)}, u32[]{:S(2)}, u32[]{:S(2)}) collective-permute-start(bf16[512,2,128]{2,0,1:T(8,128)(2,1)} %copy.133), channel_id=1, source_target_pairs={{0,4},{4,8},{8,12},{12,16},{16,20},{20,24},{24,28},{28,32},{32,36}... | collective-permute-start | bytes 786440 | tf_op jit(solution)/shard_map/ppermute | solution.py:27
  106.8 1.6 fusion.38
  108.4 2.9 %fusion.26 = f32[16,2,128,128,1]{3,2,4,1,0:T(8,128)} fusion(f32[16,2,128,32,5]{2,3,4,1,0:T(8,128)S(1)} %fusion.38, f32[16,2,5,32]{3,2,1,0:T(8,128)S(1)} %copy-done.24, bf16[16,32,2,5,128]{4,3,2,1,0:T(8,128)(2,1)S(1)} %copy-done.17), kind=kOutput, calls=%fused_computation.40 | convolution fusion | flops 169738240 | bytes 6049792 | tf_op jit(solution)/shard_map/bgrij,bigrd->bjgd/dot_general | solution.py:153
  111.3 3.2 %copy.165 = f32[16,128,256]{2,0,1:T(8,128)} copy(f32[16,128,256]{1,2,0:T(8,128)} %bitcast.215) | data formatting | bytes 4194304 | tf_op jit(solution)/shard_map/reshape | solution.py:163
  114.5 4.1 %fusion.21 = bf16[16,2,5,32,128]{4,3,2,1,0:T(8,128)(2,1)S(1)} fusion(f32[16,2,128,32,5]{2,3,4,1,0:T(8,128)} %copy-done.11, f32[16,2,5,32]{3,2,1,0:T(8,128)S(1)} %get-tuple-element.42, f32[16,2,5,32]{3,2,1,0:T(8,128)S(1)} %copy-done.24, bf16[16,128,2,128]{3,1,2,0:T(8,128)(2,1)} %gather_fusion.1, pred[16]{0:T(512)(128)(4,1)S(1)} %copy-done.30, ...), kind=kOutput, calls=%fused_computation.28 | convolution fusion | flops 171573248 | bytes 6332432 | tf_op jit(solution)/shard_map/bigrd,bjgd->bgrij/dot_general | solution.py:154
  118.6 2.1 fusion.44
  120.7 3.3 %copy.164 = f32[16,128,256]{2,0,1:T(8,128)} copy(f32[16,128,256]{1,2,0:T(8,128)} %bitcast.205) | data formatting | bytes 4194304 | tf_op jit(solution)/shard_map/reshape | solution.py:163
  124.0 3.1 %fusion.16 = f32[8,128,512]{2,0,1:T(8,128)S(1)} fusion(f32[16,128,256]{2,0,1:T(8,128)S(1)} %copy-done.6, f32[16,128,256]{2,0,1:T(8,128)} %copy.164, s32[16]{0:T(128)S(1)} %copy-done.33), kind=kOutput, calls=%fused_computation.20 | convolution fusion | flops 101712000 | bytes 6291520 | tf_op jit(solution)/shard_map/bp,bjx->pjx/dot_general | solution.py:159
  127.1 2.5 %copy.166 = f32[8,128,512]{2,1,0:T(8,128)} copy(f32[8,128,512]{2,0,1:T(8,128)S(1)} %fusion.16) | data formatting | bytes 4194304 | tf_op jit(solution)/shard_map/bp,bjx->pjx/dot_general | solution.py:159
  130.3 3.7 %copy.152 = f32[16,32,2,5,128]{4,3,2,1,0:T(8,128)} copy(f32[16,32,2,5,128]{4,1,3,2,0:T(8,128)S(1)} %convolution_bitcast_fusion) | data formatting | bytes 5242880 | tf_op jit(solution)/shard_map/bgrij,bjgd->bigrd/transpose | solution.py:156
  134.1 4.8 %reshape.226 = f32[512,1280]{1,0:T(8,128)} reshape(f32[16,32,2,5,128]{4,3,2,1,0:T(8,128)} %copy.152) | data formatting | bytes 5242880 | tf_op jit(solution)/shard_map/reshape | solution.py:171
  138.9 2.5 %fusion.47 = f32[1024,512,5]{1,0,2:T(8,128)S(1)} fusion(bf16[512,2,5,128]{0,3,2,1:T(8,128)(2,1)S(1)} %bitcast.200, bf16[512,2,128]{2,0,1:T(8,128)(2,1)} %collective-permute-done, bf16[512,2,128]{2,0,1:T(8,128)(2,1)} %copy.127), kind=kOutput, calls=%fused_computation.67 | convolution fusion | flops 671612928 | bytes 11665408 | tf_op jit(solution)/shard_map/trd,sd->rts/dot_general | solution.py:124
  141.4 3.0 %fusion.48 = f32[1024,512,5]{1,0,2:T(8,128)S(1)} fusion(bf16[512,2,5,128]{0,3,2,1:T(8,128)(2,1)S(1)} %bitcast.201, bf16[512,2,128]{2,0,1:T(8,128)(2,1)} %copy.127, bf16[512,2,128]{2,0,1:T(8,128)(2,1)} %collective-permute-done), kind=kOutput, calls=%fused_computation.68 | convolution fusion | flops 671612928 | bytes 11665408 | tf_op jit(solution)/shard_map/trd,sd->rts/dot_general | solution.py:124
  144.4 1.3 copy-done.1
  145.8 6.0 %fusion.5 = bf16[5,512,1024]{1,2,0:T(8,128)(2,1)} fusion(f32[1024,512,5]{1,0,2:T(8,128)S(1)} %fusion.47, f32[5,512]{1,0:T(8,128)S(1)} %copy-done.28, f32[5,512]{1,0:T(8,128)S(1)} %copy-done.26, pred[512,1024]{0,1:T(8,128)(4,1)S(1)} %copy-done.19, bf16[512,2,5,128]{0,3,2,1:T(8,128)(2,1)S(1)} %bitcast.219, bf16[512,2,128]{2,0,1:T(8,128)(2,1)} %collective-permute-done.1, ...), kind=kOutput, calls=%fused_computation.10 | convolution fusion | flops 687341568 | bytes 17465344 | tf_op jit(solution)/shard_map/trd,sd->rts/dot_general | solution.py:130
  151.9 3.5 %convolution_bitcast_fusion.2 = f32[512,1,5,128]{0,3,2,1:T(8,128)S(1)} fusion(bf16[5,512,1024]{1,2,0:T(8,128)(2,1)} %fusion.5, bf16[512,2,128]{2,0,1:T(8,128)(2,1)} %collective-permute-done, bf16[512,2,128]{2,0,1:T(8,128)(2,1)} %copy.127), kind=kOutput, calls=%fused_computation.39 | convolution fusion | flops 671612928 | bytes 7077888 | tf_op jit(solution)/shard_map/rts,sd->trd/dot_general | solution.py:132
  155.4 4.5 %fusion.1 = bf16[5,512,1024]{1,2,0:T(8,128)(2,1)S(1)} fusion(f32[1024,512,5]{1,0,2:T(8,128)S(1)} %fusion.48, f32[5,512]{1,0:T(8,128)S(1)} %copy-done.27, f32[5,512]{1,0:T(8,128)S(1)} %get-tuple-element.35, pred[512,1024]{0,1:T(8,128)(4,1)S(1)} %copy-done.19, bf16[512,2,5,128]{0,3,2,1:T(8,128)(2,1)S(1)} %bitcast.220, bf16[512,2,128]{2,0,1:T(8,128)(2,1)S(1)} %copy-done.23, ...), kind=kOutput, calls=%fused_computation.4 | convolution fusion | flops 687341568 | bytes 17465344 | tf_op jit(solution)/shard_map/trd,sd->rts/dot_general | solution.py:130
  159.9 2.2 convolution_bitcast_fusion.1
  162.2 1.9 pad_maximum_fusion.1
  164.1 3.4 %copy.153 = f32[512,1280]{1,0:T(8,128)} copy(f32[512,1280]{0,1:T(8,128)} %bitcast.199) | data formatting | bytes 5242880 | tf_op jit(solution)/shard_map/stack | solution.py:134
  167.6 5.8 %fusion.30 = f32[1024,1,128]{0,2,1:T(8,128)S(1)} fusion(f32[1024,512,5]{1,0,2:T(8,128)} %copy-done.1, f32[5,512]{1,0:T(8,128)S(1)} %copy-done.26, pred[512,1024]{0,1:T(8,128)(4,1)} %fusion.25, bf16[512,2,5,128]{0,3,2,1:T(8,128)(2,1)} %bitcast.217), kind=kOutput, calls=%fused_computation.45 | convolution fusion | flops 681574400 | bytes 12199936 | tf_op jit(solution)/shard_map/rts,trd->sd/dot_general | solution.py:129
  173.5 1.1 slice-done.2
  174.6 4.5 %fusion.33 = f32[1024,1,128]{0,2,1:T(8,128)S(1)} fusion(f32[1024,512,5]{1,0,2:T(8,128)S(1)} %bitcast.195, f32[5,512]{1,0:T(8,128)S(1)} %get-tuple-element.35, pred[512,1024]{0,1:T(8,128)(4,1)S(1)} %copy-done.20, bf16[512,2,5,128]{0,3,2,1:T(8,128)(2,1)} %bitcast.218), kind=kOutput, calls=%fused_computation.46 | convolution fusion | flops 681574400 | bytes 12199936 | tf_op jit(solution)/shard_map/rts,trd->sd/dot_general | solution.py:129
  179.9 2.9 %collective-permute-start.3 = (bf16[512,2,128]{0,2,1:T(8,128)(2,1)}, bf16[512,2,128]{0,2,1:T(8,128)(2,1)}, u32[]{:S(2)}, u32[]{:S(2)}) collective-permute-start(bf16[512,2,128]{0,2,1:T(8,128)(2,1)} %fusion.56), channel_id=1, source_target_pairs={{4,0},{8,4},{12,8},{16,12},{20,16},{24,20},{28,24},{32,28},{36,32}... | collective-permute-start | bytes 786440 | tf_op jit(solution)/shard_map/ppermute | solution.py:27
  182.9 1.8 convolution_bitcast_fusion.4
  184.7 1.8 convolution_bitcast_fusion.3
  187.3 3.0 %collective-permute-start.2 = (bf16[512,2,128]{0,2,1:T(8,128)(2,1)S(1)}, bf16[512,2,128]{0,2,1:T(8,128)(2,1)}, u32[]{:S(2)}, u32[]{:S(2)}) collective-permute-start(bf16[512,2,128]{0,2,1:T(8,128)(2,1)S(1)} %fusion.57), channel_id=1, source_target_pairs={{4,0},{8,4},{12,8},{16,12},{20,16},{24,20},{28,24},{32,28},{36,32}... | collective-permute-start | bytes 786440 | tf_op jit(solution)/shard_map/ppermute | solution.py:27
  190.4 3.2 %multiply_convert_fusion = bf16[512,1280]{1,0:T(8,128)(2,1)} fusion(f32[512,1280]{1,0:T(8,128)} %copy.153, f32[512,1280]{1,0:T(8,128)S(1)} %copy-done.2), kind=kLoop, calls=%fused_computation.33 | loop fusion | flops 1966080 | bytes 6553600 | tf_op jit(solution)/shard_map/convert_element_type | solution.py:178
  193.6 13.9 %reduce-scatter.6.cloned.1.call-done = f32[64,512]{1,0:T(8,128)} async-done(((f32[128,512]{1,0:T(8,128)}), f32[64,512]{1,0:T(8,128)}) %reduce-scatter.6.cloned.1.call-update) | async-done | bytes 131088 | tf_op jit(solution)/shard_map/reduce_scatter | solution.py:169
  207.5 1.1 fusion.51
  208.7 0.8 copy.168
  209.5 1.2 fusion.55
  210.7 0.8 copy.167
  211.5 21.6 %reduce-scatter.8.cloned.1.call-done = f32[16,512]{1,0:T(8,128)} async-done(((f32[64,512]{1,0:T(8,128)}), f32[16,512]{1,0:T(8,128)}) %reduce-scatter.8.cloned.1.call-update) | async-done | bytes 32784 | tf_op jit(solution)/shard_map/reduce_scatter | solution.py:169
  233.1 1.3 slice.189
  234.5 1.3 fusion.70
  (133 shorter events, 9.6 us)
Async XLA Ops:
  7.2 20.9 %copy-start.10 = (bf16[128,5120]{1,0:T(8,128)(2,1)S(1)}, bf16[128,5120]{1,0:T(8,128)(2,1)}, u32[]{:S(2)}) copy-start(bf16[128,5120]{1,0:T(8,128)(2,1)} %param.16) | copy-start | bytes 3932164
  7.2 60.3 %all-gather.2.cloned.1.call-start = ((), (), s32[]{:S(2)}) async-start(), calls=%async_computation.5 | async-start | bytes 1179648 | tf_op jit(solution)/shard_map/all_gather | solution.py:140
  28.3 5.6 %copy-start.21 = (bf16[128,1024]{1,0:T(8,128)(2,1)S(1)}, bf16[128,1024]{1,0:T(8,128)(2,1)}, u32[]{:S(2)}) copy-start(bf16[128,1024]{1,0:T(8,128)(2,1)} %param.13) | copy-start | bytes 786436
  28.3 5.7 %copy-start.22 = (bf16[128,1024]{1,0:T(8,128)(2,1)S(1)}, bf16[128,1024]{1,0:T(8,128)(2,1)}, u32[]{:S(2)}) copy-start(bf16[128,1024]{1,0:T(8,128)(2,1)} %param.14) | copy-start | bytes 786436
  29.8 8.0 %all-to-all-start.1 = ((f32[128,4,10]{0,2,1:T(8,128)}), f32[128,4,10]{0,2,1:T(8,128)S(1)}, u32[]{:S(2)}, u32[]{:S(2)}) async-start(f32[128,4,10]{0,2,1:T(8,128)} %reshape.222), calls=%async_computation.1 | async-start | bytes 65536 | tf_op jit(solution)/shard_map/all_to_all | solution.py:87
  37.8 3.9 %copy-start.29 = (s32[8,16]{1,0:T(8,128)S(1)}, s32[8,16]{1,0:T(8,128)}, u32[]{:S(2)}) copy-start(s32[8,16]{1,0:T(8,128)} %param.21) | copy-start | bytes 1540
  37.8 4.0 %copy-start.31 = (s32[128]{0:T(128)S(1)}, s32[128]{0:T(128)}, u32[]{:S(2)}) copy-start(s32[128]{0:T(128)} %param.20) | copy-start | bytes 1540
  37.8 4.8 %copy-start.25 = (f32[10,512]{1,0:T(8,128)S(1)}, f32[10,512]{1,0:T(8,128)}, u32[]{:S(2)}) copy-start(f32[10,512]{1,0:T(8,128)} %param.17) | copy-start | bytes 61444
  37.8 45.1 %all-to-all-start = ((bf16[128,4,3072]{0,2,1:T(8,128)(2,1)}), bf16[128,4,3072]{0,2,1:T(8,128)(2,1)S(1)}, u32[]{:S(2)}, u32[]{:S(2)}) async-start(bf16[128,4,3072]{0,2,1:T(8,128)(2,1)} %pad_maximum_fusion), calls=%async_computation | async-start | bytes 6291456 | tf_op jit(solution)/shard_map/all_to_all | solution.py:86
  41.7 148.6 %reduce-scatter.4.cloned.1.call-start = ((), (), s32[]{:S(2)}) async-start(), calls=%async_computation.6 | async-start | bytes 2359296 | tf_op jit(solution)/shard_map/reduce_scatter | solution.py:169
  43.0 1.8 copy-start.32
  96.3 10.4 %copy-start.3 = (bf16[16,128,2,128]{3,1,2,0:T(8,128)(2,1)S(1)}, bf16[16,128,2,128]{3,1,2,0:T(8,128)(2,1)}, u32[]{:S(2)}) copy-start(bf16[16,128,2,128]{3,1,2,0:T(8,128)(2,1)} %gather_fusion) | copy-start | bytes 3145732
  100.3 8.1 %copy-start.17 = (bf16[16,32,2,5,128]{4,3,2,1,0:T(8,128)(2,1)S(1)}, bf16[16,32,2,5,128]{4,3,2,1,0:T(8,128)(2,1)}, u32[]{:S(2)}) copy-start(bf16[16,32,2,5,128]{4,3,2,1,0:T(8,128)(2,1)} %reshape_reshape.14) | copy-start | bytes 3932164
  100.3 8.1 %copy-start.24 = (f32[16,2,5,32]{3,2,1,0:T(8,128)S(1)}, f32[16,2,5,32]{3,2,1,0:T(8,128)}, u32[]{:S(2)}) copy-start(f32[16,2,5,32]{3,2,1,0:T(8,128)} %get-tuple-element.43) | copy-start | bytes 61444
  100.3 38.6 %collective-permute-start = (bf16[512,2,128]{2,0,1:T(8,128)(2,1)}, bf16[512,2,128]{2,0,1:T(8,128)(2,1)}, u32[]{:S(2)}, u32[]{:S(2)}) collective-permute-start(bf16[512,2,128]{2,0,1:T(8,128)(2,1)} %copy.127), channel_id=1, source_target_pairs={{0,4},{4,8},{8,12},{12,16},{16,20},{20,24},{24,28},{28,32},{32,36}... | collective-permute-start | bytes 786440 | tf_op jit(solution)/shard_map/ppermute | solution.py:27
  103.3 41.2 %collective-permute-start.1 = (bf16[512,2,128]{2,0,1:T(8,128)(2,1)}, bf16[512,2,128]{2,0,1:T(8,128)(2,1)}, u32[]{:S(2)}, u32[]{:S(2)}) collective-permute-start(bf16[512,2,128]{2,0,1:T(8,128)(2,1)} %copy.133), channel_id=1, source_target_pairs={{0,4},{4,8},{8,12},{12,16},{16,20},{20,24},{24,28},{28,32},{32,36}... | collective-permute-start | bytes 786440 | tf_op jit(solution)/shard_map/ppermute | solution.py:27
  108.3 2.9 %copy-start.11 = (f32[16,2,128,32,5]{2,3,4,1,0:T(8,128)}, f32[16,2,128,32,5]{2,3,4,1,0:T(8,128)S(1)}, u32[]{:S(2)}) copy-start(f32[16,2,128,32,5]{2,3,4,1,0:T(8,128)S(1)} %fusion.38) | copy-start | bytes 7864324
  111.3 3.2 %copy-start.30 = (pred[16]{0:T(512)(128)(4,1)S(1)}, pred[16]{0:T(512)(128)(4,1)}, u32[]{:S(2)}) copy-start(pred[16]{0:T(512)(128)(4,1)} %compare_and_fusion) | copy-start | bytes 52
  118.5 2.1 copy-start.7
  120.7 3.3 %copy-start.6 = (f32[16,128,256]{2,0,1:T(8,128)S(1)}, f32[16,128,256]{2,0,1:T(8,128)}, u32[]{:S(2)}) copy-start(f32[16,128,256]{2,0,1:T(8,128)} %copy.165) | copy-start | bytes 6291460
  120.7 3.3 %copy-start.33 = (s32[16]{0:T(128)S(1)}, s32[16]{0:T(128)}, u32[]{:S(2)}) copy-start(s32[16]{0:T(128)} %copy-done.32) | copy-start | bytes 196
  127.1 2.6 %copy-start.8 = (bf16[16,2,5,32,128]{4,3,2,1,0:T(8,128)(2,1)S(1)}, bf16[16,2,5,32,128]{4,3,2,1,0:T(8,128)(2,1)}, u32[]{:S(2)}) copy-start(bf16[16,2,5,32,128]{4,3,2,1,0:T(8,128)(2,1)} %copy-done.7) | copy-start | bytes 3932164
  129.7 77.8 %reduce-scatter.6.cloned.1.call-start = ((), (), s32[]{:S(2)}) async-start(), calls=%async_computation.7 | async-start | bytes 393216 | tf_op jit(solution)/shard_map/reduce_scatter | solution.py:169
  134.1 4.8 %copy-start.4 = (bf16[512,1280]{0,1:T(8,128)(2,1)S(1)}, bf16[512,1280]{0,1:T(8,128)(2,1)}, u32[]{:S(2)}) copy-start(bf16[512,1280]{0,1:T(8,128)(2,1)} %copy.130) | copy-start | bytes 3932164
  141.4 4.4 %copy-start.1 = (f32[1024,512,5]{1,0,2:T(8,128)}, f32[1024,512,5]{1,0,2:T(8,128)S(1)}, u32[]{:S(2)}) copy-start(f32[1024,512,5]{1,0,2:T(8,128)S(1)} %fusion.47) | copy-start | bytes 31457284
  141.4 4.4 %copy-start.18 = (bf16[512,1280]{0,1:T(8,128)(2,1)S(1)}, bf16[512,1280]{0,1:T(8,128)(2,1)}, u32[]{:S(2)}) copy-start(bf16[512,1280]{0,1:T(8,128)(2,1)} %copy.135) | copy-start | bytes 3932164
  141.4 4.4 %copy-start.19 = (pred[512,1024]{0,1:T(8,128)(4,1)S(1)}, pred[512,1024]{0,1:T(8,128)(4,1)}, u32[]{:S(2)}) copy-start(pred[512,1024]{0,1:T(8,128)(4,1)} %fusion.25) | copy-start | bytes 1572868
  141.4 4.4 %copy-start.23 = (bf16[512,2,128]{2,0,1:T(8,128)(2,1)S(1)}, bf16[512,2,128]{2,0,1:T(8,128)(2,1)}, u32[]{:S(2)}) copy-start(bf16[512,2,128]{2,0,1:T(8,128)(2,1)} %copy.133) | copy-start | bytes 786436
  141.4 4.4 %copy-start.26 = (f32[5,512]{1,0:T(8,128)S(1)}, f32[5,512]{1,0:T(8,128)}, u32[]{:S(2)}) copy-start(f32[5,512]{1,0:T(8,128)} %get-tuple-element.34) | copy-start | bytes 30724
  141.4 4.4 %copy-start.28 = (f32[5,512]{1,0:T(8,128)S(1)}, f32[5,512]{1,0:T(8,128)}, u32[]{:S(2)}) copy-start(f32[5,512]{1,0:T(8,128)} %get-tuple-element.41) | copy-start | bytes 30724
  144.4 11.0 %copy-start = (f32[1024,512,5]{1,0,2:T(8,128)}, f32[1024,512,5]{1,0,2:T(8,128)S(1)}, u32[]{:S(2)}) copy-start(f32[1024,512,5]{1,0,2:T(8,128)S(1)} %fusion.48) | copy-start | bytes 31457284
  151.9 3.5 %copy-start.27 = (f32[5,512]{1,0:T(8,128)S(1)}, f32[5,512]{1,0:T(8,128)}, u32[]{:S(2)}) copy-start(f32[5,512]{1,0:T(8,128)} %get-tuple-element.40) | copy-start | bytes 30724
  159.9 2.4 copy-start.9
  164.1 9.3 %slice-start = ((s8[10485760]{0:T(1024)(128)(4,1)}), s8[2097152]{0:T(1024)(128)(4,1)S(1)}, s32[]{:S(2)}) async-start(s8[10485760]{0:T(1024)(128)(4,1)} %bitcast.194), calls=%async_computation.9 | async-start | bytes 4194304
  167.6 5.9 %slice-start.1 = ((s8[10485760]{0:T(1024)(128)(4,1)}), s8[4194304]{0:T(1024)(128)(4,1)S(1)}, s32[]{:S(2)}) async-start(s8[10485760]{0:T(1024)(128)(4,1)} %bitcast.194), calls=%async_computation.10 | async-start | bytes 8388608
  167.6 7.0 %slice-start.2 = ((s8[10485760]{0:T(1024)(128)(4,1)}), s8[4194304]{0:T(1024)(128)(4,1)S(1)}, s32[]{:S(2)}) async-start(s8[10485760]{0:T(1024)(128)(4,1)} %bitcast.194), calls=%async_computation.11 | async-start | bytes 8388608
  167.6 7.0 %copy-start.20 = (pred[512,1024]{0,1:T(8,128)(4,1)S(1)}, pred[512,1024]{0,1:T(8,128)(4,1)}, u32[]{:S(2)}) copy-start(pred[512,1024]{0,1:T(8,128)(4,1)} %fusion.25) | copy-start | bytes 1572868
  167.6 15.2 %slice-start.3 = ((s8[5242880]{0:T(1024)(128)(4,1)}), s8[4194304]{0:T(1024)(128)(4,1)S(1)}, s32[]{:S(2)}) async-start(s8[5242880]{0:T(1024)(128)(4,1)} %bitcast.206), calls=%async_computation.12 | async-start | bytes 8388608
  167.6 17.1 %slice-start.5 = ((s8[5242880]{0:T(1024)(128)(4,1)}), s8[4194304]{0:T(1024)(128)(4,1)S(1)}, s32[]{:S(2)}) async-start(s8[5242880]{0:T(1024)(128)(4,1)} %bitcast.208), calls=%async_computation.14 | async-start | bytes 8388608
  174.6 4.5 %copy-start.12 = (f32[1024,1,128]{0,2,1:T(8,128)}, f32[1024,1,128]{0,2,1:T(8,128)S(1)}, u32[]{:S(2)}) copy-start(f32[1024,1,128]{0,2,1:T(8,128)S(1)} %fusion.30) | copy-start | bytes 1572868
  174.6 8.3 %slice-start.4 = ((s8[5242880]{0:T(1024)(128)(4,1)}), s8[1048576]{0:T(1024)(128)(4,1)S(1)}, s32[]{:S(2)}) async-start(s8[5242880]{0:T(1024)(128)(4,1)} %bitcast.206), calls=%async_computation.13 | async-start | bytes 2097152
  174.6 10.1 %slice-start.6 = ((s8[5242880]{0:T(1024)(128)(4,1)}), s8[1048576]{0:T(1024)(128)(4,1)S(1)}, s32[]{:S(2)}) async-start(s8[5242880]{0:T(1024)(128)(4,1)} %bitcast.208), calls=%async_computation.15 | async-start | bytes 2097152
  179.1 5.6 %copy-start.14 = (f32[1024,1,128]{0,2,1:T(8,128)}, f32[1024,1,128]{0,2,1:T(8,128)S(1)}, u32[]{:S(2)}) copy-start(f32[1024,1,128]{0,2,1:T(8,128)S(1)} %fusion.33) | copy-start | bytes 1572868
  179.9 4.8 %copy-start.5 = (bf16[512,1280]{0,1:T(8,128)(2,1)S(1)}, bf16[512,1280]{0,1:T(8,128)(2,1)}, u32[]{:S(2)}) copy-start(bf16[512,1280]{0,1:T(8,128)(2,1)} %copy.130) | copy-start | bytes 3932164
  179.9 27.7 %collective-permute-start.3 = (bf16[512,2,128]{0,2,1:T(8,128)(2,1)}, bf16[512,2,128]{0,2,1:T(8,128)(2,1)}, u32[]{:S(2)}, u32[]{:S(2)}) collective-permute-start(bf16[512,2,128]{0,2,1:T(8,128)(2,1)} %fusion.56), channel_id=1, source_target_pairs={{4,0},{8,4},{12,8},{16,12},{20,16},{24,20},{28,24},{32,28},{36,32}... | collective-permute-start | bytes 786440 | tf_op jit(solution)/shard_map/ppermute | solution.py:27
  184.7 1.8 copy-start.15
  184.7 5.7 %copy-start.2 = (f32[512,1280]{1,0:T(8,128)S(1)}, f32[512,1280]{1,0:T(8,128)}, u32[]{:S(2)}) copy-start(f32[512,1280]{1,0:T(8,128)} %reshape.226) | copy-start | bytes 7864324
  186.5 0.8 copy-start.16
  187.3 22.2 %collective-permute-start.2 = (bf16[512,2,128]{0,2,1:T(8,128)(2,1)S(1)}, bf16[512,2,128]{0,2,1:T(8,128)(2,1)}, u32[]{:S(2)}, u32[]{:S(2)}) collective-permute-start(bf16[512,2,128]{0,2,1:T(8,128)(2,1)S(1)} %fusion.57), channel_id=1, source_target_pairs={{4,0},{8,4},{12,8},{16,12},{20,16},{24,20},{28,24},{32,28},{36,32}... | collective-permute-start | bytes 786440 | tf_op jit(solution)/shard_map/ppermute | solution.py:27
  190.3 17.2 %copy-start.13 = (f32[1024,1,128]{0,2,1:T(8,128)S(1)}, f32[1024,1,128]{0,2,1:T(8,128)}, u32[]{:S(2)}) copy-start(f32[1024,1,128]{0,2,1:T(8,128)} %copy-done.12) | copy-start | bytes 1572868
  190.3 42.8 %reduce-scatter.8.cloned.1.call-start = ((), (), s32[]{:S(2)}) async-start(), calls=%async_computation.8 | async-start | bytes 163840 | tf_op jit(solution)/shard_map/reduce_scatter | solution.py:169
Sparse Core Ops, SparseCore 0:
  26.6 40.8 all-gather.1
  129.8 42.3 reduce-scatter.3
  190.4 17.0 reduce-scatter.5
  209.9 23.2 reduce-scatter.7

commit v2 on v1

--- a/solution.py
+++ b/solution.py
@@ -136,8 +136,14 @@
         dv = jnp.stack(dv_parts, axis=1)
 
         pkv = jnp.concatenate([prefix_keys, prefix_values], axis=1)
-        for name in reversed(names):
-            pkv = lax.all_gather(pkv, name, axis=0, tiled=True)
+        nctx = math.prod(sizes)
+        pkv = lax.all_to_all(
+            jnp.broadcast_to(pkv[None], (nctx,) + pkv.shape),
+            names,
+            split_axis=0,
+            concat_axis=0,
+            tiled=True,
+        ).reshape(nctx * pkv.shape[0], pkv.shape[1])
         nprompt = pkv.shape[0] // PL
         pk_all = pkv[:, :lk].reshape(nprompt, PL, kvh, HD)
         pv_all = pkv[:, lk:].reshape(nprompt, PL, kvh, HD)
@@ -165,8 +171,13 @@
             precision=lax.Precision.HIGHEST,
             preferred_element_type=f32,
         ).reshape(nprompt * PL, 2 * lk)
-        for name in names:
-            pgrad = lax.psum_scatter(pgrad, name, scatter_dimension=0, tiled=True)
+        pgrad = lax.all_to_all(
+            pgrad.reshape(nctx, -1, pgrad.shape[1]),
+            names,
+            split_axis=0,
+            concat_axis=0,
+            tiled=True,
+        ).sum(axis=0)
 
         dq = dq + dq_p.reshape(tokens, kvh, grp, HD)
         back_k, back_v = shifted(

time: 246 us -> 228 us (0.927)
  starting transfers between devices: 19.6 us -> 45.5 us
  blocking collectives: 18.4 us -> 0 us
  between operations: 14.5 us -> 1.36 us
  waiting for transfers between devices: 56.8 us -> 51.7 us
  other arithmetic: 15.5 us -> 11 us
    reduce_scatter x3 -> x0, waiting for transfers between devices: 35.6 us -> none  [shards(): pgrad = lax.psum_scatter(pgrad, name, scatter_dimension=0, tiled=True)]
    all_to_all x0 -> x2, starting transfers between devices: none -> 25.7 us  [the longest x1 14.7 us: shards(): lax.all_to_all(jnp.broadcast_to(pkv[None], (nctx,) + pkv.shape), names, s...]
    all_to_all x0 -> x2, waiting for transfers between devices: none -> 23 us  [the longest x1 23 us: shards(): lax.all_to_all(jnp.broadcast_to(pkv[None], (nctx,) + pkv.shape), names, s...]
    all_gather x1 -> x0, waiting for transfers between devices: 21.2 us -> none  [shards(): pkv = lax.all_gather(pkv, name, axis=0, tiled=True)]
    all_gather x2 -> x0, blocking collectives: 18.4 us -> none  [shards(): pkv = lax.all_gather(pkv, name, axis=0, tiled=True)]
    all_to_all x1, waiting for transfers between devices: 0.01 us -> 16.8 us  [shards(): lax.all_to_all(packed, 'head', split_axis=1, concat_axis=0, tiled=True)]
    ppermute x4, waiting for transfers between devices: 0.01 us -> 7.94 us  [shifted(): return lax.ppermute(array, axes, pairs)]
    all_to_all x1, waiting for transfers between devices: 0.01 us -> 3.88 us  [shards(): lax.all_to_all(delta_rows.reshape(rows, nh, all_heads // nh), 'head', spl...]
  transfers between devices with their start and end apart: 10 -> 8, of which waited for: 3 -> 5; matrix products, arithmetic and copies ran while one was open for 45% -> 44% of each run, Pallas kernels for 0% -> 0%
where the time goes in v2:
time: 228 us; the launch traced here: 227 us
  local copies, waits for them, and re-layouts  67.1 us (29%)
  waiting for transfers between devices  51.7 us (23%)
  matrix products  49.9 us (22%)
  starting transfers between devices  45.5 us (20%)
  other arithmetic  11 us (5%)
    all_to_all x1, waiting for transfers between devices, shards(): lax.all_to_all(jnp.broadcast_to(pkv[None], (nctx,) + pkv.shape), names, s...  23 us
    all_to_all x1, waiting for transfers between devices, shards(): lax.all_to_all(packed, 'head', split_axis=1, concat_axis=0, tiled=True)  16.8 us
    all_to_all x1, starting transfers between devices, shards(): lax.all_to_all(jnp.broadcast_to(pkv[None], (nctx,) + pkv.shape), names, s...  14.7 us
    ppermute x4, starting transfers between devices, shifted(): return lax.ppermute(array, axes, pairs)  12.9 us
    all_to_all x1, starting transfers between devices, shards(): lax.all_to_all(pgrad.reshape(nctx, -1, pgrad.shape[1]), names, split_axis...  11 us
    dot_general x2, matrix products, shards(): dw = jnp.einsum('trd,sd->rts', dog, vg, preferred_element_type=f32)  10.5 us
    dot_general x2, matrix products, shards(): jnp.einsum('rts,trd->sd', wb, dog, preferred_element_type=f32)  10.3 us
    unnamed x86, local copies, waits for them, and re-layouts  9.04 us
  transfers between devices with their start and end apart: 8, of which 5 were waited for; matrix products, arithmetic and copies ran while one was open for 44% of the time, Pallas kernels for 0%

profile of v2, /device:TPU:22, one launch (start us, length us, event | category | flops | bytes accessed | tf_op | source)
XLA Modules:
  0.0 226.6 jit_solution(8846312914204989572)
XLA Ops:
  0.6 1.7 copy.249
  4.1 3.3 %all-to-all-start.1 = ((f32[128,4,10]{0,2,1:T(8,128)}), f32[128,4,10]{0,2,1:T(8,128)S(1)}, u32[]{:S(2)}, u32[]{:S(2)}) async-start(f32[128,4,10]{0,2,1:T(8,128)} %reshape.223), calls=%async_computation.1 | async-start | bytes 65536 | tf_op jit(solution)/shard_map/all_to_all | solution.py:87
  7.4 3.9 %all-to-all-done.1 = f32[128,4,10]{0,2,1:T(8,128)S(1)} async-done(((f32[128,4,10]{0,2,1:T(8,128)}), f32[128,4,10]{0,2,1:T(8,128)S(1)}, u32[]{:S(2)}, u32[]{:S(2)}) %all-to-all-start.1) | async-done | bytes 20512 | tf_op jit(solution)/shard_map/all_to_all | solution.py:87
  11.3 1.1 broadcast_in_dim.84
  12.4 14.7 %all-to-all-start.2 = ((bf16[64,16,512]{2,1,0:T(8,128)(2,1)}), bf16[64,16,512]{2,1,0:T(8,128)(2,1)}, u32[]{:S(2)}, u32[]{:S(2)}) async-start(bf16[64,16,512]{2,1,0:T(8,128)(2,1)} %broadcast_in_dim.84), calls=%async_computation.2 | async-start | bytes 2097152 | tf_op jit(solution)/shard_map/all_to_all | solution.py:140
  27.1 0.8 copy.169
  28.3 1.8 copy.168
  30.1 1.8 pad_maximum_fusion
  31.8 23.0 %all-to-all-done.2 = bf16[64,16,512]{2,1,0:T(8,128)(2,1)} async-done(((bf16[64,16,512]{2,1,0:T(8,128)(2,1)}), bf16[64,16,512]{2,1,0:T(8,128)(2,1)}, u32[]{:S(2)}, u32[]{:S(2)}) %all-to-all-start.2) | async-done | bytes 1048608 | tf_op jit(solution)/shard_map/all_to_all | solution.py:140
  54.9 3.7 %all-to-all-start = ((bf16[128,4,3072]{0,2,1:T(8,128)(2,1)}), bf16[128,4,3072]{0,2,1:T(8,128)(2,1)S(1)}, u32[]{:S(2)}, u32[]{:S(2)}) async-start(bf16[128,4,3072]{0,2,1:T(8,128)(2,1)} %pad_maximum_fusion), calls=%async_computation | async-start | bytes 6291456 | tf_op jit(solution)/shard_map/all_to_all | solution.py:86
  60.4 1.3 fusion.25
  63.2 2.2 fusion.93
  65.4 2.0 reshape.274
  67.4 1.9 copy.196
  69.3 2.0 reshape.273
  71.3 2.0 copy.192
  73.2 2.7 %gather_fusion.1 = bf16[16,128,2,128]{3,1,2,0:T(8,128)(2,1)} fusion(bf16[8,128,2,128]{3,1,2,0:T(8,128)(2,1)} %copy.196, s32[1024]{0:T(1024)S(1)} %pad_clamp_fusion), kind=kCustom, calls=%fused_computation.1.clone | custom fusion | bytes 2097216 | tf_op jit(solution)/shard_map/jit(_take)/gather | solution.py:151
  75.9 2.7 %gather_fusion = bf16[16,128,2,128]{3,1,2,0:T(8,128)(2,1)} fusion(bf16[8,128,2,128]{3,1,2,0:T(8,128)(2,1)} %copy.192, s32[1024]{0:T(1024)S(1)} %pad_clamp_fusion), kind=kCustom, calls=%fused_computation.clone | custom fusion | bytes 2097216 | tf_op jit(solution)/shard_map/jit(_take)/gather | solution.py:150
  78.6 16.8 %all-to-all-done = bf16[128,4,3072]{0,2,1:T(8,128)(2,1)S(1)} async-done(((bf16[128,4,3072]{0,2,1:T(8,128)(2,1)}), bf16[128,4,3072]{0,2,1:T(8,128)(2,1)S(1)}, u32[]{:S(2)}, u32[]{:S(2)}) %all-to-all-start) | async-done | bytes 3145760 | tf_op jit(solution)/shard_map/all_to_all | solution.py:86
  95.4 2.8 %copy.172 = bf16[4,128,1,3072]{3,1,0,2:T(8,128)(2,1)} copy(bf16[4,128,1,3072]{1,3,0,2:T(8,128)(2,1)S(1)} %bitcast.197) | data formatting | bytes 6291456 | tf_op jit(solution)/shard_map/all_to_all | solution.py:86
  98.2 1.9 fusion.91
  100.1 1.9 fusion.92
  102.0 1.5 copy.182
  103.5 2.4 %reshape_reshape.17 = bf16[16,32,2,5,128]{4,3,2,1,0:T(8,128)(2,1)} reshape(bf16[512,1280]{1,0:T(8,128)(2,1)S(1)} %get-tuple-element.35) | data formatting | bytes 2621440 | tf_op jit(solution)/shard_map/reshape;reshape | solution.py:153
  105.9 1.5 copy.177
  107.4 1.5 reshape_reshape.15
  108.9 1.2 copy.179
  110.0 0.8 copy.180
  110.9 1.1 copy.173
  112.0 0.8 copy.174
  112.8 4.5 %collective-permute-start = (bf16[512,2,128]{2,0,1:T(8,128)(2,1)}, bf16[512,2,128]{2,0,1:T(8,128)(2,1)}, u32[]{:S(2)}, u32[]{:S(2)}) collective-permute-start(bf16[512,2,128]{2,0,1:T(8,128)(2,1)} %copy.174), channel_id=1, source_target_pairs={{0,4},{4,8},{8,12},{12,16},{16,20},{20,24},{24,28},{28,32},{32,36}... | collective-permute-start | bytes 786440 | tf_op jit(solution)/shard_map/ppermute | solution.py:27
  117.3 3.1 %collective-permute-start.1 = (bf16[512,2,128]{2,0,1:T(8,128)(2,1)}, bf16[512,2,128]{2,0,1:T(8,128)(2,1)}, u32[]{:S(2)}, u32[]{:S(2)}) collective-permute-start(bf16[512,2,128]{2,0,1:T(8,128)(2,1)} %copy.180), channel_id=1, source_target_pairs={{0,4},{4,8},{8,12},{12,16},{16,20},{20,24},{24,28},{28,32},{32,36}... | collective-permute-start | bytes 786440 | tf_op jit(solution)/shard_map/ppermute | solution.py:27
  120.5 1.6 fusion.38
  122.1 2.9 %fusion.26 = f32[16,2,128,128,1]{3,2,4,1,0:T(8,128)} fusion(f32[16,2,128,32,5]{2,3,4,1,0:T(8,128)S(1)} %fusion.38, f32[16,2,5,32]{3,2,1,0:T(8,128)S(1)} %copy-done.19, bf16[16,32,2,5,128]{4,3,2,1,0:T(8,128)(2,1)S(1)} %copy-done.12), kind=kOutput, calls=%fused_computation.40 | convolution fusion | flops 169738240 | bytes 6049792 | tf_op jit(solution)/shard_map/bgrij,bigrd->bjgd/dot_general | solution.py:159
  125.0 3.2 %copy.212 = f32[16,128,256]{2,0,1:T(8,128)} copy(f32[16,128,256]{1,2,0:T(8,128)} %bitcast.215) | data formatting | bytes 4194304 | tf_op jit(solution)/shard_map/reshape | solution.py:169
  128.2 4.1 %fusion.21 = bf16[16,2,5,32,128]{4,3,2,1,0:T(8,128)(2,1)S(1)} fusion(f32[16,2,128,32,5]{2,3,4,1,0:T(8,128)} %copy-done.11, f32[16,2,5,32]{3,2,1,0:T(8,128)S(1)} %get-tuple-element.47, f32[16,2,5,32]{3,2,1,0:T(8,128)S(1)} %copy-done.19, bf16[16,128,2,128]{3,1,2,0:T(8,128)(2,1)} %gather_fusion.1, pred[16]{0:T(512)(128)(4,1)S(1)} %copy-done.27, ...), kind=kOutput, calls=%fused_computation.28 | convolution fusion | flops 171573248 | bytes 6332432 | tf_op jit(solution)/shard_map/bigrd,bjgd->bgrij/dot_general | solution.py:160
  132.3 2.1 fusion.44
  134.4 3.3 %copy.211 = f32[16,128,256]{2,0,1:T(8,128)} copy(f32[16,128,256]{1,2,0:T(8,128)} %bitcast.205) | data formatting | bytes 4194304 | tf_op jit(solution)/shard_map/reshape | solution.py:169
  137.7 3.1 %fusion.16 = f32[8,128,512]{2,0,1:T(8,128)S(1)} fusion(f32[16,128,256]{2,0,1:T(8,128)S(1)} %copy-done.6, f32[16,128,256]{2,0,1:T(8,128)} %copy.211, s32[16]{0:T(128)S(1)} %copy-done.30), kind=kOutput, calls=%fused_computation.20 | convolution fusion | flops 101712000 | bytes 6291520 | tf_op jit(solution)/shard_map/bp,bjx->pjx/dot_general | solution.py:165
  140.8 2.6 %copy.213 = f32[8,128,512]{2,1,0:T(8,128)} copy(f32[8,128,512]{2,0,1:T(8,128)S(1)} %fusion.16) | data formatting | bytes 4194304 | tf_op jit(solution)/shard_map/bp,bjx->pjx/dot_general | solution.py:165
  143.4 11.0 %all-to-all-start.3 = ((f32[64,16,512]{2,1,0:T(8,128)}), f32[64,16,512]{2,1,0:T(8,128)}, u32[]{:S(2)}, u32[]{:S(2)}) async-start(f32[64,16,512]{2,1,0:T(8,128)} %bitcast.68), calls=%async_computation.3 | async-start | bytes 4194304 | tf_op jit(solution)/shard_map/all_to_all | solution.py:174
  155.0 3.7 %copy.199 = f32[16,32,2,5,128]{4,3,2,1,0:T(8,128)} copy(f32[16,32,2,5,128]{4,1,3,2,0:T(8,128)S(1)} %convolution_bitcast_fusion) | data formatting | bytes 5242880 | tf_op jit(solution)/shard_map/bgrij,bjgd->bigrd/transpose | solution.py:162
  158.8 4.8 %reshape.228 = f32[512,1280]{1,0:T(8,128)} reshape(f32[16,32,2,5,128]{4,3,2,1,0:T(8,128)} %copy.199) | data formatting | bytes 5242880 | tf_op jit(solution)/shard_map/reshape | solution.py:182
  163.6 2.5 %fusion.47 = f32[1024,512,5]{1,0,2:T(8,128)S(1)} fusion(bf16[512,2,5,128]{0,3,2,1:T(8,128)(2,1)S(1)} %bitcast.201, bf16[512,2,128]{2,0,1:T(8,128)(2,1)} %collective-permute-done, bf16[512,2,128]{2,0,1:T(8,128)(2,1)} %copy.174), kind=kOutput, calls=%fused_computation.67 | convolution fusion | flops 671612928 | bytes 11665408 | tf_op jit(solution)/shard_map/trd,sd->rts/dot_general | solution.py:124
  166.1 3.0 %fusion.48 = f32[1024,512,5]{1,0,2:T(8,128)S(1)} fusion(bf16[512,2,5,128]{0,3,2,1:T(8,128)(2,1)S(1)} %bitcast.202, bf16[512,2,128]{2,0,1:T(8,128)(2,1)} %copy.174, bf16[512,2,128]{2,0,1:T(8,128)(2,1)} %collective-permute-done), kind=kOutput, calls=%fused_computation.68 | convolution fusion | flops 671612928 | bytes 11665408 | tf_op jit(solution)/shard_map/trd,sd->rts/dot_general | solution.py:124
  169.1 1.3 copy-done.1
  170.5 6.1 %fusion.5 = bf16[5,512,1024]{1,2,0:T(8,128)(2,1)} fusion(f32[1024,512,5]{1,0,2:T(8,128)S(1)} %fusion.47, f32[5,512]{1,0:T(8,128)S(1)} %copy-done.23, f32[5,512]{1,0:T(8,128)S(1)} %copy-done.21, pred[512,1024]{0,1:T(8,128)(4,1)S(1)} %copy-done.14, bf16[512,2,5,128]{0,3,2,1:T(8,128)(2,1)S(1)} %bitcast.219, bf16[512,2,128]{2,0,1:T(8,128)(2,1)} %collective-permute-done.1, ...), kind=kOutput, calls=%fused_computation.10 | convolution fusion | flops 687341568 | bytes 17465344 | tf_op jit(solution)/shard_map/trd,sd->rts/dot_general | solution.py:130
  176.5 3.5 %convolution_bitcast_fusion.2 = f32[512,1,5,128]{0,3,2,1:T(8,128)S(1)} fusion(bf16[5,512,1024]{1,2,0:T(8,128)(2,1)} %fusion.5, bf16[512,2,128]{2,0,1:T(8,128)(2,1)} %collective-permute-done, bf16[512,2,128]{2,0,1:T(8,128)(2,1)} %copy.174), kind=kOutput, calls=%fused_computation.39 | convolution fusion | flops 671612928 | bytes 7077888 | tf_op jit(solution)/shard_map/rts,sd->trd/dot_general | solution.py:132
  180.1 4.5 %fusion.1 = bf16[5,512,1024]{1,2,0:T(8,128)(2,1)S(1)} fusion(f32[1024,512,5]{1,0,2:T(8,128)S(1)} %fusion.48, f32[5,512]{1,0:T(8,128)S(1)} %copy-done.22, f32[5,512]{1,0:T(8,128)S(1)} %get-tuple-element.40, pred[512,1024]{0,1:T(8,128)(4,1)S(1)} %copy-done.14, bf16[512,2,5,128]{0,3,2,1:T(8,128)(2,1)S(1)} %bitcast.220, bf16[512,2,128]{2,0,1:T(8,128)(2,1)S(1)} %copy-done.18, ...), kind=kOutput, calls=%fused_computation.4 | convolution fusion | flops 687341568 | bytes 17465344 | tf_op jit(solution)/shard_map/trd,sd->rts/dot_general | solution.py:130
  184.6 2.2 convolution_bitcast_fusion.1
  187.0 1.9 pad_maximum_fusion.1
  188.8 3.4 %copy.200 = f32[512,1280]{1,0:T(8,128)} copy(f32[512,1280]{0,1:T(8,128)} %bitcast.200) | data formatting | bytes 5242880 | tf_op jit(solution)/shard_map/stack | solution.py:134
  192.2 6.0 %fusion.30 = f32[1024,1,128]{0,2,1:T(8,128)S(1)} fusion(f32[1024,512,5]{1,0,2:T(8,128)} %copy-done.1, f32[5,512]{1,0:T(8,128)S(1)} %copy-done.21, pred[512,1024]{0,1:T(8,128)(4,1)} %fusion.25, bf16[512,2,5,128]{0,3,2,1:T(8,128)(2,1)} %bitcast.217), kind=kOutput, calls=%fused_computation.45 | convolution fusion | flops 681574400 | bytes 12199936 | tf_op jit(solution)/shard_map/rts,trd->sd/dot_general | solution.py:129
  199.1 4.3 %fusion.33 = f32[1024,1,128]{0,2,1:T(8,128)S(1)} fusion(f32[1024,512,5]{1,0,2:T(8,128)S(1)} %bitcast.196, f32[5,512]{1,0:T(8,128)S(1)} %get-tuple-element.40, pred[512,1024]{0,1:T(8,128)(4,1)S(1)} %copy-done.15, bf16[512,2,5,128]{0,3,2,1:T(8,128)(2,1)} %bitcast.218), kind=kOutput, calls=%fused_computation.46 | convolution fusion | flops 681574400 | bytes 12199936 | tf_op jit(solution)/shard_map/rts,trd->sd/dot_general | solution.py:129
  203.4 2.8 %collective-permute-start.3 = (bf16[512,2,128]{0,2,1:T(8,128)(2,1)S(1)}, bf16[512,2,128]{0,2,1:T(8,128)(2,1)S(1)}, u32[]{:S(2)}, u32[]{:S(2)}) collective-permute-start(bf16[512,2,128]{0,2,1:T(8,128)(2,1)S(1)} %fusion.56), channel_id=1, source_target_pairs={{4,0},{8,4},{12,8},{16,12},{20,16},{24,20},{28,24},{32,28},{36,32}... | collective-permute-start | bytes 786440 | tf_op jit(solution)/shard_map/ppermute | solution.py:27
  206.2 1.8 convolution_bitcast_fusion.4
  208.1 1.8 convolution_bitcast_fusion.3
  209.9 2.5 %collective-permute-start.2 = (bf16[512,2,128]{0,2,1:T(8,128)(2,1)S(1)}, bf16[512,2,128]{0,2,1:T(8,128)(2,1)S(1)}, u32[]{:S(2)}, u32[]{:S(2)}) collective-permute-start(bf16[512,2,128]{0,2,1:T(8,128)(2,1)S(1)} %fusion.57), channel_id=1, source_target_pairs={{4,0},{8,4},{12,8},{16,12},{20,16},{24,20},{28,24},{32,28},{36,32}... | collective-permute-start | bytes 786440 | tf_op jit(solution)/shard_map/ppermute | solution.py:27
  212.4 1.4 multiply_convert_fusion
  213.8 2.6 %collective-permute-done.3 = bf16[512,2,128]{0,2,1:T(8,128)(2,1)S(1)} collective-permute-done((bf16[512,2,128]{0,2,1:T(8,128)(2,1)S(1)}, bf16[512,2,128]{0,2,1:T(8,128)(2,1)S(1)}, u32[]{:S(2)}, u32[]{:S(2)}) %collective-permute-start.3) | collective-permute-done | bytes 262176 | tf_op jit(solution)/shard_map/ppermute | solution.py:27
  216.5 0.8 copy.215
  217.4 5.3 %collective-permute-done.2 = bf16[512,2,128]{0,2,1:T(8,128)(2,1)S(1)} collective-permute-done((bf16[512,2,128]{0,2,1:T(8,128)(2,1)S(1)}, bf16[512,2,128]{0,2,1:T(8,128)(2,1)S(1)}, u32[]{:S(2)}, u32[]{:S(2)}) %collective-permute-start.2) | collective-permute-done | bytes 262176 | tf_op jit(solution)/shard_map/ppermute | solution.py:27
  222.8 0.8 copy.214
  223.6 1.7 reduce_sum.39
  (119 shorter events, 8.5 us)
Async XLA Ops:
  0.6 1.7 copy-start.10
  2.3 5.0 %copy-start.24 = (bf16[16,256]{1,0:T(8,128)(2,1)S(1)}, bf16[16,256]{1,0:T(8,128)(2,1)}, u32[]{:S(2)}) copy-start(bf16[16,256]{1,0:T(8,128)(2,1)} %param.19) | copy-start | bytes 24580
  2.3 5.1 %copy-start.25 = (bf16[16,256]{1,0:T(8,128)(2,1)S(1)}, bf16[16,256]{1,0:T(8,128)(2,1)}, u32[]{:S(2)}) copy-start(bf16[16,256]{1,0:T(8,128)(2,1)} %param.18) | copy-start | bytes 24580
  4.1 7.2 %all-to-all-start.1 = ((f32[128,4,10]{0,2,1:T(8,128)}), f32[128,4,10]{0,2,1:T(8,128)S(1)}, u32[]{:S(2)}, u32[]{:S(2)}) async-start(f32[128,4,10]{0,2,1:T(8,128)} %reshape.223), calls=%async_computation.1 | async-start | bytes 65536 | tf_op jit(solution)/shard_map/all_to_all | solution.py:87
  12.4 15.5 %copy-start.16 = (bf16[128,1024]{1,0:T(8,128)(2,1)S(1)}, bf16[128,1024]{1,0:T(8,128)(2,1)}, u32[]{:S(2)}) copy-start(bf16[128,1024]{1,0:T(8,128)(2,1)} %param.13) | copy-start | bytes 786436
  12.4 15.7 %copy-start.17 = (bf16[128,1024]{1,0:T(8,128)(2,1)S(1)}, bf16[128,1024]{1,0:T(8,128)(2,1)}, u32[]{:S(2)}) copy-start(bf16[128,1024]{1,0:T(8,128)(2,1)} %param.14) | copy-start | bytes 786436
  12.4 42.5 %all-to-all-start.2 = ((bf16[64,16,512]{2,1,0:T(8,128)(2,1)}), bf16[64,16,512]{2,1,0:T(8,128)(2,1)}, u32[]{:S(2)}, u32[]{:S(2)}) async-start(bf16[64,16,512]{2,1,0:T(8,128)(2,1)} %broadcast_in_dim.84), calls=%async_computation.2 | async-start | bytes 2097152 | tf_op jit(solution)/shard_map/all_to_all | solution.py:140
  31.8 26.8 %copy-start.26 = (s32[8,16]{1,0:T(8,128)S(1)}, s32[8,16]{1,0:T(8,128)}, u32[]{:S(2)}) copy-start(s32[8,16]{1,0:T(8,128)} %param.21) | copy-start | bytes 1540
  31.8 26.9 %copy-start.28 = (s32[128]{0:T(128)S(1)}, s32[128]{0:T(128)}, u32[]{:S(2)}) copy-start(s32[128]{0:T(128)} %param.20) | copy-start | bytes 1540
  31.8 27.6 %copy-start.20 = (f32[10,512]{1,0:T(8,128)S(1)}, f32[10,512]{1,0:T(8,128)}, u32[]{:S(2)}) copy-start(f32[10,512]{1,0:T(8,128)} %param.17) | copy-start | bytes 61444
  54.9 40.6 %all-to-all-start = ((bf16[128,4,3072]{0,2,1:T(8,128)(2,1)}), bf16[128,4,3072]{0,2,1:T(8,128)(2,1)S(1)}, u32[]{:S(2)}, u32[]{:S(2)}) async-start(bf16[128,4,3072]{0,2,1:T(8,128)(2,1)} %pad_maximum_fusion), calls=%async_computation | async-start | bytes 6291456 | tf_op jit(solution)/shard_map/all_to_all | solution.py:86
  59.8 1.8 copy-start.29
  108.8 11.6 %copy-start.4 = (bf16[16,128,2,128]{3,1,2,0:T(8,128)(2,1)S(1)}, bf16[16,128,2,128]{3,1,2,0:T(8,128)(2,1)}, u32[]{:S(2)}) copy-start(bf16[16,128,2,128]{3,1,2,0:T(8,128)(2,1)} %gather_fusion) | copy-start | bytes 3145732
  112.8 9.3 %copy-start.12 = (bf16[16,32,2,5,128]{4,3,2,1,0:T(8,128)(2,1)S(1)}, bf16[16,32,2,5,128]{4,3,2,1,0:T(8,128)(2,1)}, u32[]{:S(2)}) copy-start(bf16[16,32,2,5,128]{4,3,2,1,0:T(8,128)(2,1)} %reshape_reshape.17) | copy-start | bytes 3932164
  112.8 9.3 %copy-start.19 = (f32[16,2,5,32]{3,2,1,0:T(8,128)S(1)}, f32[16,2,5,32]{3,2,1,0:T(8,128)}, u32[]{:S(2)}) copy-start(f32[16,2,5,32]{3,2,1,0:T(8,128)} %get-tuple-element.48) | copy-start | bytes 61444
  112.8 50.8 %collective-permute-start = (bf16[512,2,128]{2,0,1:T(8,128)(2,1)}, bf16[512,2,128]{2,0,1:T(8,128)(2,1)}, u32[]{:S(2)}, u32[]{:S(2)}) collective-permute-start(bf16[512,2,128]{2,0,1:T(8,128)(2,1)} %copy.174), channel_id=1, source_target_pairs={{0,4},{4,8},{8,12},{12,16},{16,20},{20,24},{24,28},{28,32},{32,36}... | collective-permute-start | bytes 786440 | tf_op jit(solution)/shard_map/ppermute | solution.py:27
  117.3 51.8 %collective-permute-start.1 = (bf16[512,2,128]{2,0,1:T(8,128)(2,1)}, bf16[512,2,128]{2,0,1:T(8,128)(2,1)}, u32[]{:S(2)}, u32[]{:S(2)}) collective-permute-start(bf16[512,2,128]{2,0,1:T(8,128)(2,1)} %copy.180), channel_id=1, source_target_pairs={{0,4},{4,8},{8,12},{12,16},{16,20},{20,24},{24,28},{28,32},{32,36}... | collective-permute-start | bytes 786440 | tf_op jit(solution)/shard_map/ppermute | solution.py:27
  122.1 2.9 %copy-start.11 = (f32[16,2,128,32,5]{2,3,4,1,0:T(8,128)}, f32[16,2,128,32,5]{2,3,4,1,0:T(8,128)S(1)}, u32[]{:S(2)}) copy-start(f32[16,2,128,32,5]{2,3,4,1,0:T(8,128)S(1)} %fusion.38) | copy-start | bytes 7864324
  125.0 3.2 %copy-start.27 = (pred[16]{0:T(512)(128)(4,1)S(1)}, pred[16]{0:T(512)(128)(4,1)}, u32[]{:S(2)}) copy-start(pred[16]{0:T(512)(128)(4,1)} %compare_and_fusion) | copy-start | bytes 52
  132.3 2.1 copy-start.7
  134.4 3.3 %copy-start.6 = (f32[16,128,256]{2,0,1:T(8,128)S(1)}, f32[16,128,256]{2,0,1:T(8,128)}, u32[]{:S(2)}) copy-start(f32[16,128,256]{2,0,1:T(8,128)} %copy.212) | copy-start | bytes 6291460
  134.4 3.3 %copy-start.30 = (s32[16]{0:T(128)S(1)}, s32[16]{0:T(128)}, u32[]{:S(2)}) copy-start(s32[16]{0:T(128)} %copy-done.29) | copy-start | bytes 196
  143.4 11.0 %copy-start.8 = (bf16[16,2,5,32,128]{4,3,2,1,0:T(8,128)(2,1)S(1)}, bf16[16,2,5,32,128]{4,3,2,1,0:T(8,128)(2,1)}, u32[]{:S(2)}) copy-start(bf16[16,2,5,32,128]{4,3,2,1,0:T(8,128)(2,1)} %copy-done.7) | copy-start | bytes 3932164
  143.4 80.2 %all-to-all-start.3 = ((f32[64,16,512]{2,1,0:T(8,128)}), f32[64,16,512]{2,1,0:T(8,128)}, u32[]{:S(2)}, u32[]{:S(2)}) async-start(f32[64,16,512]{2,1,0:T(8,128)} %bitcast.68), calls=%async_computation.3 | async-start | bytes 4194304 | tf_op jit(solution)/shard_map/all_to_all | solution.py:174
  158.7 4.8 %copy-start.5 = (bf16[512,1280]{0,1:T(8,128)(2,1)S(1)}, bf16[512,1280]{0,1:T(8,128)(2,1)}, u32[]{:S(2)}) copy-start(bf16[512,1280]{0,1:T(8,128)(2,1)} %copy.177) | copy-start | bytes 3932164
  166.0 4.4 %copy-start.1 = (f32[1024,512,5]{1,0,2:T(8,128)}, f32[1024,512,5]{1,0,2:T(8,128)S(1)}, u32[]{:S(2)}) copy-start(f32[1024,512,5]{1,0,2:T(8,128)S(1)} %fusion.47) | copy-start | bytes 31457284
  166.1 4.4 %copy-start.13 = (bf16[512,1280]{0,1:T(8,128)(2,1)S(1)}, bf16[512,1280]{0,1:T(8,128)(2,1)}, u32[]{:S(2)}) copy-start(bf16[512,1280]{0,1:T(8,128)(2,1)} %copy.182) | copy-start | bytes 3932164
  166.1 4.4 %copy-start.14 = (pred[512,1024]{0,1:T(8,128)(4,1)S(1)}, pred[512,1024]{0,1:T(8,128)(4,1)}, u32[]{:S(2)}) copy-start(pred[512,1024]{0,1:T(8,128)(4,1)} %fusion.25) | copy-start | bytes 1572868
  166.1 4.4 %copy-start.18 = (bf16[512,2,128]{2,0,1:T(8,128)(2,1)S(1)}, bf16[512,2,128]{2,0,1:T(8,128)(2,1)}, u32[]{:S(2)}) copy-start(bf16[512,2,128]{2,0,1:T(8,128)(2,1)} %copy.180) | copy-start | bytes 786436
  166.1 4.4 %copy-start.21 = (f32[5,512]{1,0:T(8,128)S(1)}, f32[5,512]{1,0:T(8,128)}, u32[]{:S(2)}) copy-start(f32[5,512]{1,0:T(8,128)} %get-tuple-element.39) | copy-start | bytes 30724
  166.1 4.4 %copy-start.23 = (f32[5,512]{1,0:T(8,128)S(1)}, f32[5,512]{1,0:T(8,128)}, u32[]{:S(2)}) copy-start(f32[5,512]{1,0:T(8,128)} %get-tuple-element.46) | copy-start | bytes 30724
  169.1 11.0 %copy-start = (f32[1024,512,5]{1,0,2:T(8,128)}, f32[1024,512,5]{1,0,2:T(8,128)S(1)}, u32[]{:S(2)}) copy-start(f32[1024,512,5]{1,0,2:T(8,128)S(1)} %fusion.48) | copy-start | bytes 31457284
  176.5 3.5 %copy-start.22 = (f32[5,512]{1,0:T(8,128)S(1)}, f32[5,512]{1,0:T(8,128)}, u32[]{:S(2)}) copy-start(f32[5,512]{1,0:T(8,128)} %get-tuple-element.45) | copy-start | bytes 30724
  184.6 2.4 %copy-start.9 = (bf16[5,512,1024]{1,2,0:T(8,128)(2,1)}, bf16[5,512,1024]{1,2,0:T(8,128)(2,1)S(1)}, u32[]{:S(2)}) copy-start(bf16[5,512,1024]{1,2,0:T(8,128)(2,1)S(1)} %fusion.1) | copy-start | bytes 15728644
  188.8 9.4 %slice-start = ((s8[10485760]{0:T(1024)(128)(4,1)}), s8[2097152]{0:T(1024)(128)(4,1)S(1)}, s32[]{:S(2)}) async-start(s8[10485760]{0:T(1024)(128)(4,1)} %bitcast.195), calls=%async_computation.4 | async-start | bytes 4194304
  192.2 6.1 %slice-start.1 = ((s8[10485760]{0:T(1024)(128)(4,1)}), s8[4194304]{0:T(1024)(128)(4,1)S(1)}, s32[]{:S(2)}) async-start(s8[10485760]{0:T(1024)(128)(4,1)} %bitcast.195), calls=%async_computation.5 | async-start | bytes 8388608
  192.2 6.9 %slice-start.2 = ((s8[10485760]{0:T(1024)(128)(4,1)}), s8[4194304]{0:T(1024)(128)(4,1)S(1)}, s32[]{:S(2)}) async-start(s8[10485760]{0:T(1024)(128)(4,1)} %bitcast.195), calls=%async_computation.6 | async-start | bytes 8388608
  192.2 6.9 %copy-start.15 = (pred[512,1024]{0,1:T(8,128)(4,1)S(1)}, pred[512,1024]{0,1:T(8,128)(4,1)}, u32[]{:S(2)}) copy-start(pred[512,1024]{0,1:T(8,128)(4,1)} %fusion.25) | copy-start | bytes 1572868
  192.2 14.0 %slice-start.3 = ((s8[5242880]{0:T(1024)(128)(4,1)}), s8[4194304]{0:T(1024)(128)(4,1)S(1)}, s32[]{:S(2)}) async-start(s8[5242880]{0:T(1024)(128)(4,1)} %bitcast.206), calls=%async_computation.7 | async-start | bytes 8388608
  192.2 15.8 %slice-start.5 = ((s8[5242880]{0:T(1024)(128)(4,1)}), s8[4194304]{0:T(1024)(128)(4,1)S(1)}, s32[]{:S(2)}) async-start(s8[5242880]{0:T(1024)(128)(4,1)} %bitcast.208), calls=%async_computation.9 | async-start | bytes 8388608
  199.1 7.1 %slice-start.4 = ((s8[5242880]{0:T(1024)(128)(4,1)}), s8[1048576]{0:T(1024)(128)(4,1)S(1)}, s32[]{:S(2)}) async-start(s8[5242880]{0:T(1024)(128)(4,1)} %bitcast.206), calls=%async_computation.8 | async-start | bytes 2097152
  199.1 8.9 %slice-start.6 = ((s8[5242880]{0:T(1024)(128)(4,1)}), s8[1048576]{0:T(1024)(128)(4,1)S(1)}, s32[]{:S(2)}) async-start(s8[5242880]{0:T(1024)(128)(4,1)} %bitcast.208), calls=%async_computation.10 | async-start | bytes 2097152
  203.4 13.0 %collective-permute-start.3 = (bf16[512,2,128]{0,2,1:T(8,128)(2,1)S(1)}, bf16[512,2,128]{0,2,1:T(8,128)(2,1)S(1)}, u32[]{:S(2)}, u32[]{:S(2)}) collective-permute-start(bf16[512,2,128]{0,2,1:T(8,128)(2,1)S(1)} %fusion.56), channel_id=1, source_target_pairs={{4,0},{8,4},{12,8},{16,12},{20,16},{24,20},{28,24},{32,28},{36,32}... | collective-permute-start | bytes 786440 | tf_op jit(solution)/shard_map/ppermute | solution.py:27
  208.0 4.3 %copy-start.2 = (f32[512,1280]{1,0:T(8,128)S(1)}, f32[512,1280]{1,0:T(8,128)}, u32[]{:S(2)}) copy-start(f32[512,1280]{1,0:T(8,128)} %reshape.228) | copy-start | bytes 7864324
  208.1 4.3 %copy-start.3 = (f32[512,1280]{1,0:T(8,128)S(1)}, f32[512,1280]{1,0:T(8,128)}, u32[]{:S(2)}) copy-start(f32[512,1280]{1,0:T(8,128)} %copy.200) | copy-start | bytes 7864324
  209.9 12.8 %collective-permute-start.2 = (bf16[512,2,128]{0,2,1:T(8,128)(2,1)S(1)}, bf16[512,2,128]{0,2,1:T(8,128)(2,1)S(1)}, u32[]{:S(2)}, u32[]{:S(2)}) collective-permute-start(bf16[512,2,128]{0,2,1:T(8,128)(2,1)S(1)} %fusion.57), channel_id=1, source_target_pairs={{4,0},{8,4},{12,8},{16,12},{20,16},{24,20},{28,24},{32,28},{36,32}... | collective-permute-start | bytes 786440 | tf_op jit(solution)/shard_map/ppermute | solution.py:27

commit v3 on v2

--- a/solution.py
+++ b/solution.py
@@ -4,6 +4,8 @@
 import jax.numpy as jnp
 import numpy as np
 from jax import lax
+from jax.experimental import pallas as pl
+from jax.experimental.pallas import tpu as pltpu
 from jax.sharding import Mesh
 from jax.sharding import PartitionSpec as P
 
@@ -43,6 +45,88 @@
     chosen = numbers[None, :] == current[:, None]
     prompt_block = jnp.sum(jnp.where(chosen, prompt_of[None, :], 0), axis=1)
     return first, prompt_block
+
+
+TT = 256
+
+
+def tile_body(q_ref, do_ref, k_ref, v_ref, n_ref, d_ref, ls_ref, dq_ref, dk_ref, dv_ref):
+    i = pl.program_id(1)
+    f32, bf16 = jnp.float32, jnp.bfloat16
+    scale = 1.0 / math.sqrt(HD)
+    keys, values = k_ref[...], v_ref[...]
+    span, rows = keys.shape[0], q_ref.shape[0]
+    own = span // 2
+    tok = i * rows + lax.broadcasted_iota(jnp.int32, (span, rows), 1)
+    u = lax.broadcasted_iota(jnp.int32, (span, rows), 0) - own
+    allowed = (u >= ls_ref[...]) & (u <= tok)
+    nrm, dlt = n_ref[0], d_ref[0]
+    nt = (((1,), (1,)), ((), ()))
+    dk_acc = jnp.zeros((span, HD), f32)
+    dv_acc = jnp.zeros((span, HD), f32)
+    for r in range(nrm.shape[0]):
+        cols = slice(r * HD, (r + 1) * HD)
+        qr, dor = q_ref[:, cols], do_ref[:, cols]
+        st = lax.dot_general(keys, qr, nt, preferred_element_type=f32)
+        wt = jnp.where(allowed, jnp.exp(st * scale - nrm[r : r + 1, :]), 0.0)
+        dv_acc = dv_acc + jnp.dot(wt.astype(bf16), dor, preferred_element_type=f32)
+        dwt = lax.dot_general(values, dor, nt, preferred_element_type=f32)
+        dlt_r = wt * (dwt - dlt[r : r + 1, :])
+        dlb = dlt_r.astype(bf16)
+        dk_acc = dk_acc + jnp.dot(dlb, qr, preferred_element_type=f32)
+        dq_ref[:, cols] = jnp.dot(
+            dlt_r.T.astype(bf16), keys, preferred_element_type=f32
+        )
+
+    @pl.when(i == 0)
+    def _():
+        dk_ref[...] = dk_acc
+        dv_ref[...] = dv_acc
+
+    @pl.when(i > 0)
+    def _():
+        dk_ref[...] += dk_acc
+        dv_ref[...] += dv_acc
+
+
+def tile_kernel(q, do, keys, values, norms, delta, local_start):
+    tokens, lq = q.shape
+    span, lk = keys.shape
+    kvh, grp = norms.shape[0], norms.shape[1]
+    rows = min(TT, tokens)
+    width = grp * HD
+    flops = 10 * tokens * span * HD * kvh * grp
+    return pl.pallas_call(
+        tile_body,
+        grid=(kvh, tokens // rows),
+        in_specs=[
+            pl.BlockSpec((rows, width), lambda g, i: (i, g)),
+            pl.BlockSpec((rows, width), lambda g, i: (i, g)),
+            pl.BlockSpec((span, HD), lambda g, i: (0, g)),
+            pl.BlockSpec((span, HD), lambda g, i: (0, g)),
+            pl.BlockSpec((1, grp, rows), lambda g, i: (g, 0, i)),
+            pl.BlockSpec((1, grp, rows), lambda g, i: (g, 0, i)),
+            pl.BlockSpec((1, rows), lambda g, i: (0, i)),
+        ],
+        out_specs=[
+            pl.BlockSpec((rows, width), lambda g, i: (i, g)),
+            pl.BlockSpec((span, HD), lambda g, i: (0, g)),
+            pl.BlockSpec((span, HD), lambda g, i: (0, g)),
+        ],
+        out_shape=[
+            jax.ShapeDtypeStruct((tokens, lq), jnp.float32),
+            jax.ShapeDtypeStruct((span, lk), jnp.float32),
+            jax.ShapeDtypeStruct((span, lk), jnp.float32),
+        ],
+        compiler_params=pltpu.CompilerParams(
+            dimension_semantics=("arbitrary", "arbitrary")
+        ),
+        cost_estimate=pl.CostEstimate(
+            flops=flops,
+            transcendentals=tokens * span * kvh * grp,
+            bytes_accessed=4 * tokens * lq * 2 + 2 * span * lk * 5,
+        ),
+    )(q, do, keys, values, norms, delta, local_start)
 
 
 def make_shards(parts):
@@ -112,28 +196,19 @@
         local_start = jnp.repeat(first * BLK, BLK) - base
 
         k_prior, v_prior = shifted((k, v), names, sizes, 1)
-        keys = jnp.concatenate([k_prior, k], axis=0)
-        values = jnp.concatenate([v_prior, v], axis=0)
-        u = jnp.arange(2 * tokens, dtype=jnp.int32) - tokens
-        t = jnp.arange(tokens, dtype=jnp.int32)
-        allowed = (u[None, :] >= local_start[:, None]) & (u[None, :] <= t[:, None])
-
-        dq_parts, dk_parts, dv_parts = [], [], []
-        for g in range(kvh):
-            qg, dog, kg, vg = q[:, g], do[:, g], keys[:, g], values[:, g]
-            logits = jnp.einsum("trd,sd->rts", qg, kg, preferred_element_type=f32)
-            w = jnp.where(
-                allowed[None], jnp.exp(logits * scale - norms[g][:, :, None]), 0.0
-            )
-            wb = w.astype(bf16)
-            dv_parts.append(jnp.einsum("rts,trd->sd", wb, dog, preferred_element_type=f32))
-            dw = jnp.einsum("trd,sd->rts", dog, vg, preferred_element_type=f32)
-            dl = (w * (dw - delta[g][:, :, None])).astype(bf16)
-            dq_parts.append(jnp.einsum("rts,sd->trd", dl, kg, preferred_element_type=f32))
-            dk_parts.append(jnp.einsum("rts,trd->sd", dl, qg, preferred_element_type=f32))
-        dq = jnp.stack(dq_parts, axis=1)
-        dk = jnp.stack(dk_parts, axis=1)
-        dv = jnp.stack(dv_parts, axis=1)
+
+        dq, dk, dv = tile_kernel(
+            got[:, :lq],
+            got[:, lq : 2 * lq],
+            jnp.concatenate([k_prior, k], axis=0).reshape(2 * tokens, lk),
+            jnp.concatenate([v_prior, v], axis=0).reshape(2 * tokens, lk),
+            norms,
+            delta,
+            local_start.reshape(1, tokens).astype(jnp.int32),
+        )
+        dq = dq.reshape(tokens, kvh, grp, HD)
+        dk = dk.reshape(2 * tokens, kvh, HD)
+        dv = dv.reshape(2 * tokens, kvh, HD)
 
         pkv = jnp.concatenate([prefix_keys, prefix_values], axis=1)
         nctx = math.prod(sizes)

time: 228 us -> 245 us (1.075)
  waiting for transfers between devices: 51.7 us -> 89.3 us
  matrix products: 49.9 us -> 18.2 us
  Pallas kernels: 0 us -> 19.7 us
  local copies, waits for them, and re-layouts: 67.1 us -> 61.4 us
  starting transfers between devices: 45.5 us -> 40.8 us
    dot_general x10 -> x0, matrix products: 35.6 us -> none  [the longest x2 10.5 us: shards(): dw = jnp.einsum('trd,sd->rts', dog, vg, preferred_element_type=f32)]
    ppermute x4, waiting for transfers between devices: 7.94 us -> 41.9 us  [shifted(): return lax.ppermute(array, axes, pairs)]
    pallas_call x0 -> x1, Pallas kernels: none -> 19.7 us  [tile_kernel(): pl.pallas_call(tile_body, grid=(kvh, tokens // rows), in_specs=[pl.BlockS...]
    another operation x2 -> x1, local copies, waits for them, and re-layouts: 3.49 us -> 0.11 us  [the longest x1 3.38 us: shards(): dq = jnp.stack(dq_parts, axis=1)]
    all_to_all x1 -> x0, local copies, waits for them, and re-layouts: 2.8 us -> none  [shards(): lax.all_to_all(packed, 'head', split_axis=1, concat_axis=0, tiled=True)]
    reshape x0 -> x4, local copies, waits for them, and re-layouts: none -> 2.73 us  [the longest x1 1.49 us: shards(): out_grad.reshape(rows, nh, qw // nh)]
    another operation x1, local copies, waits for them, and re-layouts: 1.48 us -> 4.08 us  [shards(): qb = q.reshape(nblk, BLK, kvh, grp, HD)]
    all_to_all x1, starting transfers between devices: 11 us -> 8.51 us  [shards(): lax.all_to_all(pgrad.reshape(nctx, -1, pgrad.shape[1]), names, split_axis...]
  transfers between devices with their start and end apart: 8 -> 8, of which waited for: 5 -> 7; matrix products, arithmetic and copies ran while one was open for 44% -> 20% of each run, Pallas kernels for 0% -> 8%
where the time goes in v3:
time: 245 us; the launch traced here: 243 us
  waiting for transfers between devices  89.3 us (36%)
  local copies, waits for them, and re-layouts  61.4 us (25%)
  starting transfers between devices  40.8 us (17%)
  Pallas kernels  19.7 us (8%)
  matrix products  18.2 us (7%)
  other arithmetic  12.3 us (5%)
    ppermute x4, waiting for transfers between devices, shifted(): return lax.ppermute(array, axes, pairs)  41.9 us
    all_to_all x1, waiting for transfers between devices, shards(): lax.all_to_all(jnp.broadcast_to(pkv[None], (nctx,) + pkv.shape), names, s...  24.4 us
    pallas_call x1, Pallas kernels, tile_kernel(): pl.pallas_call(tile_body, grid=(kvh, tokens // rows), in_specs=[pl.BlockS...  19.7 us
    all_to_all x1, waiting for transfers between devices, shards(): lax.all_to_all(packed, 'head', split_axis=1, concat_axis=0, tiled=True)  19.1 us
    all_to_all x1, starting transfers between devices, shards(): lax.all_to_all(jnp.broadcast_to(pkv[None], (nctx,) + pkv.shape), names, s...  14.4 us
    ppermute x4, starting transfers between devices, shifted(): return lax.ppermute(array, axes, pairs)  10.8 us
    all_to_all x1, starting transfers between devices, shards(): lax.all_to_all(pgrad.reshape(nctx, -1, pgrad.shape[1]), names, split_axis...  8.51 us
    unnamed x44, local copies, waits for them, and re-layouts  7.16 us
  transfers between devices with their start and end apart: 8, of which 7 were waited for; matrix products, arithmetic and copies ran while one was open for 20% of the time, Pallas kernels for 8%

profile of v3, /device:TPU:22, one launch (start us, length us, event | category | flops | bytes accessed | tf_op | source)
XLA Modules:
  0.0 242.7 jit_solution(1504786794081028889)
XLA Ops:
  0.6 1.7 copy.124
  2.6 0.8 fusion.7
  3.5 0.6 reshape.176
  4.1 3.3 %all-to-all-start.1 = ((f32[128,4,10]{0,2,1:T(8,128)}), f32[128,4,10]{0,2,1:T(8,128)S(1)}, u32[]{:S(2)}, u32[]{:S(2)}) async-start(f32[128,4,10]{0,2,1:T(8,128)} %reshape.176), calls=%async_computation.1 | async-start | bytes 65536 | tf_op jit(solution)/shard_map/all_to_all | solution.py:171
  7.5 3.9 %all-to-all-done.1 = f32[128,4,10]{0,2,1:T(8,128)S(1)} async-done(((f32[128,4,10]{0,2,1:T(8,128)}), f32[128,4,10]{0,2,1:T(8,128)S(1)}, u32[]{:S(2)}, u32[]{:S(2)}) %all-to-all-start.1) | async-done | bytes 20512 | tf_op jit(solution)/shard_map/all_to_all | solution.py:171
  11.3 1.1 broadcast_in_dim.60
  12.4 14.4 %all-to-all-start.2 = ((bf16[64,16,512]{2,1,0:T(8,128)(2,1)}), bf16[64,16,512]{2,1,0:T(8,128)(2,1)S(1)}, u32[]{:S(2)}, u32[]{:S(2)}) async-start(bf16[64,16,512]{2,1,0:T(8,128)(2,1)} %broadcast_in_dim.60), calls=%async_computation.2 | async-start | bytes 2097152 | tf_op jit(solution)/shard_map/all_to_all | solution.py:215
  26.9 1.5 copy_bitcast_fusion
  28.4 1.9 pad_maximum_fusion
  30.2 24.4 %all-to-all-done.2 = bf16[64,16,512]{2,1,0:T(8,128)(2,1)S(1)} async-done(((bf16[64,16,512]{2,1,0:T(8,128)(2,1)}), bf16[64,16,512]{2,1,0:T(8,128)(2,1)S(1)}, u32[]{:S(2)}, u32[]{:S(2)}) %all-to-all-start.2) | async-done | bytes 1048608 | tf_op jit(solution)/shard_map/all_to_all | solution.py:215
  54.7 1.0 copy-done.3
  55.6 3.9 %all-to-all-start = ((bf16[128,4,3072]{2,0,1:T(8,128)(2,1)}), bf16[128,4,3072]{2,0,1:T(8,128)(2,1)S(1)}, u32[]{:S(2)}, u32[]{:S(2)}) async-start(bf16[128,4,3072]{2,0,1:T(8,128)(2,1)} %pad_maximum_fusion), calls=%async_computation | async-start | bytes 6291456 | tf_op jit(solution)/shard_map/all_to_all | solution.py:170
  60.8 0.7 copy_bitcast_fusion.8
  61.5 2.3 fusion.38
  63.8 2.0 reshape.220
  65.8 1.9 copy.94
  67.7 2.0 reshape.219
  69.7 1.9 copy.90
  71.6 2.7 %gather_fusion.1 = bf16[16,128,2,128]{3,1,2,0:T(8,128)(2,1)} fusion(bf16[8,128,2,128]{3,1,2,0:T(8,128)(2,1)} %copy.94, s32[1024]{0:T(1024)S(1)} %pad_clamp_fusion), kind=kCustom, calls=%fused_computation.1.clone | custom fusion | bytes 2097216 | tf_op jit(solution)/shard_map/jit(_take)/gather | solution.py:226
  74.3 2.8 %gather_fusion = bf16[16,128,2,128]{3,1,2,0:T(8,128)(2,1)} fusion(bf16[8,128,2,128]{3,1,2,0:T(8,128)(2,1)} %copy.90, s32[1024]{0:T(1024)S(1)} %pad_clamp_fusion), kind=kCustom, calls=%fused_computation.clone | custom fusion | bytes 2097216 | tf_op jit(solution)/shard_map/jit(_take)/gather | solution.py:225
  77.1 19.1 %all-to-all-done = bf16[128,4,3072]{2,0,1:T(8,128)(2,1)S(1)} async-done(((bf16[128,4,3072]{2,0,1:T(8,128)(2,1)}), bf16[128,4,3072]{2,0,1:T(8,128)(2,1)S(1)}, u32[]{:S(2)}, u32[]{:S(2)}) %all-to-all-start) | async-done | bytes 3145760 | tf_op jit(solution)/shard_map/all_to_all | solution.py:170
  96.2 1.7 fusion.37
  97.9 4.1 %reshape_reshape.17 = bf16[16,32,2,5,128]{4,3,2,1,0:T(8,128)(2,1)} reshape(bf16[512,1280]{1,0:T(8,128)(2,1)} %get-tuple-element.16.do_ref) | data formatting | bytes 2621440 | tf_op jit(solution)/shard_map/reshape;reshape | solution.py:228
  102.0 4.1 %reshape_reshape.15 = bf16[16,32,2,5,128]{4,3,2,1,0:T(8,128)(2,1)} reshape(bf16[512,1280]{1,0:T(8,128)(2,1)} %get-tuple-element.17.q_ref) | data formatting | bytes 2621440 | tf_op jit(solution)/shard_map/reshape;reshape | solution.py:227
  106.1 3.0 %fusion.15 = f32[16,2,128,32,5]{2,3,4,1,0:T(8,128)S(1)} fusion(bf16[16,32,2,5,128]{4,3,2,1,0:T(8,128)(2,1)} %reshape_reshape.15, bf16[16,128,2,128]{3,1,2,0:T(8,128)(2,1)} %gather_fusion, pred[16]{0:T(512)(128)(4,1)S(1)} %compare_and_fusion), kind=kOutput, calls=%fused_computation.24 | convolution fusion | flops 168296448 | bytes 4980752 | tf_op jit(solution)/shard_map/bigrd,bjgd->bgrij/dot_general | solution.py:231
  109.1 2.8 %fusion.9 = f32[16,2,128,128,1]{3,2,4,1,0:T(8,128)} fusion(f32[16,2,128,32,5]{2,3,4,1,0:T(8,128)S(1)} %fusion.15, f32[16,2,5,32]{3,2,1,0:T(8,128)S(1)} %copy-done.13, bf16[16,32,2,5,128]{4,3,2,1,0:T(8,128)(2,1)S(1)} %copy-done.6), kind=kOutput, calls=%fused_computation.17 | convolution fusion | flops 169738240 | bytes 6049792 | tf_op jit(solution)/shard_map/bgrij,bigrd->bjgd/dot_general | solution.py:234
  111.9 3.1 %copy.101 = f32[16,128,256]{2,0,1:T(8,128)} copy(f32[16,128,256]{1,2,0:T(8,128)} %bitcast.114) | data formatting | bytes 4194304 | tf_op jit(solution)/shard_map/reshape | solution.py:244
  114.9 4.2 %fusion.5 = bf16[16,2,5,32,128]{4,3,2,1,0:T(8,128)(2,1)S(1)} fusion(f32[16,2,128,32,5]{2,3,4,1,0:T(8,128)} %copy-done.4, f32[16,2,5,32]{3,2,1,0:T(8,128)S(1)} %get-tuple-element.26, f32[16,2,5,32]{3,2,1,0:T(8,128)S(1)} %copy-done.13, bf16[16,128,2,128]{3,1,2,0:T(8,128)(2,1)} %gather_fusion.1, pred[16]{0:T(512)(128)(4,1)S(1)} %compare_and_fusion, ...), kind=kOutput, calls=%fused_computation.9 | convolution fusion | flops 171573248 | bytes 6332432 | tf_op jit(solution)/shard_map/bigrd,bjgd->bgrij/dot_general | solution.py:235
  119.2 2.1 fusion.21
  121.3 3.1 %copy.100 = f32[16,128,256]{2,0,1:T(8,128)} copy(f32[16,128,256]{1,2,0:T(8,128)} %bitcast.108) | data formatting | bytes 4194304 | tf_op jit(solution)/shard_map/reshape | solution.py:244
  124.4 3.8 %fusion = f32[8,128,512]{2,0,1:T(8,128)S(1)} fusion(f32[16,128,256]{2,0,1:T(8,128)} %copy.101, f32[16,128,256]{2,0,1:T(8,128)} %copy.100, s32[16]{0:T(128)S(1)} %select_reduce_fusion.1), kind=kOutput, calls=%fused_computation.2 | convolution fusion | flops 101712000 | bytes 6291520 | tf_op jit(solution)/shard_map/bp,bjx->pjx/dot_general | solution.py:240
  128.3 2.6 %copy.102 = f32[8,128,512]{2,1,0:T(8,128)} copy(f32[8,128,512]{2,0,1:T(8,128)S(1)} %fusion) | data formatting | bytes 4194304 | tf_op jit(solution)/shard_map/bp,bjx->pjx/dot_general | solution.py:240
  130.9 8.5 %all-to-all-start.3 = ((f32[64,16,512]{2,1,0:T(8,128)}), f32[64,16,512]{2,1,0:T(8,128)}, u32[]{:S(2)}, u32[]{:S(2)}) async-start(f32[64,16,512]{2,1,0:T(8,128)} %bitcast.107), calls=%async_computation.3 | async-start | bytes 4194304 | tf_op jit(solution)/shard_map/all_to_all | solution.py:249
  139.4 0.6 reshape.173.n_ref
  140.0 0.7 sub.48.ls_ref
  140.7 0.6 reshape.178.d_ref
  141.3 0.7 fusion.36
  142.0 0.8 reshape.172
  142.8 1.7 reshape.171
  144.5 3.4 %collective-permute-start = (bf16[512,2,128]{2,1,0:T(2,128)(2,1)}, bf16[512,2,128]{2,1,0:T(2,128)(2,1)S(1)}, u32[]{:S(2)}, u32[]{:S(2)}) collective-permute-start(bf16[512,2,128]{2,1,0:T(2,128)(2,1)} %reshape.171), channel_id=1, source_target_pairs={{0,4},{4,8},{8,12},{12,16},{16,20},{20,24},{24,28},{28,32},{32,36}... | collective-permute-start | bytes 786440 | tf_op jit(solution)/shard_map/ppermute | solution.py:29
  147.9 3.6 %collective-permute-start.1 = (bf16[512,2,128]{2,1,0:T(2,128)(2,1)}, bf16[512,2,128]{2,1,0:T(2,128)(2,1)}, u32[]{:S(2)}, u32[]{:S(2)}) collective-permute-start(bf16[512,2,128]{2,1,0:T(2,128)(2,1)} %reshape.172), channel_id=1, source_target_pairs={{0,4},{4,8},{8,12},{12,16},{16,20},{20,24},{24,28},{28,32},{32,36}... | collective-permute-start | bytes 786440 | tf_op jit(solution)/shard_map/ppermute | solution.py:29
  151.5 2.2 convolution_bitcast_fusion
  153.7 3.7 %copy.97 = f32[16,32,2,5,128]{4,3,2,1,0:T(8,128)} copy(f32[16,32,2,5,128]{4,1,3,2,0:T(8,128)S(1)} %convolution_bitcast_fusion) | data formatting | bytes 5242880 | tf_op jit(solution)/shard_map/bgrij,bjgd->bigrd/transpose | solution.py:237
  157.4 3.3 %reshape.184 = f32[512,1280]{1,0:T(8,128)S(1)} reshape(f32[16,32,2,5,128]{4,3,2,1,0:T(8,128)} %copy.97) | data formatting | bytes 5242880 | tf_op jit(solution)/shard_map/reshape | solution.py:257
  160.7 30.0 %collective-permute-done = bf16[512,2,128]{2,1,0:T(2,128)(2,1)S(1)} collective-permute-done((bf16[512,2,128]{2,1,0:T(2,128)(2,1)}, bf16[512,2,128]{2,1,0:T(2,128)(2,1)S(1)}, u32[]{:S(2)}, u32[]{:S(2)}) %collective-permute-start) | collective-permute-done | bytes 262176 | tf_op jit(solution)/shard_map/ppermute | solution.py:29
  190.8 0.7 copy-done.9
  191.5 1.0 copy.150
  192.5 2.2 collective-permute-done.1
  194.7 1.0 copy.149
  195.7 0.8 pad_maximum_fusion.1.k_ref
  196.5 0.8 pad_maximum_fusion.2.v_ref
  197.3 19.7 %shard_map.137 = (f32[512,1280]{1,0:T(8,128)}, f32[1024,256]{1,0:T(8,128)}, f32[1024,256]{1,0:T(8,128)}) custom-call(bf16[512,1280]{1,0:T(8,128)(2,1)} %get-tuple-element.17.q_ref, bf16[512,1280]{1,0:T(8,128)(2,1)} %get-tuple-element.16.do_ref, bf16[1024,256]{1,0:T(8,128)(2,1)} %pad_maximum_fusion.1.k_ref, bf16[1024,256]{1,0:T(8,128)(2,1)} %pad_maximum_fusion.2.v_ref, ...), custom_call_target="tpu_custom_call" | custom-call | flops 6710886400 | bytes 7864320 | tf_op jit(solution)/shard_map/pallas_call | solution.py:99
  217.0 1.1 slice.84
  218.1 1.1 slice.83
  219.3 1.9 collective-permute-start.3
  221.2 1.9 collective-permute-start.2
  223.2 3.3 %multiply_convert_fusion = bf16[512,1280]{1,0:T(8,128)(2,1)} fusion(f32[512,1280]{1,0:T(8,128)} %get-tuple-element.9, f32[512,1280]{1,0:T(8,128)S(1)} %reshape.184), kind=kLoop, calls=%fused_computation.14 | loop fusion | flops 1966080 | bytes 6553600 | tf_op jit(solution)/shard_map/convert_element_type | solution.py:264
  227.1 8.3 %collective-permute-done.3 = bf16[512,2,128]{2,1,0:T(2,128)(2,1)} collective-permute-done((bf16[512,2,128]{2,1,0:T(2,128)(2,1)S(1)}, bf16[512,2,128]{2,1,0:T(2,128)(2,1)}, u32[]{:S(2)}, u32[]{:S(2)}) %collective-permute-start.3) | collective-permute-done | bytes 262176 | tf_op jit(solution)/shard_map/ppermute | solution.py:29
  235.4 1.2 add_convert_fusion
  236.7 0.7 copy.147
  237.4 1.3 collective-permute-done.2
  239.0 0.7 copy.148
  239.8 1.7 reduce_sum.39
  241.5 0.6 slice.85
  (67 shorter events, 3.4 us)
Async XLA Ops:
  0.6 1.7 copy-start.2
  2.6 4.8 %copy-start.14 = (bf16[16,256]{1,0:T(8,128)(2,1)S(1)}, bf16[16,256]{1,0:T(8,128)(2,1)}, u32[]{:S(2)}) copy-start(bf16[16,256]{1,0:T(8,128)(2,1)} %param.19) | copy-start | bytes 24580
  2.6 4.8 %copy-start.15 = (bf16[16,256]{1,0:T(8,128)(2,1)S(1)}, bf16[16,256]{1,0:T(8,128)(2,1)}, u32[]{:S(2)}) copy-start(bf16[16,256]{1,0:T(8,128)(2,1)} %param.18) | copy-start | bytes 24580
  3.4 23.4 %copy-start.10 = (bf16[128,1024]{1,0:T(8,128)(2,1)S(1)}, bf16[128,1024]{1,0:T(8,128)(2,1)}, u32[]{:S(2)}) copy-start(bf16[128,1024]{1,0:T(8,128)(2,1)} %param.14) | copy-start | bytes 786436
  3.4 23.4 %copy-start.11 = (bf16[128,1024]{1,0:T(8,128)(2,1)S(1)}, bf16[128,1024]{1,0:T(8,128)(2,1)}, u32[]{:S(2)}) copy-start(bf16[128,1024]{1,0:T(8,128)(2,1)} %param.13) | copy-start | bytes 786436
  4.1 7.2 %all-to-all-start.1 = ((f32[128,4,10]{0,2,1:T(8,128)}), f32[128,4,10]{0,2,1:T(8,128)S(1)}, u32[]{:S(2)}, u32[]{:S(2)}) async-start(f32[128,4,10]{0,2,1:T(8,128)} %reshape.176), calls=%async_computation.1 | async-start | bytes 65536 | tf_op jit(solution)/shard_map/all_to_all | solution.py:171
  12.4 42.2 %all-to-all-start.2 = ((bf16[64,16,512]{2,1,0:T(8,128)(2,1)}), bf16[64,16,512]{2,1,0:T(8,128)(2,1)S(1)}, u32[]{:S(2)}, u32[]{:S(2)}) async-start(bf16[64,16,512]{2,1,0:T(8,128)(2,1)} %broadcast_in_dim.60), calls=%async_computation.2 | async-start | bytes 2097152 | tf_op jit(solution)/shard_map/all_to_all | solution.py:215
  30.2 29.3 %copy-start.16 = (s32[8,16]{1,0:T(8,128)S(1)}, s32[8,16]{1,0:T(8,128)}, u32[]{:S(2)}) copy-start(s32[8,16]{1,0:T(8,128)} %param.21) | copy-start | bytes 1540
  30.2 29.4 %copy-start.17 = (s32[128]{0:T(128)S(1)}, s32[128]{0:T(128)}, u32[]{:S(2)}) copy-start(s32[128]{0:T(128)} %param.20) | copy-start | bytes 1540
  30.2 29.8 %copy-start.12 = (f32[10,512]{1,0:T(8,128)S(1)}, f32[10,512]{1,0:T(8,128)}, u32[]{:S(2)}) copy-start(f32[10,512]{1,0:T(8,128)} %param.17) | copy-start | bytes 61444
  54.7 1.0 copy-start.3
  55.6 40.6 %all-to-all-start = ((bf16[128,4,3072]{2,0,1:T(8,128)(2,1)}), bf16[128,4,3072]{2,0,1:T(8,128)(2,1)S(1)}, u32[]{:S(2)}, u32[]{:S(2)}) async-start(bf16[128,4,3072]{2,0,1:T(8,128)(2,1)} %pad_maximum_fusion), calls=%async_computation | async-start | bytes 6291456 | tf_op jit(solution)/shard_map/all_to_all | solution.py:170
  106.1 3.0 %copy-start.6 = (bf16[16,32,2,5,128]{4,3,2,1,0:T(8,128)(2,1)S(1)}, bf16[16,32,2,5,128]{4,3,2,1,0:T(8,128)(2,1)}, u32[]{:S(2)}) copy-start(bf16[16,32,2,5,128]{4,3,2,1,0:T(8,128)(2,1)} %reshape_reshape.17) | copy-start | bytes 3932164
  106.1 3.0 %copy-start.13 = (f32[16,2,5,32]{3,2,1,0:T(8,128)S(1)}, f32[16,2,5,32]{3,2,1,0:T(8,128)}, u32[]{:S(2)}) copy-start(f32[16,2,5,32]{3,2,1,0:T(8,128)} %get-tuple-element.27) | copy-start | bytes 61444
  109.0 2.8 %copy-start.4 = (f32[16,2,128,32,5]{2,3,4,1,0:T(8,128)}, f32[16,2,128,32,5]{2,3,4,1,0:T(8,128)S(1)}, u32[]{:S(2)}) copy-start(f32[16,2,128,32,5]{2,3,4,1,0:T(8,128)S(1)} %fusion.15) | copy-start | bytes 7864324
  114.9 4.2 %copy-start = (bf16[16,32,2,5,128]{4,3,2,1,0:T(8,128)(2,1)S(1)}, bf16[16,32,2,5,128]{4,3,2,1,0:T(8,128)(2,1)}, u32[]{:S(2)}) copy-start(bf16[16,32,2,5,128]{4,3,2,1,0:T(8,128)(2,1)} %reshape_reshape.15) | copy-start | bytes 3932164
  119.2 2.2 copy-start.1
  130.9 108.9 %all-to-all-start.3 = ((f32[64,16,512]{2,1,0:T(8,128)}), f32[64,16,512]{2,1,0:T(8,128)}, u32[]{:S(2)}, u32[]{:S(2)}) async-start(f32[64,16,512]{2,1,0:T(8,128)} %bitcast.107), calls=%async_computation.3 | async-start | bytes 4194304 | tf_op jit(solution)/shard_map/all_to_all | solution.py:249
  144.5 46.2 %collective-permute-start = (bf16[512,2,128]{2,1,0:T(2,128)(2,1)}, bf16[512,2,128]{2,1,0:T(2,128)(2,1)S(1)}, u32[]{:S(2)}, u32[]{:S(2)}) collective-permute-start(bf16[512,2,128]{2,1,0:T(2,128)(2,1)} %reshape.171), channel_id=1, source_target_pairs={{0,4},{4,8},{8,12},{12,16},{16,20},{20,24},{24,28},{28,32},{32,36}... | collective-permute-start | bytes 786440 | tf_op jit(solution)/shard_map/ppermute | solution.py:29
  147.9 46.8 %collective-permute-start.1 = (bf16[512,2,128]{2,1,0:T(2,128)(2,1)}, bf16[512,2,128]{2,1,0:T(2,128)(2,1)}, u32[]{:S(2)}, u32[]{:S(2)}) collective-permute-start(bf16[512,2,128]{2,1,0:T(2,128)(2,1)} %reshape.172), channel_id=1, source_target_pairs={{0,4},{4,8},{8,12},{12,16},{16,20},{20,24},{24,28},{28,32},{32,36}... | collective-permute-start | bytes 786440 | tf_op jit(solution)/shard_map/ppermute | solution.py:29
  157.4 38.2 %copy-start.5 = (bf16[512,256]{1,0:T(8,128)(2,1)S(1)}, bf16[512,256]{1,0:T(8,128)(2,1)}, u32[]{:S(2)}) copy-start(bf16[512,256]{1,0:T(8,128)(2,1)} %get-tuple-element.15) | copy-start | bytes 786436
  190.8 0.7 copy-start.9
  219.3 16.2 %collective-permute-start.3 = (bf16[512,2,128]{2,1,0:T(2,128)(2,1)S(1)}, bf16[512,2,128]{2,1,0:T(2,128)(2,1)}, u32[]{:S(2)}, u32[]{:S(2)}) collective-permute-start(bf16[512,2,128]{2,1,0:T(2,128)(2,1)S(1)} %convert_element_type.44), channel_id=1, source_target_pairs={{4,0},{8,4},{12,8},{16,12},{20,16},{24,20},{28,24},{32,28},{36,32}... | collective-permute-start | bytes 786440 | tf_op jit(solution)/shard_map/ppermute | solution.py:29
  221.2 17.5 %collective-permute-start.2 = (bf16[512,2,128]{2,1,0:T(2,128)(2,1)S(1)}, bf16[512,2,128]{2,1,0:T(2,128)(2,1)S(1)}, u32[]{:S(2)}, u32[]{:S(2)}) collective-permute-start(bf16[512,2,128]{2,1,0:T(2,128)(2,1)S(1)} %convert_element_type.41), channel_id=1, source_target_pairs={{4,0},{8,4},{12,8},{16,12},{20,16},{24,20},{28,24},{32,28},{36,32}... | collective-permute-start | bytes 786440 | tf_op jit(solution)/shard_map/ppermute | solution.py:29
  223.1 3.3 %copy-start.8 = (f32[1024,256]{1,0:T(8,128)S(1)}, f32[1024,256]{1,0:T(8,128)}, u32[]{:S(2)}) copy-start(f32[1024,256]{1,0:T(8,128)} %get-tuple-element.10) | copy-start | bytes 3145732
  223.2 3.3 %copy-start.7 = (f32[1024,256]{1,0:T(8,128)S(1)}, f32[1024,256]{1,0:T(8,128)}, u32[]{:S(2)}) copy-start(f32[1024,256]{1,0:T(8,128)} %get-tuple-element.11) | copy-start | bytes 3145732

commit v4 on v3

--- a/solution.py
+++ b/solution.py
@@ -129,6 +129,78 @@
     )(q, do, keys, values, norms, delta, local_start)
 
 
+def prompt_body(pb_ref, q_ref, do_ref, k_ref, v_ref, n_ref, d_ref, dk_ref, dv_ref, dq_ref):
+    f32, bf16 = jnp.float32, jnp.bfloat16
+    scale = 1.0 / math.sqrt(HD)
+    nt = (((1,), (1,)), ((), ()))
+    grp = n_ref.shape[2]
+    dk_ref[...] = jnp.zeros_like(dk_ref)
+    dv_ref[...] = jnp.zeros_like(dv_ref)
+
+    def step(b, carry):
+        rows = pl.ds(pl.multiple_of(b * BLK, BLK), BLK)
+        keys_at = pl.ds(pl.multiple_of(pb_ref[b] * PL, PL), PL)
+        kb, vb = k_ref[keys_at, :], v_ref[keys_at, :]
+        nrm, dlt = n_ref[0, rows, :], d_ref[0, rows, :]
+        dk_b = jnp.zeros((PL, HD), f32)
+        dv_b = jnp.zeros((PL, HD), f32)
+        for r in range(grp):
+            cols = slice(r * HD, (r + 1) * HD)
+            qr, dor = q_ref[rows, cols], do_ref[rows, cols]
+            s = lax.dot_general(qr, kb, nt, preferred_element_type=f32)
+            w = jnp.exp(s * scale - nrm[:, r : r + 1])
+            dv_b = dv_b + jnp.dot(w.T.astype(bf16), dor, preferred_element_type=f32)
+            dw = lax.dot_general(dor, vb, nt, preferred_element_type=f32)
+            dl = w * (dw - dlt[:, r : r + 1])
+            dq_ref[rows, cols] = jnp.dot(dl.astype(bf16), kb, preferred_element_type=f32)
+            dk_b = dk_b + jnp.dot(dl.T.astype(bf16), qr, preferred_element_type=f32)
+        dk_ref[keys_at, :] += dk_b
+        dv_ref[keys_at, :] += dv_b
+        return carry
+
+    lax.fori_loop(0, pb_ref.shape[0], step, 0)
+
+
+def prompt_kernel(q, do, pk, pv, norms, delta, prompt_block):
+    tokens, lq = q.shape
+    span, lk = pk.shape
+    kvh, grp = norms.shape[0], norms.shape[2]
+    width = grp * HD
+    flops = 10 * tokens * PL * HD * kvh * grp
+    grid_spec = pltpu.PrefetchScalarGridSpec(
+        num_scalar_prefetch=1,
+        grid=(kvh,),
+        in_specs=[
+            pl.BlockSpec((tokens, width), lambda g, pb: (0, g)),
+            pl.BlockSpec((tokens, width), lambda g, pb: (0, g)),
+            pl.BlockSpec((span, HD), lambda g, pb: (0, g)),
+            pl.BlockSpec((span, HD), lambda g, pb: (0, g)),
+            pl.BlockSpec((1, tokens, grp), lambda g, pb: (g, 0, 0)),
+            pl.BlockSpec((1, tokens, grp), lambda g, pb: (g, 0, 0)),
+        ],
+        out_specs=[
+            pl.BlockSpec((span, HD), lambda g, pb: (0, g)),
+            pl.BlockSpec((span, HD), lambda g, pb: (0, g)),
+            pl.BlockSpec((tokens, width), lambda g, pb: (0, g)),
+        ],
+    )
+    return pl.pallas_call(
+        prompt_body,
+        grid_spec=grid_spec,
+        out_shape=[
+            jax.ShapeDtypeStruct((span, lk), jnp.float32),
+            jax.ShapeDtypeStruct((span, lk), jnp.float32),
+            jax.ShapeDtypeStruct((tokens, lq), jnp.float32),
+        ],
+        compiler_params=pltpu.CompilerParams(dimension_semantics=("arbitrary",)),
+        cost_estimate=pl.CostEstimate(
+            flops=flops,
+            transcendentals=tokens * PL * kvh * grp,
+            bytes_accessed=4 * tokens * lq * 2 + 4 * span * lk * 3,
+        ),
+    )(prompt_block, q, do, pk, pv, norms, delta)
+
+
 def make_shards(parts):
     names = tuple(n for n, _ in parts)
     sizes = tuple(s for _, s in parts)
@@ -210,7 +282,9 @@
         dk = dk.reshape(2 * tokens, kvh, HD)
         dv = dv.reshape(2 * tokens, kvh, HD)
 
-        pkv = jnp.concatenate([prefix_keys, prefix_values], axis=1)
+        pkv, _ = lax.optimization_barrier(
+            (jnp.concatenate([prefix_keys, prefix_values], axis=1), got)
+        )
         nctx = math.prod(sizes)
         pkv = lax.all_to_all(
             jnp.broadcast_to(pkv[None], (nctx,) + pkv.shape),
@@ -219,33 +293,16 @@
             concat_axis=0,
             tiled=True,
         ).reshape(nctx * pkv.shape[0], pkv.shape[1])
-        nprompt = pkv.shape[0] // PL
-        pk_all = pkv[:, :lk].reshape(nprompt, PL, kvh, HD)
-        pv_all = pkv[:, lk:].reshape(nprompt, PL, kvh, HD)
-        pkb = jnp.take(pk_all, prompt_block, axis=0)
-        pvb = jnp.take(pv_all, prompt_block, axis=0)
-        qb = q.reshape(nblk, BLK, kvh, grp, HD)
-        dob = do.reshape(nblk, BLK, kvh, grp, HD)
-        normb = norms.reshape(kvh, grp, nblk, BLK).transpose(2, 0, 1, 3)
-        deltab = delta.reshape(kvh, grp, nblk, BLK).transpose(2, 0, 1, 3)
-        lp = jnp.einsum("bigrd,bjgd->bgrij", qb, pkb, preferred_element_type=f32)
-        wp = jnp.exp(lp * scale - normb[..., None])
-        wpb = wp.astype(bf16)
-        dv_pb = jnp.einsum("bgrij,bigrd->bjgd", wpb, dob, preferred_element_type=f32)
-        dwp = jnp.einsum("bigrd,bjgd->bgrij", dob, pvb, preferred_element_type=f32)
-        dlp = (wp * (dwp - deltab[..., None])).astype(bf16)
-        dq_p = jnp.einsum("bgrij,bjgd->bigrd", dlp, pkb, preferred_element_type=f32)
-        dk_pb = jnp.einsum("bgrij,bigrd->bjgd", dlp, qb, preferred_element_type=f32)
-        onehot = (prompt_block[:, None] == jnp.arange(nprompt)[None, :]).astype(f32)
-        pgrad = jnp.einsum(
-            "bp,bjx->pjx",
-            onehot,
-            jnp.concatenate(
-                [dk_pb.reshape(nblk, PL, lk), dv_pb.reshape(nblk, PL, lk)], axis=2
-            ),
-            precision=lax.Precision.HIGHEST,
-            preferred_element_type=f32,
-        ).reshape(nprompt * PL, 2 * lk)
+        pgrad_k, pgrad_v, dq_p = prompt_kernel(
+            got[:, :lq],
+            got[:, lq : 2 * lq],
+            pkv[:, :lk],
+            pkv[:, lk:],
+            norms.transpose(0, 2, 1),
+            delta.transpose(0, 2, 1),
+            prompt_block.astype(jnp.int32),
+        )
+        pgrad = jnp.concatenate([pgrad_k, pgrad_v], axis=1)
         pgrad = lax.all_to_all(
             pgrad.reshape(nctx, -1, pgrad.shape[1]),
             names,

time: 245 us -> 273 us (1.11)
  Pallas kernels: 19.7 us -> 76.1 us
  local copies, waits for them, and re-layouts: 61.4 us -> 24.1 us
  waiting for transfers between devices: 89.3 us -> 112 us
  matrix products: 18.2 us -> 0 us
  other arithmetic: 12.3 us -> 16.2 us
    pallas_call x0 -> x1, Pallas kernels: none -> 56.4 us  [prompt_kernel(): pl.pallas_call(prompt_body, grid_spec=grid_spec, out_shape=[jax.ShapeDtyp...]
    dot_general x6 -> x0, matrix products: 18.2 us -> none  [the longest x1 4.22 us: shards(): dwp = jnp.einsum('bigrd,bjgd->bgrij', dob, pvb, preferred_element_type=f32)]
    reshape x7 -> x0, local copies, waits for them, and re-layouts: 17.3 us -> none  [the longest x2 3.9 us: shards(): pk_all = pkv[:, :lk].reshape(nprompt, PL, kvh, HD)]
    all_to_all x1, waiting for transfers between devices: 19.1 us -> 33.3 us  [shards(): lax.all_to_all(packed, 'head', split_axis=1, concat_axis=0, tiled=True)]
    ppermute x4, waiting for transfers between devices: 41.9 us -> 52.8 us  [shifted(): return lax.ppermute(array, axes, pairs)]
    another operation x5 -> x1, local copies, waits for them, and re-layouts: 8.49 us -> 0.11 us  [the longest x1 4.13 us: shards(): dob = do.reshape(nblk, BLK, kvh, grp, HD)]
    gather x2 -> x0, local copies, waits for them, and re-layouts: 5.46 us -> none  [the longest x1 2.77 us: shards(): pkb = jnp.take(pk_all, prompt_block, axis=0)]
    transpose x2 -> x0, local copies, waits for them, and re-layouts: 4.44 us -> none  [the longest x1 3.72 us: shards(): dq_p = jnp.einsum('bgrij,bjgd->bigrd', dlp, pkb, preferred_element_type=f32)]
  transfers between devices with their start and end apart: 8 -> 8, of which waited for: 7 -> 7; matrix products, arithmetic and copies ran while one was open for 20% -> 10% of each run, Pallas kernels for 8% -> 7%
where the time goes in v4:
time: 273 us; the launch traced here: 270 us
  waiting for transfers between devices  112 us (41%)
  Pallas kernels  76.1 us (28%)
  starting transfers between devices  40.6 us (15%)
  local copies, waits for them, and re-layouts  24.1 us (9%)
  other arithmetic  16.2 us (6%)
    pallas_call x1, Pallas kernels, prompt_kernel(): pl.pallas_call(prompt_body, grid_spec=grid_spec, out_shape=[jax.ShapeDtyp...  56.4 us
    ppermute x4, waiting for transfers between devices, shifted(): return lax.ppermute(array, axes, pairs)  52.8 us
    all_to_all x1, waiting for transfers between devices, shards(): lax.all_to_all(packed, 'head', split_axis=1, concat_axis=0, tiled=True)  33.3 us
    all_to_all x1, waiting for transfers between devices, shards(): lax.all_to_all(jnp.broadcast_to(pkv[None], (nctx,) + pkv.shape), names, s...  22.4 us
    pallas_call x1, Pallas kernels, tile_kernel(): pl.pallas_call(tile_body, grid=(kvh, tokens // rows), in_specs=[pl.BlockS...  19.6 us
    all_to_all x1, starting transfers between devices, shards(): lax.all_to_all(jnp.broadcast_to(pkv[None], (nctx,) + pkv.shape), names, s...  14.6 us
    ppermute x4, starting transfers between devices, shifted(): return lax.ppermute(array, axes, pairs)  10.6 us
    all_to_all x1, starting transfers between devices, shards(): lax.all_to_all(pgrad.reshape(nctx, -1, pgrad.shape[1]), names, split_axis...  8.51 us
  transfers between devices with their start and end apart: 8, of which 7 were waited for; matrix products, arithmetic and copies ran while one was open for 10% of the time, Pallas kernels for 7%

profile of v4, /device:TPU:22, one launch (start us, length us, event | category | flops | bytes accessed | tf_op | source)
XLA Modules:
  0.0 270.4 jit_solution(6852228673717466037)
XLA Ops:
  0.7 1.9 copy_bitcast_fusion
  2.7 1.9 pad_maximum_fusion
  4.5 3.7 %all-to-all-start = ((bf16[128,4,3072]{2,0,1:T(8,128)(2,1)}), bf16[128,4,3072]{2,0,1:T(8,128)(2,1)S(1)}, u32[]{:S(2)}, u32[]{:S(2)}) async-start(bf16[128,4,3072]{2,0,1:T(8,128)(2,1)} %pad_maximum_fusion), calls=%async_computation | async-start | bytes 6291456 | tf_op jit(solution)/shard_map/all_to_all | solution.py:242
  8.2 0.0 copy-start.2
  8.2 1.7 copy.50
  9.9 0.0 copy-done.2
  10.0 0.3 copy.51
  10.2 0.0 copy-start.12
  10.3 0.0 copy-start.11
  10.3 0.8 fusion
  11.0 0.1 copy.42
  11.1 0.6 reshape.156
  11.7 33.3 %all-to-all-done = bf16[128,4,3072]{2,0,1:T(8,128)(2,1)S(1)} async-done(((bf16[128,4,3072]{2,0,1:T(8,128)(2,1)}), bf16[128,4,3072]{2,0,1:T(8,128)(2,1)S(1)}, u32[]{:S(2)}, u32[]{:S(2)}) %all-to-all-start) | async-done | bytes 3145760 | tf_op jit(solution)/shard_map/all_to_all | solution.py:242
  45.1 3.3 %all-to-all-start.1 = ((f32[128,4,10]{0,2,1:T(8,128)}), f32[128,4,10]{0,2,1:T(8,128)S(1)}, u32[]{:S(2)}, u32[]{:S(2)}) async-start(f32[128,4,10]{0,2,1:T(8,128)} %reshape.156), calls=%async_computation.1 | async-start | bytes 65536 | tf_op jit(solution)/shard_map/all_to_all | solution.py:243
  48.4 3.9 %all-to-all-done.1 = f32[128,4,10]{0,2,1:T(8,128)S(1)} async-done(((f32[128,4,10]{0,2,1:T(8,128)}), f32[128,4,10]{0,2,1:T(8,128)S(1)}, u32[]{:S(2)}, u32[]{:S(2)}) %all-to-all-start.1) | async-done | bytes 20512 | tf_op jit(solution)/shard_map/all_to_all | solution.py:243
  52.3 1.1 broadcast_in_dim.50
  53.4 14.6 %all-to-all-start.2 = ((bf16[64,16,512]{2,1,0:T(8,128)(2,1)}), bf16[64,16,512]{2,1,0:T(8,128)(2,1)}, u32[]{:S(2)}, u32[]{:S(2)}) async-start(bf16[64,16,512]{2,1,0:T(8,128)(2,1)} %broadcast_in_dim.50), calls=%async_computation.2 | async-start | bytes 2097152 | tf_op jit(solution)/shard_map/all_to_all | solution.py:289
  68.0 0.1 copy.35
  68.1 0.2 reduce-window.9
  68.3 0.1 reduce.1
  68.5 0.1 eq.31
  68.5 1.0 copy.36
  69.6 0.2 fusion.3
  69.8 0.1 select_reduce_fusion
  69.9 0.7 select_reduce_fusion.1.pb_ref
  70.6 1.0 copy.37
  71.7 1.7 fusion.5
  73.3 22.4 %all-to-all-done.2 = bf16[64,16,512]{2,1,0:T(8,128)(2,1)} async-done(((bf16[64,16,512]{2,1,0:T(8,128)(2,1)}), bf16[64,16,512]{2,1,0:T(8,128)(2,1)}, u32[]{:S(2)}, u32[]{:S(2)}) %all-to-all-start.2) | async-done | bytes 1048608 | tf_op jit(solution)/shard_map/all_to_all | solution.py:289
  95.8 2.3 fusion.6
  98.0 56.4 %shard_map.138 = (f32[1024,256]{1,0:T(8,128)}, f32[1024,256]{1,0:T(8,128)}, f32[512,1280]{1,0:T(8,128)}) custom-call(s32[16]{0:T(128)} %select_reduce_fusion.1.pb_ref, bf16[512,1280]{1,0:T(8,128)(2,1)} %get-tuple-element.24.q_ref, bf16[512,1280]{1,0:T(8,128)(2,1)} %get-tuple-element.23.do_ref, bf16[1024,256]{1,0:T(8,128)(2,1)} %get-tuple-element.26.k_ref, ...), custom_call_target="tpu_custom_call" | custom-call | flops 838860800 | bytes 8388608 | tf_op jit(solution)/shard_map/pallas_call | solution.py:187
  154.5 3.1 %pad_maximum_fusion.1 = f32[1024,512]{1,0:T(8,128)} fusion(f32[1024,256]{1,0:T(8,128)} %get-tuple-element.18, f32[1024,256]{1,0:T(8,128)} %get-tuple-element.17), kind=kLoop, calls=%fused_computation.4 | loop fusion | flops 524288 | bytes 4194304 | tf_op jit(solution)/shard_map/concatenate | solution.py:305
  157.6 8.5 %all-to-all-start.3 = ((f32[64,16,512]{2,1,0:T(8,128)}), f32[64,16,512]{2,1,0:T(8,128)}, u32[]{:S(2)}, u32[]{:S(2)}) async-start(f32[64,16,512]{2,1,0:T(8,128)} %bitcast.59), calls=%async_computation.3 | async-start | bytes 4194304 | tf_op jit(solution)/shard_map/all_to_all | solution.py:306
  166.1 0.7 fusion.4
  166.9 1.0 reshape.152
  167.9 3.4 %collective-permute-start.1 = (bf16[512,2,128]{2,1,0:T(2,128)(2,1)S(1)}, bf16[512,2,128]{2,1,0:T(2,128)(2,1)S(1)}, u32[]{:S(2)}, u32[]{:S(2)}) collective-permute-start(bf16[512,2,128]{2,1,0:T(2,128)(2,1)S(1)} %reshape.152), channel_id=1, source_target_pairs={{0,4},{4,8},{8,12},{12,16},{16,20},{20,24},{24,28},{28,32},{32,36}... | collective-permute-start | bytes 786440 | tf_op jit(solution)/shard_map/ppermute | solution.py:29
  171.3 0.1 reshape.151
  171.3 3.4 %collective-permute-start = (bf16[512,2,128]{2,1,0:T(2,128)(2,1)S(1)}, bf16[512,2,128]{2,1,0:T(2,128)(2,1)S(1)}, u32[]{:S(2)}, u32[]{:S(2)}) collective-permute-start(bf16[512,2,128]{2,1,0:T(2,128)(2,1)S(1)} %reshape.151), channel_id=1, source_target_pairs={{0,4},{4,8},{8,12},{12,16},{16,20},{20,24},{24,28},{28,32},{32,36}... | collective-permute-start | bytes 786440 | tf_op jit(solution)/shard_map/ppermute | solution.py:29
  174.7 0.1 broadcast_in_dim.46
  174.8 0.7 sub.32.ls_ref
  175.5 42.0 %collective-permute-done.1 = bf16[512,2,128]{2,1,0:T(2,128)(2,1)S(1)} collective-permute-done((bf16[512,2,128]{2,1,0:T(2,128)(2,1)S(1)}, bf16[512,2,128]{2,1,0:T(2,128)(2,1)S(1)}, u32[]{:S(2)}, u32[]{:S(2)}) %collective-permute-start.1) | collective-permute-done | bytes 262176 | tf_op jit(solution)/shard_map/ppermute | solution.py:29
  217.5 3.2 %collective-permute-done = bf16[512,2,128]{2,1,0:T(2,128)(2,1)S(1)} collective-permute-done((bf16[512,2,128]{2,1,0:T(2,128)(2,1)S(1)}, bf16[512,2,128]{2,1,0:T(2,128)(2,1)S(1)}, u32[]{:S(2)}, u32[]{:S(2)}) %collective-permute-start) | collective-permute-done | bytes 262176 | tf_op jit(solution)/shard_map/ppermute | solution.py:29
  220.7 1.8 pad_maximum_fusion.3.v_ref
  222.5 0.9 pad_maximum_fusion.2.k_ref
  223.4 19.6 %shard_map.137 = (f32[512,1280]{1,0:T(8,128)}, f32[1024,256]{1,0:T(8,128)}, f32[1024,256]{1,0:T(8,128)}) custom-call(bf16[512,1280]{1,0:T(8,128)(2,1)} %get-tuple-element.24.q_ref, bf16[512,1280]{1,0:T(8,128)(2,1)} %get-tuple-element.23.do_ref, bf16[1024,256]{1,0:T(8,128)(2,1)} %pad_maximum_fusion.2.k_ref, bf16[1024,256]{1,0:T(8,128)(2,1)} %pad_maximum_fusion.3.v_ref, ...), custom_call_target="tpu_custom_call" | custom-call | flops 6710886400 | bytes 7864320 | tf_op jit(solution)/shard_map/pallas_call | solution.py:99
  243.0 1.2 slice.79
  244.2 0.8 convert_element_type.36
  245.0 1.9 collective-permute-start.3
  246.9 1.1 slice.80
  247.9 0.1 convert_element_type.33
  248.0 1.9 collective-permute-start.2
  249.9 1.1 slice.58
  251.0 0.8 slice.55
  251.9 1.1 slice.59
  252.9 1.3 slice.56
  254.2 7.0 %collective-permute-done.3 = bf16[512,2,128]{2,1,0:T(2,128)(2,1)} collective-permute-done((bf16[512,2,128]{2,1,0:T(2,128)(2,1)}, bf16[512,2,128]{2,1,0:T(2,128)(2,1)}, u32[]{:S(2)}, u32[]{:S(2)}) %collective-permute-start.3) | collective-permute-done | bytes 262176 | tf_op jit(solution)/shard_map/ppermute | solution.py:29
  261.2 1.4 add_convert_fusion
  262.6 0.7 copy.64
  263.3 0.7 collective-permute-done.2
  264.0 1.3 multiply_convert_fusion.1
  265.3 0.7 copy.65
  266.1 1.4 multiply_convert_fusion
  267.5 1.7 reduce_sum.39
  269.2 0.6 fusion.1
  269.8 0.6 slice.81
  (37 shorter events, 0.2 us)
Async XLA Ops:
  0.6 2.0 copy-start.4
  0.6 2.0 copy-start.5
  4.5 40.6 %all-to-all-start = ((bf16[128,4,3072]{2,0,1:T(8,128)(2,1)}), bf16[128,4,3072]{2,0,1:T(8,128)(2,1)S(1)}, u32[]{:S(2)}, u32[]{:S(2)}) async-start(bf16[128,4,3072]{2,0,1:T(8,128)(2,1)} %pad_maximum_fusion), calls=%async_computation | async-start | bytes 6291456 | tf_op jit(solution)/shard_map/all_to_all | solution.py:242
  8.2 1.7 copy-start.2
  9.9 38.4 %copy-start.9 = (bf16[16,256]{1,0:T(8,128)(2,1)S(1)}, bf16[16,256]{1,0:T(8,128)(2,1)}, u32[]{:S(2)}) copy-start(bf16[16,256]{1,0:T(8,128)(2,1)} %param.17) | copy-start | bytes 24580
  9.9 38.4 %copy-start.10 = (bf16[16,256]{1,0:T(8,128)(2,1)S(1)}, bf16[16,256]{1,0:T(8,128)(2,1)}, u32[]{:S(2)}) copy-start(bf16[16,256]{1,0:T(8,128)(2,1)} %param.16) | copy-start | bytes 24580
  10.2 57.8 %copy-start.12 = (s32[128]{0:T(128)S(1)}, s32[128]{0:T(128)}, u32[]{:S(2)}) copy-start(s32[128]{0:T(128)} %param.18) | copy-start | bytes 1540
  10.2 58.2 %copy-start.8 = (f32[10,512]{1,0:T(8,128)S(1)}, f32[10,512]{1,0:T(8,128)}, u32[]{:S(2)}) copy-start(f32[10,512]{1,0:T(8,128)} %param.15) | copy-start | bytes 61444
  10.3 58.2 %copy-start.11 = (s32[8,16]{1,0:T(8,128)S(1)}, s32[8,16]{1,0:T(8,128)}, u32[]{:S(2)}) copy-start(s32[8,16]{1,0:T(8,128)} %param.19) | copy-start | bytes 1540
  45.1 7.2 %all-to-all-start.1 = ((f32[128,4,10]{0,2,1:T(8,128)}), f32[128,4,10]{0,2,1:T(8,128)S(1)}, u32[]{:S(2)}, u32[]{:S(2)}) async-start(f32[128,4,10]{0,2,1:T(8,128)} %reshape.156), calls=%async_computation.1 | async-start | bytes 65536 | tf_op jit(solution)/shard_map/all_to_all | solution.py:243
  53.4 42.3 %all-to-all-start.2 = ((bf16[64,16,512]{2,1,0:T(8,128)(2,1)}), bf16[64,16,512]{2,1,0:T(8,128)(2,1)}, u32[]{:S(2)}, u32[]{:S(2)}) async-start(bf16[64,16,512]{2,1,0:T(8,128)(2,1)} %broadcast_in_dim.50), calls=%async_computation.2 | async-start | bytes 2097152 | tf_op jit(solution)/shard_map/all_to_all | solution.py:289
  68.4 4.9 %copy-start.6 = (f32[2,5,512]{2,1,0:T(8,128)}, f32[2,5,512]{2,1,0:T(8,128)S(1)}, u32[]{:S(2)}) copy-start(f32[2,5,512]{2,1,0:T(8,128)S(1)} %reshape.153.n_ref) | copy-start | bytes 61444
  70.6 2.7 %copy-start.7 = (f32[2,5,512]{2,1,0:T(8,128)}, f32[2,5,512]{2,1,0:T(8,128)S(1)}, u32[]{:S(2)}) copy-start(f32[2,5,512]{2,1,0:T(8,128)S(1)} %reshape.158.d_ref) | copy-start | bytes 61444
  157.6 109.9 %all-to-all-start.3 = ((f32[64,16,512]{2,1,0:T(8,128)}), f32[64,16,512]{2,1,0:T(8,128)}, u32[]{:S(2)}, u32[]{:S(2)}) async-start(f32[64,16,512]{2,1,0:T(8,128)} %bitcast.59), calls=%async_computation.3 | async-start | bytes 4194304 | tf_op jit(solution)/shard_map/all_to_all | solution.py:306
  167.9 49.5 %collective-permute-start.1 = (bf16[512,2,128]{2,1,0:T(2,128)(2,1)S(1)}, bf16[512,2,128]{2,1,0:T(2,128)(2,1)S(1)}, u32[]{:S(2)}, u32[]{:S(2)}) collective-permute-start(bf16[512,2,128]{2,1,0:T(2,128)(2,1)S(1)} %reshape.152), channel_id=1, source_target_pairs={{0,4},{4,8},{8,12},{12,16},{16,20},{20,24},{24,28},{28,32},{32,36}... | collective-permute-start | bytes 786440 | tf_op jit(solution)/shard_map/ppermute | solution.py:29
  171.3 49.3 %collective-permute-start = (bf16[512,2,128]{2,1,0:T(2,128)(2,1)S(1)}, bf16[512,2,128]{2,1,0:T(2,128)(2,1)S(1)}, u32[]{:S(2)}, u32[]{:S(2)}) collective-permute-start(bf16[512,2,128]{2,1,0:T(2,128)(2,1)S(1)} %reshape.151), channel_id=1, source_target_pairs={{0,4},{4,8},{8,12},{12,16},{16,20},{20,24},{24,28},{28,32},{32,36}... | collective-permute-start | bytes 786440 | tf_op jit(solution)/shard_map/ppermute | solution.py:29
  243.0 8.0 %copy-start.3 = (f32[1024,256]{1,0:T(8,128)S(1)}, f32[1024,256]{1,0:T(8,128)}, u32[]{:S(2)}) copy-start(f32[1024,256]{1,0:T(8,128)} %get-tuple-element.15) | copy-start | bytes 3145732
  245.0 16.3 %collective-permute-start.3 = (bf16[512,2,128]{2,1,0:T(2,128)(2,1)}, bf16[512,2,128]{2,1,0:T(2,128)(2,1)}, u32[]{:S(2)}, u32[]{:S(2)}) collective-permute-start(bf16[512,2,128]{2,1,0:T(2,128)(2,1)} %convert_element_type.36), channel_id=1, source_target_pairs={{4,0},{8,4},{12,8},{16,12},{20,16},{24,20},{28,24},{32,28},{36,32}... | collective-permute-start | bytes 786440 | tf_op jit(solution)/shard_map/ppermute | solution.py:29
  248.0 16.0 %collective-permute-start.2 = (bf16[512,2,128]{2,1,0:T(2,128)(2,1)S(1)}, bf16[512,2,128]{2,1,0:T(2,128)(2,1)}, u32[]{:S(2)}, u32[]{:S(2)}) collective-permute-start(bf16[512,2,128]{2,1,0:T(2,128)(2,1)S(1)} %convert_element_type.33), channel_id=1, source_target_pairs={{4,0},{8,4},{12,8},{16,12},{20,16},{24,20},{28,24},{32,28},{36,32}... | collective-permute-start | bytes 786440 | tf_op jit(solution)/shard_map/ppermute | solution.py:29
  251.9 14.2 %copy-start = (f32[512,1280]{1,0:T(8,128)S(1)}, f32[512,1280]{1,0:T(8,128)}, u32[]{:S(2)}) copy-start(f32[512,1280]{1,0:T(8,128)} %get-tuple-element.14) | copy-start | bytes 7864324
  254.2 11.9 %copy-start.1 = (f32[512,1280]{1,0:T(8,128)S(1)}, f32[512,1280]{1,0:T(8,128)}, u32[]{:S(2)}) copy-start(f32[512,1280]{1,0:T(8,128)} %get-tuple-element.12) | copy-start | bytes 7864324

commit v5 on v3

--- a/solution.py
+++ b/solution.py
@@ -50,16 +50,14 @@
 TT = 256
 
 
-def tile_body(q_ref, do_ref, k_ref, v_ref, n_ref, d_ref, ls_ref, dq_ref, dk_ref, dv_ref):
+def tile_body(q_ref, do_ref, k_ref, v_ref, n_ref, d_ref, lo_ref, hi_ref, dq_ref, dk_ref, dv_ref):
     i = pl.program_id(1)
     f32, bf16 = jnp.float32, jnp.bfloat16
     scale = 1.0 / math.sqrt(HD)
     keys, values = k_ref[...], v_ref[...]
     span, rows = keys.shape[0], q_ref.shape[0]
-    own = span // 2
-    tok = i * rows + lax.broadcasted_iota(jnp.int32, (span, rows), 1)
-    u = lax.broadcasted_iota(jnp.int32, (span, rows), 0) - own
-    allowed = (u >= ls_ref[...]) & (u <= tok)
+    u = lax.broadcasted_iota(jnp.int32, (span, rows), 0)
+    allowed = (u >= lo_ref[...]) & (u <= hi_ref[...])
     nrm, dlt = n_ref[0], d_ref[0]
     nt = (((1,), (1,)), ((), ()))
     dk_acc = jnp.zeros((span, HD), f32)
@@ -89,7 +87,7 @@
         dv_ref[...] += dv_acc
 
 
-def tile_kernel(q, do, keys, values, norms, delta, local_start):
+def tile_kernel(q, do, keys, values, norms, delta, lo, hi):
     tokens, lq = q.shape
     span, lk = keys.shape
     kvh, grp = norms.shape[0], norms.shape[1]
@@ -106,6 +104,7 @@
             pl.BlockSpec((span, HD), lambda g, i: (0, g)),
             pl.BlockSpec((1, grp, rows), lambda g, i: (g, 0, i)),
             pl.BlockSpec((1, grp, rows), lambda g, i: (g, 0, i)),
+            pl.BlockSpec((1, rows), lambda g, i: (0, i)),
             pl.BlockSpec((1, rows), lambda g, i: (0, i)),
         ],
         out_specs=[
@@ -126,7 +125,7 @@
             transcendentals=tokens * span * kvh * grp,
             bytes_accessed=4 * tokens * lq * 2 + 2 * span * lk * 5,
         ),
-    )(q, do, keys, values, norms, delta, local_start)
+    )(q, do, keys, values, norms, delta, lo, hi)
 
 
 def make_shards(parts):
@@ -204,13 +203,16 @@
             jnp.concatenate([v_prior, v], axis=0).reshape(2 * tokens, lk),
             norms,
             delta,
-            local_start.reshape(1, tokens).astype(jnp.int32),
+            (local_start + tokens).reshape(1, tokens).astype(jnp.int32),
+            (jnp.arange(tokens, dtype=jnp.int32) + tokens).reshape(1, tokens),
         )
         dq = dq.reshape(tokens, kvh, grp, HD)
         dk = dk.reshape(2 * tokens, kvh, HD)
         dv = dv.reshape(2 * tokens, kvh, HD)
 
-        pkv = jnp.concatenate([prefix_keys, prefix_values], axis=1)
+        pkv, _ = lax.optimization_barrier(
+            (jnp.concatenate([prefix_keys, prefix_values], axis=1), got)
+        )
         nctx = math.prod(sizes)
         pkv = lax.all_to_all(
             jnp.broadcast_to(pkv[None], (nctx,) + pkv.shape),
@@ -219,33 +221,19 @@
             concat_axis=0,
             tiled=True,
         ).reshape(nctx * pkv.shape[0], pkv.shape[1])
-        nprompt = pkv.shape[0] // PL
-        pk_all = pkv[:, :lk].reshape(nprompt, PL, kvh, HD)
-        pv_all = pkv[:, lk:].reshape(nprompt, PL, kvh, HD)
-        pkb = jnp.take(pk_all, prompt_block, axis=0)
-        pvb = jnp.take(pv_all, prompt_block, axis=0)
-        qb = q.reshape(nblk, BLK, kvh, grp, HD)
-        dob = do.reshape(nblk, BLK, kvh, grp, HD)
-        normb = norms.reshape(kvh, grp, nblk, BLK).transpose(2, 0, 1, 3)
-        deltab = delta.reshape(kvh, grp, nblk, BLK).transpose(2, 0, 1, 3)
-        lp = jnp.einsum("bigrd,bjgd->bgrij", qb, pkb, preferred_element_type=f32)
-        wp = jnp.exp(lp * scale - normb[..., None])
-        wpb = wp.astype(bf16)
-        dv_pb = jnp.einsum("bgrij,bigrd->bjgd", wpb, dob, preferred_element_type=f32)
-        dwp = jnp.einsum("bigrd,bjgd->bgrij", dob, pvb, preferred_element_type=f32)
-        dlp = (wp * (dwp - deltab[..., None])).astype(bf16)
-        dq_p = jnp.einsum("bgrij,bjgd->bigrd", dlp, pkb, preferred_element_type=f32)
-        dk_pb = jnp.einsum("bgrij,bigrd->bjgd", dlp, qb, preferred_element_type=f32)
-        onehot = (prompt_block[:, None] == jnp.arange(nprompt)[None, :]).astype(f32)
-        pgrad = jnp.einsum(
-            "bp,bjx->pjx",
-            onehot,
-            jnp.concatenate(
-                [dk_pb.reshape(nblk, PL, lk), dv_pb.reshape(nblk, PL, lk)], axis=2
-            ),
-            precision=lax.Precision.HIGHEST,
-            preferred_element_type=f32,
-        ).reshape(nprompt * PL, 2 * lk)
+        pkv, dq = lax.optimization_barrier((pkv, dq))
+        prompt_lo = (jnp.repeat(prompt_block, BLK) * PL).astype(jnp.int32)
+        dq_p, pgrad_k, pgrad_v = tile_kernel(
+            got[:, :lq],
+            got[:, lq : 2 * lq],
+            pkv[:, :lk],
+            pkv[:, lk:],
+            norms,
+            delta,
+            prompt_lo.reshape(1, tokens),
+            (prompt_lo + PL - 1).reshape(1, tokens),
+        )
+        pgrad = jnp.concatenate([pgrad_k, pgrad_v], axis=1)
         pgrad = lax.all_to_all(
             pgrad.reshape(nctx, -1, pgrad.shape[1]),
             names,

time: 245 us -> 237 us (0.967)
  local copies, waits for them, and re-layouts: 61.4 us -> 36.2 us
  Pallas kernels: 19.7 us -> 39.6 us
  matrix products: 18.2 us -> 0 us
  starting transfers between devices: 40.8 us -> 47.7 us
  other arithmetic: 12.3 us -> 17.9 us
  waiting for transfers between devices: 89.3 us -> 93.7 us
    all_to_all x1, waiting for transfers between devices: 24.4 us -> 0.01 us  [shards(): lax.all_to_all(jnp.broadcast_to(pkv[None], (nctx,) + pkv.shape), names, s...]
    pallas_call x1 -> x2, Pallas kernels: 19.7 us -> 39.6 us  [tile_kernel(): pl.pallas_call(tile_body, grid=(kvh, tokens // rows), in_specs=[pl.BlockS...]
    dot_general x6 -> x0, matrix products: 18.2 us -> none  [the longest x1 4.22 us: shards(): dwp = jnp.einsum('bigrd,bjgd->bgrij', dob, pvb, preferred_element_type=f32)]
    reshape x7 -> x0, local copies, waits for them, and re-layouts: 17.3 us -> none  [the longest x2 3.9 us: shards(): pk_all = pkv[:, :lk].reshape(nprompt, PL, kvh, HD)]
    ppermute x4, waiting for transfers between devices: 41.9 us -> 59 us  [shifted(): return lax.ppermute(array, axes, pairs)]
    all_to_all x1, waiting for transfers between devices: 19.1 us -> 32.4 us  [shards(): lax.all_to_all(packed, 'head', split_axis=1, concat_axis=0, tiled=True)]
    another operation x5 -> x1, local copies, waits for them, and re-layouts: 8.49 us -> 0.11 us  [the longest x1 4.13 us: shards(): dob = do.reshape(nblk, BLK, kvh, grp, HD)]
    gather x2 -> x0, local copies, waits for them, and re-layouts: 5.46 us -> none  [the longest x1 2.77 us: shards(): pkb = jnp.take(pk_all, prompt_block, axis=0)]
  transfers between devices with their start and end apart: 8 -> 8, of which waited for: 7 -> 6; matrix products, arithmetic and copies ran while one was open for 20% -> 17% of each run, Pallas kernels for 8% -> 8%
where the time goes in v5:
time: 237 us; the launch traced here: 236 us
  waiting for transfers between devices  93.7 us (40%)
  starting transfers between devices  47.7 us (20%)
  Pallas kernels  39.6 us (17%)
  local copies, waits for them, and re-layouts  36.2 us (15%)
  other arithmetic  17.9 us (8%)
    ppermute x4, waiting for transfers between devices, shifted(): return lax.ppermute(array, axes, pairs)  59 us
    pallas_call x2, Pallas kernels, tile_kernel(): pl.pallas_call(tile_body, grid=(kvh, tokens // rows), in_specs=[pl.BlockS...  39.6 us
    all_to_all x1, waiting for transfers between devices, shards(): lax.all_to_all(packed, 'head', split_axis=1, concat_axis=0, tiled=True)  32.4 us
    all_to_all x1, starting transfers between devices, shards(): lax.all_to_all(jnp.broadcast_to(pkv[None], (nctx,) + pkv.shape), names, s...  14.6 us
    all_to_all x1, starting transfers between devices, shards(): lax.all_to_all(pgrad.reshape(nctx, -1, pgrad.shape[1]), names, split_axis...  13.5 us
    ppermute x4, starting transfers between devices, shifted(): return lax.ppermute(array, axes, pairs)  12.5 us
    unnamed x25, local copies, waits for them, and re-layouts  5.97 us
    pallas_call x2, local copies, waits for them, and re-layouts, tile_kernel(): pl.pallas_call(tile_body, grid=(kvh, tokens // rows), in_specs=[pl.BlockS...  5.37 us
  transfers between devices with their start and end apart: 8, of which 6 were waited for; matrix products, arithmetic and copies ran while one was open for 17% of the time, Pallas kernels for 8%

profile of v5, /device:TPU:22, one launch (start us, length us, event | category | flops | bytes accessed | tf_op | source)
XLA Modules:
  0.0 236.1 jit_solution(10810454502111143589)
XLA Ops:
  0.6 1.1 copy_bitcast_fusion.6
  1.7 1.9 copy_bitcast_fusion
  3.6 1.9 pad_maximum_fusion
  5.5 3.8 %all-to-all-start = ((bf16[128,4,3072]{2,0,1:T(8,128)(2,1)}), bf16[128,4,3072]{2,0,1:T(8,128)(2,1)S(1)}, u32[]{:S(2)}, u32[]{:S(2)}) async-start(bf16[128,4,3072]{2,0,1:T(8,128)(2,1)} %pad_maximum_fusion), calls=%async_computation | async-start | bytes 6291456 | tf_op jit(solution)/shard_map/all_to_all | solution.py:169
  9.3 0.1 eq.31
  9.4 0.1 copy.42
  9.5 0.2 reduce-window.9
  9.7 0.1 reduce.1
  9.8 1.7 copy.59
  11.6 0.3 copy.58
  11.8 0.8 fusion
  12.7 0.6 reshape.198
  13.3 0.2 fusion.3
  13.5 0.1 select_reduce_fusion
  13.6 0.2 select_reduce_fusion.1
  13.8 32.4 %all-to-all-done = bf16[128,4,3072]{2,0,1:T(8,128)(2,1)S(1)} async-done(((bf16[128,4,3072]{2,0,1:T(8,128)(2,1)}), bf16[128,4,3072]{2,0,1:T(8,128)(2,1)S(1)}, u32[]{:S(2)}, u32[]{:S(2)}) %all-to-all-start) | async-done | bytes 3145760 | tf_op jit(solution)/shard_map/all_to_all | solution.py:169
  46.2 3.3 %all-to-all-start.2 = ((f32[128,4,10]{0,2,1:T(8,128)}), f32[128,4,10]{0,2,1:T(8,128)S(1)}, u32[]{:S(2)}, u32[]{:S(2)}) async-start(f32[128,4,10]{0,2,1:T(8,128)} %reshape.198), calls=%async_computation.2 | async-start | bytes 65536 | tf_op jit(solution)/shard_map/all_to_all | solution.py:170
  49.5 0.6 reshape.195.n_ref
  50.1 0.1 broadcast_in_dim.54
  50.2 0.1 mul.57.lo_ref
  50.3 0.7 add.76.lo_ref
  51.0 2.4 %all-to-all-done.2 = f32[128,4,10]{0,2,1:T(8,128)S(1)} async-done(((f32[128,4,10]{0,2,1:T(8,128)}), f32[128,4,10]{0,2,1:T(8,128)S(1)}, u32[]{:S(2)}, u32[]{:S(2)}) %all-to-all-start.2) | async-done | bytes 20512 | tf_op jit(solution)/shard_map/all_to_all | solution.py:170
  53.4 1.1 broadcast_in_dim.48
  54.5 14.6 %all-to-all-start.1 = ((bf16[64,16,512]{2,1,0:T(8,128)(2,1)}), bf16[64,16,512]{2,1,0:T(8,128)(2,1)}, u32[]{:S(2)}, u32[]{:S(2)}) async-start(bf16[64,16,512]{2,1,0:T(8,128)(2,1)} %broadcast_in_dim.48), calls=%async_computation.1 | async-start | bytes 2097152 | tf_op jit(solution)/shard_map/all_to_all | solution.py:217
  69.0 0.6 iota_add_fusion.hi_ref
  69.6 0.5 broadcast_add_fusion.hi_ref
  70.2 0.6 reshape.200.d_ref
  70.8 0.7 fusion.4
  71.5 0.8 reshape.194
  72.3 1.7 reshape.193
  74.0 3.5 %collective-permute-start = (bf16[512,2,128]{2,1,0:T(2,128)(2,1)}, bf16[512,2,128]{2,1,0:T(2,128)(2,1)S(1)}, u32[]{:S(2)}, u32[]{:S(2)}) collective-permute-start(bf16[512,2,128]{2,1,0:T(2,128)(2,1)} %reshape.193), channel_id=1, source_target_pairs={{0,4},{4,8},{8,12},{12,16},{16,20},{20,24},{24,28},{28,32},{32,36}... | collective-permute-start | bytes 786440 | tf_op jit(solution)/shard_map/ppermute | solution.py:29
  77.5 3.6 %collective-permute-start.1 = (bf16[512,2,128]{2,1,0:T(2,128)(2,1)}, bf16[512,2,128]{2,1,0:T(2,128)(2,1)S(1)}, u32[]{:S(2)}, u32[]{:S(2)}) collective-permute-start(bf16[512,2,128]{2,1,0:T(2,128)(2,1)} %reshape.194), channel_id=1, source_target_pairs={{0,4},{4,8},{8,12},{12,16},{16,20},{20,24},{24,28},{28,32},{32,36}... | collective-permute-start | bytes 786440 | tf_op jit(solution)/shard_map/ppermute | solution.py:29
  81.1 1.7 fusion.5
  82.7 15.2 %collective-permute-done = bf16[512,2,128]{2,1,0:T(2,128)(2,1)S(1)} collective-permute-done((bf16[512,2,128]{2,1,0:T(2,128)(2,1)}, bf16[512,2,128]{2,1,0:T(2,128)(2,1)S(1)}, u32[]{:S(2)}, u32[]{:S(2)}) %collective-permute-start) | collective-permute-done | bytes 262176 | tf_op jit(solution)/shard_map/ppermute | solution.py:29
  98.0 4.1 %collective-permute-done.1 = bf16[512,2,128]{2,1,0:T(2,128)(2,1)S(1)} collective-permute-done((bf16[512,2,128]{2,1,0:T(2,128)(2,1)}, bf16[512,2,128]{2,1,0:T(2,128)(2,1)S(1)}, u32[]{:S(2)}, u32[]{:S(2)}) %collective-permute-start.1) | collective-permute-done | bytes 262176 | tf_op jit(solution)/shard_map/ppermute | solution.py:29
  102.1 0.8 pad_maximum_fusion.2.k_ref
  103.0 0.8 pad_maximum_fusion.3.v_ref
  103.8 19.8 %shard_map.137 = (f32[512,1280]{1,0:T(8,128)}, f32[1024,256]{1,0:T(8,128)}, f32[1024,256]{1,0:T(8,128)}) custom-call(bf16[512,1280]{1,0:T(8,128)(2,1)} %get-tuple-element.43.q_ref, bf16[512,1280]{1,0:T(8,128)(2,1)} %get-tuple-element.42.do_ref, bf16[1024,256]{1,0:T(8,128)(2,1)} %pad_maximum_fusion.2.k_ref, bf16[1024,256]{1,0:T(8,128)(2,1)} %pad_maximum_fusion.3.v_ref, ...), custom_call_target="tpu_custom_call" | custom-call | flops 6710886400 | bytes 7864320 | tf_op jit(solution)/shard_map/pallas_call | solution.py:97
  123.6 2.1 copy.43
  125.8 2.3 fusion.6
  128.1 19.8 %shard_map.138 = (f32[512,1280]{1,0:T(8,128)}, f32[1024,256]{1,0:T(8,128)}, f32[1024,256]{1,0:T(8,128)}) custom-call(bf16[512,1280]{1,0:T(8,128)(2,1)} %get-tuple-element.43.q_ref, bf16[512,1280]{1,0:T(8,128)(2,1)} %get-tuple-element.42.do_ref, bf16[1024,256]{1,0:T(8,128)(2,1)} %get-tuple-element.45.k_ref, bf16[1024,256]{1,0:T(8,128)(2,1)} %get-tuple-element.44.v_ref, ...), custom_call_target="tpu_custom_call" | custom-call | flops 6710886400 | bytes 7864320 | tf_op jit(solution)/shard_map/pallas_call | solution.py:97
  147.9 3.2 %pad_maximum_fusion.1 = f32[1024,512]{1,0:T(8,128)} fusion(f32[1024,256]{1,0:T(8,128)} %get-tuple-element.22, f32[1024,256]{1,0:T(8,128)} %get-tuple-element.21), kind=kLoop, calls=%fused_computation.4 | loop fusion | flops 524288 | bytes 4194304 | tf_op jit(solution)/shard_map/concatenate | solution.py:236
  151.0 13.5 %all-to-all-start.3 = ((f32[64,16,512]{2,1,0:T(8,128)}), f32[64,16,512]{2,1,0:T(8,128)}, u32[]{:S(2)}, u32[]{:S(2)}) async-start(f32[64,16,512]{2,1,0:T(8,128)} %bitcast.62), calls=%async_computation.3 | async-start | bytes 4194304 | tf_op jit(solution)/shard_map/all_to_all | solution.py:237
  164.6 1.1 slice.77
  165.6 0.8 convert_element_type.35
  166.4 2.8 %collective-permute-start.3 = (bf16[512,2,128]{2,1,0:T(2,128)(2,1)}, bf16[512,2,128]{2,1,0:T(2,128)(2,1)}, u32[]{:S(2)}, u32[]{:S(2)}) collective-permute-start(bf16[512,2,128]{2,1,0:T(2,128)(2,1)} %convert_element_type.35), channel_id=1, source_target_pairs={{4,0},{8,4},{12,8},{16,12},{20,16},{24,20},{28,24},{32,28},{36,32}... | collective-permute-start | bytes 786440 | tf_op jit(solution)/shard_map/ppermute | solution.py:29
  169.2 1.1 slice.78
  170.3 2.7 %collective-permute-start.2 = (bf16[512,2,128]{2,1,0:T(2,128)(2,1)S(1)}, bf16[512,2,128]{2,1,0:T(2,128)(2,1)}, u32[]{:S(2)}, u32[]{:S(2)}) collective-permute-start(bf16[512,2,128]{2,1,0:T(2,128)(2,1)S(1)} %convert_element_type.32), channel_id=1, source_target_pairs={{4,0},{8,4},{12,8},{16,12},{20,16},{24,20},{28,24},{32,28},{36,32}... | collective-permute-start | bytes 786440 | tf_op jit(solution)/shard_map/ppermute | solution.py:29
  173.0 1.9 slice.55
  174.9 1.9 slice.58
  176.8 1.3 slice.56
  178.1 2.1 slice.59
  180.2 37.4 %collective-permute-done.3 = bf16[512,2,128]{2,1,0:T(2,128)(2,1)} collective-permute-done((bf16[512,2,128]{2,1,0:T(2,128)(2,1)}, bf16[512,2,128]{2,1,0:T(2,128)(2,1)}, u32[]{:S(2)}, u32[]{:S(2)}) %collective-permute-start.3) | collective-permute-done | bytes 262176 | tf_op jit(solution)/shard_map/ppermute | solution.py:29
  217.6 1.4 add_convert_fusion
  219.0 0.7 copy.72
  219.7 2.2 collective-permute-done.2
  222.0 1.3 multiply_convert_fusion.1
  223.3 0.7 copy.73
  224.0 3.2 %copy.44 = f32[512,1280]{0,1:T(8,128)} copy(f32[512,1280]{1,0:T(8,128)} %get-tuple-element.18) | data formatting | bytes 5242880 | tf_op jit(solution)/shard_map/pallas_call | solution.py:97
  227.2 3.5 %multiply_convert_fusion = bf16[512,2,5,128]{0,3,2,1:T(8,128)(2,1)} fusion(f32[512,2,5,128]{0,3,2,1:T(8,128)S(1)} %bitcast.60, f32[512,2,5,128]{0,3,2,1:T(8,128)} %bitcast.61), kind=kLoop, calls=%fused_computation.3 | loop fusion | flops 1966080 | bytes 6553600 | tf_op jit(solution)/shard_map/convert_element_type | solution.py:252
  230.7 2.4 %copy.45 = bf16[512,1280]{1,0:T(8,128)(2,1)} copy(bf16[512,1280]{0,1:T(8,128)(2,1)} %bitcast.67) | data formatting | bytes 2621440
  233.2 1.7 reduce_sum.39
  234.9 0.6 slice.79
  235.5 0.6 fusion.1
  (32 shorter events, 0.4 us)
Async XLA Ops:
  5.5 3.9 %copy-start.6 = (s32[8,16]{1,0:T(8,128)S(1)}, s32[8,16]{1,0:T(8,128)}, u32[]{:S(2)}) copy-start(s32[8,16]{1,0:T(8,128)} %param.19) | copy-start | bytes 1540
  5.5 3.9 %copy-start.7 = (s32[128]{0:T(128)S(1)}, s32[128]{0:T(128)}, u32[]{:S(2)}) copy-start(s32[128]{0:T(128)} %param.18) | copy-start | bytes 1540
  5.5 40.7 %all-to-all-start = ((bf16[128,4,3072]{2,0,1:T(8,128)(2,1)}), bf16[128,4,3072]{2,0,1:T(8,128)(2,1)S(1)}, u32[]{:S(2)}, u32[]{:S(2)}) async-start(bf16[128,4,3072]{2,0,1:T(8,128)(2,1)} %pad_maximum_fusion), calls=%async_computation | async-start | bytes 6291456 | tf_op jit(solution)/shard_map/all_to_all | solution.py:169
  9.8 1.7 copy-start
  11.5 37.9 %copy-start.4 = (bf16[16,256]{1,0:T(8,128)(2,1)S(1)}, bf16[16,256]{1,0:T(8,128)(2,1)}, u32[]{:S(2)}) copy-start(bf16[16,256]{1,0:T(8,128)(2,1)} %param.17) | copy-start | bytes 24580
  11.5 37.9 %copy-start.5 = (bf16[16,256]{1,0:T(8,128)(2,1)S(1)}, bf16[16,256]{1,0:T(8,128)(2,1)}, u32[]{:S(2)}) copy-start(bf16[16,256]{1,0:T(8,128)(2,1)} %param.16) | copy-start | bytes 24580
  11.5 37.9 %copy-start.2 = (f32[10,512]{1,0:T(8,128)S(1)}, f32[10,512]{1,0:T(8,128)}, u32[]{:S(2)}) copy-start(f32[10,512]{1,0:T(8,128)} %param.15) | copy-start | bytes 61444
  46.2 7.2 %all-to-all-start.2 = ((f32[128,4,10]{0,2,1:T(8,128)}), f32[128,4,10]{0,2,1:T(8,128)S(1)}, u32[]{:S(2)}, u32[]{:S(2)}) async-start(f32[128,4,10]{0,2,1:T(8,128)} %reshape.198), calls=%async_computation.2 | async-start | bytes 65536 | tf_op jit(solution)/shard_map/all_to_all | solution.py:170
  50.3 23.8 %copy-start.3 = (s32[1,512]{1,0:T(1,128)}, s32[1,512]{1,0:T(1,128)S(1)}, u32[]{:S(2)}) copy-start(s32[1,512]{1,0:T(1,128)S(1)} %mul.57.lo_ref) | copy-start | bytes 6148
  54.5 71.3 %all-to-all-start.1 = ((bf16[64,16,512]{2,1,0:T(8,128)(2,1)}), bf16[64,16,512]{2,1,0:T(8,128)(2,1)}, u32[]{:S(2)}, u32[]{:S(2)}) async-start(bf16[64,16,512]{2,1,0:T(8,128)(2,1)} %broadcast_in_dim.48), calls=%async_computation.1 | async-start | bytes 2097152 | tf_op jit(solution)/shard_map/all_to_all | solution.py:217
  74.0 28.1 %copy-start.1 = (bf16[512,256]{1,0:T(8,128)(2,1)S(1)}, bf16[512,256]{1,0:T(8,128)(2,1)}, u32[]{:S(2)}) copy-start(bf16[512,256]{1,0:T(8,128)(2,1)} %get-tuple-element.41) | copy-start | bytes 786436
  74.0 23.9 %collective-permute-start = (bf16[512,2,128]{2,1,0:T(2,128)(2,1)}, bf16[512,2,128]{2,1,0:T(2,128)(2,1)S(1)}, u32[]{:S(2)}, u32[]{:S(2)}) collective-permute-start(bf16[512,2,128]{2,1,0:T(2,128)(2,1)} %reshape.193), channel_id=1, source_target_pairs={{0,4},{4,8},{8,12},{12,16},{16,20},{20,24},{24,28},{28,32},{32,36}... | collective-permute-start | bytes 786440 | tf_op jit(solution)/shard_map/ppermute | solution.py:29
  77.5 24.6 %collective-permute-start.1 = (bf16[512,2,128]{2,1,0:T(2,128)(2,1)}, bf16[512,2,128]{2,1,0:T(2,128)(2,1)S(1)}, u32[]{:S(2)}, u32[]{:S(2)}) collective-permute-start(bf16[512,2,128]{2,1,0:T(2,128)(2,1)} %reshape.194), channel_id=1, source_target_pairs={{0,4},{4,8},{8,12},{12,16},{16,20},{20,24},{24,28},{28,32},{32,36}... | collective-permute-start | bytes 786440 | tf_op jit(solution)/shard_map/ppermute | solution.py:29
  151.0 82.1 %all-to-all-start.3 = ((f32[64,16,512]{2,1,0:T(8,128)}), f32[64,16,512]{2,1,0:T(8,128)}, u32[]{:S(2)}, u32[]{:S(2)}) async-start(f32[64,16,512]{2,1,0:T(8,128)} %bitcast.62), calls=%async_computation.3 | async-start | bytes 4194304 | tf_op jit(solution)/shard_map/all_to_all | solution.py:237
  166.4 51.2 %collective-permute-start.3 = (bf16[512,2,128]{2,1,0:T(2,128)(2,1)}, bf16[512,2,128]{2,1,0:T(2,128)(2,1)}, u32[]{:S(2)}, u32[]{:S(2)}) collective-permute-start(bf16[512,2,128]{2,1,0:T(2,128)(2,1)} %convert_element_type.35), channel_id=1, source_target_pairs={{4,0},{8,4},{12,8},{16,12},{20,16},{24,20},{28,24},{32,28},{36,32}... | collective-permute-start | bytes 786440 | tf_op jit(solution)/shard_map/ppermute | solution.py:29
  170.3 51.7 %collective-permute-start.2 = (bf16[512,2,128]{2,1,0:T(2,128)(2,1)S(1)}, bf16[512,2,128]{2,1,0:T(2,128)(2,1)}, u32[]{:S(2)}, u32[]{:S(2)}) collective-permute-start(bf16[512,2,128]{2,1,0:T(2,128)(2,1)S(1)} %convert_element_type.32), channel_id=1, source_target_pairs={{4,0},{8,4},{12,8},{16,12},{20,16},{24,20},{28,24},{32,28},{36,32}... | collective-permute-start | bytes 786440 | tf_op jit(solution)/shard_map/ppermute | solution.py:29

commit v6 on v5

--- a/solution.py
+++ b/solution.py
@@ -47,85 +47,91 @@
     return first, prompt_block
 
 
-TT = 256
-
-
-def tile_body(q_ref, do_ref, k_ref, v_ref, n_ref, d_ref, lo_ref, hi_ref, dq_ref, dk_ref, dv_ref):
-    i = pl.program_id(1)
+CH = 128
+
+
+def tile_body(need_ref, q_ref, do_ref, k_ref, v_ref, n_ref, d_ref, lo_ref, hi_ref, dq_ref, dkv_ref):
     f32, bf16 = jnp.float32, jnp.bfloat16
     scale = 1.0 / math.sqrt(HD)
-    keys, values = k_ref[...], v_ref[...]
-    span, rows = keys.shape[0], q_ref.shape[0]
-    u = lax.broadcasted_iota(jnp.int32, (span, rows), 0)
-    allowed = (u >= lo_ref[...]) & (u <= hi_ref[...])
+    nt = (((1,), (1,)), ((), ()))
+    rows, span, grp = q_ref.shape[0], k_ref.shape[0], n_ref.shape[1]
     nrm, dlt = n_ref[0], d_ref[0]
-    nt = (((1,), (1,)), ((), ()))
-    dk_acc = jnp.zeros((span, HD), f32)
-    dv_acc = jnp.zeros((span, HD), f32)
-    for r in range(nrm.shape[0]):
-        cols = slice(r * HD, (r + 1) * HD)
-        qr, dor = q_ref[:, cols], do_ref[:, cols]
-        st = lax.dot_general(keys, qr, nt, preferred_element_type=f32)
-        wt = jnp.where(allowed, jnp.exp(st * scale - nrm[r : r + 1, :]), 0.0)
-        dv_acc = dv_acc + jnp.dot(wt.astype(bf16), dor, preferred_element_type=f32)
-        dwt = lax.dot_general(values, dor, nt, preferred_element_type=f32)
-        dlt_r = wt * (dwt - dlt[r : r + 1, :])
-        dlb = dlt_r.astype(bf16)
-        dk_acc = dk_acc + jnp.dot(dlb, qr, preferred_element_type=f32)
-        dq_ref[:, cols] = jnp.dot(
-            dlt_r.T.astype(bf16), keys, preferred_element_type=f32
-        )
-
-    @pl.when(i == 0)
-    def _():
-        dk_ref[...] = dk_acc
-        dv_ref[...] = dv_acc
-
-    @pl.when(i > 0)
-    def _():
-        dk_ref[...] += dk_acc
-        dv_ref[...] += dv_acc
+    lo, hi = lo_ref[...], hi_ref[...]
+    dq_ref[...] = jnp.zeros_like(dq_ref)
+    for c in range(span // CH):
+        ks = slice(c * CH, (c + 1) * CH)
+
+        @pl.when(need_ref[c] > 0)
+        def _():
+            keys, values = k_ref[ks, :], v_ref[ks, :]
+            u = c * CH + lax.broadcasted_iota(jnp.int32, (CH, rows), 0)
+            allowed = (u >= lo) & (u <= hi)
+            dk_acc = jnp.zeros((CH, HD), f32)
+            dv_acc = jnp.zeros((CH, HD), f32)
+            for r in range(grp):
+                cols = slice(r * HD, (r + 1) * HD)
+                qr, dor = q_ref[:, cols], do_ref[:, cols]
+                st = lax.dot_general(keys, qr, nt, preferred_element_type=f32)
+                wt = jnp.where(allowed, jnp.exp(st * scale - nrm[r : r + 1, :]), 0.0)
+                dv_acc = dv_acc + jnp.dot(wt.astype(bf16), dor, preferred_element_type=f32)
+                dwt = lax.dot_general(values, dor, nt, preferred_element_type=f32)
+                dlt_r = wt * (dwt - dlt[r : r + 1, :])
+                dk_acc = dk_acc + jnp.dot(dlt_r.astype(bf16), qr, preferred_element_type=f32)
+                dq_ref[:, cols] += jnp.dot(
+                    dlt_r.T.astype(bf16), keys, preferred_element_type=f32
+                )
+            dkv_ref[ks, 0:HD] = dk_acc
+            dkv_ref[ks, HD : 2 * HD] = dv_acc
+
+        @pl.when(need_ref[c] == 0)
+        def _():
+            dkv_ref[ks, :] = jnp.zeros((CH, 2 * HD), f32)
 
 
 def tile_kernel(q, do, keys, values, norms, delta, lo, hi):
     tokens, lq = q.shape
     span, lk = keys.shape
     kvh, grp = norms.shape[0], norms.shape[1]
-    rows = min(TT, tokens)
     width = grp * HD
+    starts = jnp.arange(span // CH, dtype=jnp.int32) * CH
+    need = jnp.any(
+        (lo.reshape(-1)[None, :] <= starts[:, None] + CH - 1)
+        & (hi.reshape(-1)[None, :] >= starts[:, None]),
+        axis=1,
+    ).astype(jnp.int32)
     flops = 10 * tokens * span * HD * kvh * grp
+    grid_spec = pltpu.PrefetchScalarGridSpec(
+        num_scalar_prefetch=1,
+        grid=(kvh,),
+        in_specs=[
+            pl.BlockSpec((tokens, width), lambda g, n: (0, g)),
+            pl.BlockSpec((tokens, width), lambda g, n: (0, g)),
+            pl.BlockSpec((span, HD), lambda g, n: (0, g)),
+            pl.BlockSpec((span, HD), lambda g, n: (0, g)),
+            pl.BlockSpec((1, grp, tokens), lambda g, n: (g, 0, 0)),
+            pl.BlockSpec((1, grp, tokens), lambda g, n: (g, 0, 0)),
+            pl.BlockSpec((1, tokens), lambda g, n: (0, 0)),
+            pl.BlockSpec((1, tokens), lambda g, n: (0, 0)),
+        ],
+        out_specs=[
+            pl.BlockSpec((tokens, width), lambda g, n: (0, g)),
+            pl.BlockSpec((span, 2 * HD), lambda g, n: (0, g)),
+        ],
+    )
     return pl.pallas_call(
         tile_body,
-        grid=(kvh, tokens // rows),
-        in_specs=[
-            pl.BlockSpec((rows, width), lambda g, i: (i, g)),
-            pl.BlockSpec((rows, width), lambda g, i: (i, g)),
-            pl.BlockSpec((span, HD), lambda g, i: (0, g)),
-            pl.BlockSpec((span, HD), lambda g, i: (0, g)),
-            pl.BlockSpec((1, grp, rows), lambda g, i: (g, 0, i)),
-            pl.BlockSpec((1, grp, rows), lambda g, i: (g, 0, i)),
-            pl.BlockSpec((1, rows), lambda g, i: (0, i)),
-            pl.BlockSpec((1, rows), lambda g, i: (0, i)),
-        ],
-        out_specs=[
-            pl.BlockSpec((rows, width), lambda g, i: (i, g)),
-            pl.BlockSpec((span, HD), lambda g, i: (0, g)),
-            pl.BlockSpec((span, HD), lambda g, i: (0, g)),
-        ],
+        grid_spec=grid_spec,
         out_shape=[
             jax.ShapeDtypeStruct((tokens, lq), jnp.float32),
-            jax.ShapeDtypeStruct((span, lk), jnp.float32),
-            jax.ShapeDtypeStruct((span, lk), jnp.float32),
+            jax.ShapeDtypeStruct((span, 2 * lk), jnp.float32),
         ],
-        compiler_params=pltpu.CompilerParams(
-            dimension_semantics=("arbitrary", "arbitrary")
-        ),
+        compiler_params=pltpu.CompilerParams(dimension_semantics=("arbitrary",)),
         cost_estimate=pl.CostEstimate(
             flops=flops,
             transcendentals=tokens * span * kvh * grp,
-            bytes_accessed=4 * tokens * lq * 2 + 2 * span * lk * 5,
+            bytes_accessed=4 * tokens * lq * 2 + 2 * span * lk * 6,
         ),
-    )(q, do, keys, values, norms, delta, lo, hi)
+    )(need, q, do, keys, values, norms, delta, lo, hi)
 
 
 def make_shards(parts):
@@ -194,21 +200,18 @@
         )
         local_start = jnp.repeat(first * BLK, BLK) - base
 
-        k_prior, v_prior = shifted((k, v), names, sizes, 1)
-
-        dq, dk, dv = tile_kernel(
+        kv = got[:, 2 * lq :]
+        kv_prior = shifted(kv, names, sizes, 1)
+        dq, dkv = tile_kernel(
             got[:, :lq],
             got[:, lq : 2 * lq],
-            jnp.concatenate([k_prior, k], axis=0).reshape(2 * tokens, lk),
-            jnp.concatenate([v_prior, v], axis=0).reshape(2 * tokens, lk),
+            jnp.concatenate([kv_prior[:, :lk], kv[:, :lk]], axis=0),
+            jnp.concatenate([kv_prior[:, lk:], kv[:, lk:]], axis=0),
             norms,
             delta,
             (local_start + tokens).reshape(1, tokens).astype(jnp.int32),
             (jnp.arange(tokens, dtype=jnp.int32) + tokens).reshape(1, tokens),
         )
-        dq = dq.reshape(tokens, kvh, grp, HD)
-        dk = dk.reshape(2 * tokens, kvh, HD)
-        dv = dv.reshape(2 * tokens, kvh, HD)
 
         pkv, _ = lax.optimization_barrier(
             (jnp.concatenate([prefix_keys, prefix_values], axis=1), got)
@@ -223,7 +226,7 @@
         ).reshape(nctx * pkv.shape[0], pkv.shape[1])
         pkv, dq = lax.optimization_barrier((pkv, dq))
         prompt_lo = (jnp.repeat(prompt_block, BLK) * PL).astype(jnp.int32)
-        dq_p, pgrad_k, pgrad_v = tile_kernel(
+        dq_p, pgrad = tile_kernel(
             got[:, :lq],
             got[:, lq : 2 * lq],
             pkv[:, :lk],
@@ -233,7 +236,6 @@
             prompt_lo.reshape(1, tokens),
             (prompt_lo + PL - 1).reshape(1, tokens),
         )
-        pgrad = jnp.concatenate([pgrad_k, pgrad_v], axis=1)
         pgrad = lax.all_to_all(
             pgrad.reshape(nctx, -1, pgrad.shape[1]),
             names,
@@ -241,19 +243,16 @@
             concat_axis=0,
             tiled=True,
         ).sum(axis=0)
-
-        dq = dq + dq_p.reshape(tokens, kvh, grp, HD)
-        back_k, back_v = shifted(
-            (dk[:tokens].astype(bf16), dv[:tokens].astype(bf16)), names, sizes, -1
-        )
-        key_grad = (dk[tokens:] + back_k.astype(f32)) * scale
-        value_grad = dv[tokens:] + back_v.astype(f32)
+        pgrad = pgrad.reshape(-1, kvh, 2, HD)
+
+        back = shifted(dkv[:tokens].astype(bf16), names, sizes, -1)
+        kv_grad = (dkv[tokens:] + back.astype(f32)).reshape(tokens, kvh, 2, HD)
         return (
-            (dq * scale).astype(bf16).reshape(tokens, lq),
-            key_grad.astype(bf16).reshape(tokens, lk),
-            value_grad.astype(bf16).reshape(tokens, lk),
-            (pgrad[:, :lk] * scale).astype(bf16),
-            pgrad[:, lk:].astype(bf16),
+            ((dq + dq_p) * scale).astype(bf16),
+            (kv_grad[:, :, 0] * scale).astype(bf16).reshape(tokens, lk),
+            kv_grad[:, :, 1].astype(bf16).reshape(tokens, lk),
+            (pgrad[:, :, 0] * scale).astype(bf16).reshape(-1, lk),
+            pgrad[:, :, 1].astype(bf16).reshape(-1, lk),
         )
 
     return shards, names

time: 237 us -> 239 us (level)
  waiting for transfers between devices: 93.7 us -> 112 us
  local copies, waits for them, and re-layouts: 36.2 us -> 22.4 us
  Pallas kernels: 39.6 us -> 49.6 us
  starting transfers between devices: 47.7 us -> 41.1 us
  other arithmetic: 17.9 us -> 13.2 us
    ppermute x4 -> x2, waiting for transfers between devices: 59 us -> 79.6 us  [shifted(): return lax.ppermute(array, axes, pairs)]
    pallas_call x2, Pallas kernels: 39.6 us -> 49.6 us  [tile_kernel(): pl.pallas_call(tile_body, grid_spec=grid_spec, out_shape=[jax.ShapeDtypeS...]
    slice x8 -> x7, local copies, waits for them, and re-layouts: 10.6 us -> 3.24 us  [the longest x1 1.84 us: shards(): kv_grad[:, :, 1].astype(bf16).reshape(tokens, lk)]
    ppermute x4 -> x2, starting transfers between devices: 12.5 us -> 6.14 us  [shifted(): return lax.ppermute(array, axes, pairs)]
    pallas_call x2 -> x0, local copies, waits for them, and re-layouts: 5.37 us -> none  [tile_kernel(): pl.pallas_call(tile_body, grid=(kvh, tokens // rows), in_specs=[pl.BlockS...]
    concatenate x3 -> x2, other arithmetic: 4.84 us -> 1.67 us  [the longest x1 0.85 us: shards(): jnp.concatenate([kv_prior[:, :lk], kv[:, :lk]], axis=0)]
    unnamed x25 -> x24, local copies, waits for them, and re-layouts: 5.97 us -> 6.24 us
  transfers between devices with their start and end apart: 8 -> 6, of which waited for: 6 -> 4; matrix products, arithmetic and copies ran while one was open for 17% -> 11% of each run, Pallas kernels for 8% -> 14%
where the time goes in v6:
time: 239 us
  waiting for transfers between devices  112 us (47%)
  Pallas kernels  49.6 us (21%)
  starting transfers between devices  41.1 us (17%)
  local copies, waits for them, and re-layouts  22.4 us (9%)
  other arithmetic  13.2 us (6%)
    ppermute x2, waiting for transfers between devices, shifted(): return lax.ppermute(array, axes, pairs)  79.6 us
    pallas_call x2, Pallas kernels, tile_kernel(): pl.pallas_call(tile_body, grid_spec=grid_spec, out_shape=[jax.ShapeDtypeS...  49.6 us
    all_to_all x1, waiting for transfers between devices, shards(): lax.all_to_all(packed, 'head', split_axis=1, concat_axis=0, tiled=True)  31.1 us
    all_to_all x1, starting transfers between devices, shards(): lax.all_to_all(jnp.broadcast_to(pkv[None], (nctx,) + pkv.shape), names, s...  14.6 us
    all_to_all x1, starting transfers between devices, shards(): lax.all_to_all(pgrad.reshape(nctx, -1, pgrad.shape[1]), names, split_axis...  13.4 us
    unnamed x24, local copies, waits for them, and re-layouts  6.24 us
    ppermute x2, starting transfers between devices, shifted(): return lax.ppermute(array, axes, pairs)  6.14 us
  transfers between devices with their start and end apart: 6, of which 4 were waited for; matrix products, arithmetic and copies ran while one was open for 11% of the time, Pallas kernels for 14%

profile of v6, /device:TPU:22, one launch (start us, length us, event | category | flops | bytes accessed | tf_op | source)
XLA Modules:
  0.0 239.4 jit_solution(3009787184199924463)
XLA Ops:
  0.6 1.1 copy_bitcast_fusion.2
  1.7 1.9 copy_bitcast_fusion
  3.6 1.9 pad_maximum_fusion
  5.5 3.8 %all-to-all-start = ((bf16[128,4,3072]{2,0,1:T(8,128)(2,1)}), bf16[128,4,3072]{2,0,1:T(8,128)(2,1)S(1)}, u32[]{:S(2)}, u32[]{:S(2)}) async-start(bf16[128,4,3072]{2,0,1:T(8,128)(2,1)} %pad_maximum_fusion), calls=%async_computation | async-start | bytes 6291456 | tf_op jit(solution)/shard_map/all_to_all | solution.py:175
  9.3 0.0 copy-done.5
  9.3 0.1 eq.31
  9.4 0.1 copy.43
  9.5 0.2 reduce-window.9
  9.7 0.1 reduce.1
  9.9 0.2 fusion.5
  10.0 0.1 select_reduce_fusion
  10.2 0.2 select_reduce_fusion.1
  10.4 0.1 broadcast_in_dim.58
  10.4 0.1 mul.86.lo_ref
  10.5 0.1 mul.85
  10.6 0.1 broadcast_in_dim.54
  10.7 0.1 add.94
  10.7 1.7 copy.62
  12.4 0.0 copy-done
  12.5 0.0 copy-start.1
  12.5 0.3 copy.61
  12.8 0.8 fusion
  13.5 0.1 copy.53
  13.6 0.6 reshape.202
  14.2 0.2 and_reduce_fusion
  14.5 0.6 broadcast_add_fusion.hi_ref
  15.1 31.1 %all-to-all-done = bf16[128,4,3072]{2,0,1:T(8,128)(2,1)S(1)} async-done(((bf16[128,4,3072]{2,0,1:T(8,128)(2,1)}), bf16[128,4,3072]{2,0,1:T(8,128)(2,1)S(1)}, u32[]{:S(2)}, u32[]{:S(2)}) %all-to-all-start) | async-done | bytes 3145760 | tf_op jit(solution)/shard_map/all_to_all | solution.py:175
  46.2 3.3 %all-to-all-start.2 = ((f32[128,4,10]{0,2,1:T(8,128)}), f32[128,4,10]{0,2,1:T(8,128)S(1)}, u32[]{:S(2)}, u32[]{:S(2)}) async-start(f32[128,4,10]{0,2,1:T(8,128)} %reshape.202), calls=%async_computation.2 | async-start | bytes 65536 | tf_op jit(solution)/shard_map/all_to_all | solution.py:176
  49.5 0.7 add.96.lo_ref
  50.1 0.6 reshape.199.n_ref
  50.8 0.5 convert_element_type.42.need_ref
  51.3 0.5 convert_element_type.40.need_ref
  51.9 1.5 all-to-all-done.2
  53.4 1.2 broadcast_in_dim.52
  54.6 14.6 %all-to-all-start.1 = ((bf16[64,16,512]{2,1,0:T(8,128)(2,1)}), bf16[64,16,512]{2,1,0:T(8,128)(2,1)}, u32[]{:S(2)}, u32[]{:S(2)}) async-start(bf16[64,16,512]{2,1,0:T(8,128)(2,1)} %broadcast_in_dim.52), calls=%async_computation.1 | async-start | bytes 2097152 | tf_op jit(solution)/shard_map/all_to_all | solution.py:220
  69.1 0.6 iota_add_fusion.hi_ref
  69.8 0.6 reshape.204.d_ref
  70.4 3.4 %collective-permute-start = (bf16[512,512]{1,0:T(8,128)(2,1)S(1)}, bf16[512,512]{1,0:T(8,128)(2,1)S(1)}, u32[]{:S(2)}, u32[]{:S(2)}) collective-permute-start(bf16[512,512]{1,0:T(8,128)(2,1)S(1)} %slice.69), channel_id=1, source_target_pairs={{0,4},{4,8},{8,12},{12,16},{16,20},{20,24},{24,28},{28,32},{32,36}... | collective-permute-start | bytes 1572872 | tf_op jit(solution)/shard_map/ppermute | solution.py:29
  73.8 1.7 fusion.7
  75.5 26.6 %collective-permute-done = bf16[512,512]{1,0:T(8,128)(2,1)S(1)} collective-permute-done((bf16[512,512]{1,0:T(8,128)(2,1)S(1)}, bf16[512,512]{1,0:T(8,128)(2,1)S(1)}, u32[]{:S(2)}, u32[]{:S(2)}) %collective-permute-start) | collective-permute-done | bytes 524320 | tf_op jit(solution)/shard_map/ppermute | solution.py:29
  102.1 0.8 pad_maximum_fusion.2.v_ref
  102.9 0.8 pad_maximum_fusion.1.k_ref
  103.8 34.0 %shard_map.137 = (f32[512,1280]{1,0:T(8,128)}, f32[1024,512]{1,0:T(8,128)}) custom-call(s32[8]{0:T(128)} %convert_element_type.40.need_ref, bf16[512,1280]{1,0:T(8,128)(2,1)} %get-tuple-element.43.q_ref, bf16[512,1280]{1,0:T(8,128)(2,1)} %get-tuple-element.42.do_ref, bf16[1024,256]{1,0:T(8,128)(2,1)} %pad_maximum_fusion.1.k_ref, ...), custom_call_target="tpu_custom_call" | custom-call | flops 6710886400 | bytes 8388608 | tf_op jit(solution)/shard_map/pallas_call | solution.py:121
  137.8 0.0 all-to-all-done.1
  137.8 2.2 fusion.8
  140.0 15.6 %shard_map.138 = (f32[512,1280]{1,0:T(8,128)}, f32[1024,512]{1,0:T(8,128)}) custom-call(s32[8]{0:T(128)} %convert_element_type.42.need_ref, bf16[512,1280]{1,0:T(8,128)(2,1)} %get-tuple-element.43.q_ref, bf16[512,1280]{1,0:T(8,128)(2,1)} %get-tuple-element.42.do_ref, bf16[1024,256]{1,0:T(8,128)(2,1)} %get-tuple-element.45.k_ref, ...), custom_call_target="tpu_custom_call" | custom-call | flops 6710886400 | bytes 8388608 | tf_op jit(solution)/shard_map/pallas_call | solution.py:121
  155.6 13.4 %all-to-all-start.3 = ((f32[64,16,512]{2,1,0:T(8,128)}), f32[64,16,512]{2,1,0:T(8,128)S(1)}, u32[]{:S(2)}, u32[]{:S(2)}) async-start(f32[64,16,512]{2,1,0:T(8,128)} %bitcast.56), calls=%async_computation.3 | async-start | bytes 4194304 | tf_op jit(solution)/shard_map/all_to_all | solution.py:239
  169.0 1.3 slice.89
  170.3 2.8 %collective-permute-start.1 = (bf16[512,512]{1,0:T(8,128)(2,1)S(1)}, bf16[512,512]{1,0:T(8,128)(2,1)S(1)}, u32[]{:S(2)}, u32[]{:S(2)}) collective-permute-start(bf16[512,512]{1,0:T(8,128)(2,1)S(1)} %slice.89), channel_id=1, source_target_pairs={{4,0},{8,4},{12,8},{16,12},{20,16},{24,20},{28,24},{32,28},{36,32}... | collective-permute-start | bytes 1572872 | tf_op jit(solution)/shard_map/ppermute | solution.py:29
  173.1 53.0 %collective-permute-done.1 = bf16[512,512]{1,0:T(8,128)(2,1)S(1)} collective-permute-done((bf16[512,512]{1,0:T(8,128)(2,1)S(1)}, bf16[512,512]{1,0:T(8,128)(2,1)S(1)}, u32[]{:S(2)}, u32[]{:S(2)}) %collective-permute-start.1) | collective-permute-done | bytes 524320 | tf_op jit(solution)/shard_map/ppermute | solution.py:29
  226.1 1.4 convert_add_fusion
  227.4 1.6 reshape.205
  229.1 1.8 slice.76
  230.9 0.7 copy.56
  231.6 0.8 copy.48
  232.4 0.0 slice-done
  232.4 0.7 copy.55
  233.2 0.8 copy.47
  234.0 3.9 %multiply_convert_fusion = bf16[512,1280]{1,0:T(8,128)(2,1)} fusion(f32[512,1280]{1,0:T(8,128)} %get-tuple-element.14, f32[512,1280]{1,0:T(8,128)} %get-tuple-element.16), kind=kLoop, calls=%fused_computation.3 | loop fusion | flops 1966080 | bytes 6553600 | tf_op jit(solution)/shard_map/convert_element_type | solution.py:251
  237.9 0.0 all-to-all-done.3
  237.9 0.1 reduce_sum.39
  238.1 0.1 fusion.1
  238.2 0.6 copy.74
  238.8 0.6 copy.75
  (29 shorter events, 0.3 us)
Async XLA Ops:
  5.5 3.9 %copy-start.5 = (s32[8,16]{1,0:T(8,128)S(1)}, s32[8,16]{1,0:T(8,128)}, u32[]{:S(2)}) copy-start(s32[8,16]{1,0:T(8,128)} %param.19) | copy-start | bytes 1540
  5.5 3.9 %copy-start.6 = (s32[128]{0:T(128)S(1)}, s32[128]{0:T(128)}, u32[]{:S(2)}) copy-start(s32[128]{0:T(128)} %param.18) | copy-start | bytes 1540
  5.5 40.7 %all-to-all-start = ((bf16[128,4,3072]{2,0,1:T(8,128)(2,1)}), bf16[128,4,3072]{2,0,1:T(8,128)(2,1)S(1)}, u32[]{:S(2)}, u32[]{:S(2)}) async-start(bf16[128,4,3072]{2,0,1:T(8,128)(2,1)} %pad_maximum_fusion), calls=%async_computation | async-start | bytes 6291456 | tf_op jit(solution)/shard_map/all_to_all | solution.py:175
  10.5 4.0 %copy-start.2 = (s32[1,512]{1,0:T(1,128)}, s32[1,512]{1,0:T(1,128)S(1)}, u32[]{:S(2)}) copy-start(s32[1,512]{1,0:T(1,128)S(1)} %mul.86.lo_ref) | copy-start | bytes 6148
  10.7 1.7 copy-start
  12.5 37.0 %copy-start.3 = (bf16[16,256]{1,0:T(8,128)(2,1)S(1)}, bf16[16,256]{1,0:T(8,128)(2,1)}, u32[]{:S(2)}) copy-start(bf16[16,256]{1,0:T(8,128)(2,1)} %param.17) | copy-start | bytes 24580
  12.5 37.0 %copy-start.4 = (bf16[16,256]{1,0:T(8,128)(2,1)S(1)}, bf16[16,256]{1,0:T(8,128)(2,1)}, u32[]{:S(2)}) copy-start(bf16[16,256]{1,0:T(8,128)(2,1)} %param.16) | copy-start | bytes 24580
  12.5 37.7 %copy-start.1 = (f32[10,512]{1,0:T(8,128)S(1)}, f32[10,512]{1,0:T(8,128)}, u32[]{:S(2)}) copy-start(f32[10,512]{1,0:T(8,128)} %param.15) | copy-start | bytes 61444
  46.2 7.2 %all-to-all-start.2 = ((f32[128,4,10]{0,2,1:T(8,128)}), f32[128,4,10]{0,2,1:T(8,128)S(1)}, u32[]{:S(2)}, u32[]{:S(2)}) async-start(f32[128,4,10]{0,2,1:T(8,128)} %reshape.202), calls=%async_computation.2 | async-start | bytes 65536 | tf_op jit(solution)/shard_map/all_to_all | solution.py:176
  54.6 83.2 %all-to-all-start.1 = ((bf16[64,16,512]{2,1,0:T(8,128)(2,1)}), bf16[64,16,512]{2,1,0:T(8,128)(2,1)}, u32[]{:S(2)}, u32[]{:S(2)}) async-start(bf16[64,16,512]{2,1,0:T(8,128)(2,1)} %broadcast_in_dim.52), calls=%async_computation.1 | async-start | bytes 2097152 | tf_op jit(solution)/shard_map/all_to_all | solution.py:220
  70.4 31.7 %collective-permute-start = (bf16[512,512]{1,0:T(8,128)(2,1)S(1)}, bf16[512,512]{1,0:T(8,128)(2,1)S(1)}, u32[]{:S(2)}, u32[]{:S(2)}) collective-permute-start(bf16[512,512]{1,0:T(8,128)(2,1)S(1)} %slice.69), channel_id=1, source_target_pairs={{0,4},{4,8},{8,12},{12,16},{16,20},{20,24},{24,28},{28,32},{32,36}... | collective-permute-start | bytes 1572872 | tf_op jit(solution)/shard_map/ppermute | solution.py:29
  155.6 82.3 %all-to-all-start.3 = ((f32[64,16,512]{2,1,0:T(8,128)}), f32[64,16,512]{2,1,0:T(8,128)S(1)}, u32[]{:S(2)}, u32[]{:S(2)}) async-start(f32[64,16,512]{2,1,0:T(8,128)} %bitcast.56), calls=%async_computation.3 | async-start | bytes 4194304 | tf_op jit(solution)/shard_map/all_to_all | solution.py:239
  170.3 55.8 %collective-permute-start.1 = (bf16[512,512]{1,0:T(8,128)(2,1)S(1)}, bf16[512,512]{1,0:T(8,128)(2,1)S(1)}, u32[]{:S(2)}, u32[]{:S(2)}) collective-permute-start(bf16[512,512]{1,0:T(8,128)(2,1)S(1)} %slice.89), channel_id=1, source_target_pairs={{4,0},{8,4},{12,8},{16,12},{20,16},{24,20},{28,24},{32,28},{36,32}... | collective-permute-start | bytes 1572872 | tf_op jit(solution)/shard_map/ppermute | solution.py:29
  229.1 3.4 %slice-start = ((f32[512,2,2,128]{3,2,1,0:T(2,128)}), f32[512,2,1,128]{3,2,1,0:T(1,128)S(1)}, s32[]{:S(2)}) async-start(f32[512,2,2,128]{3,2,1,0:T(2,128)} %reshape.205), calls=%async_computation.4 | async-start | bytes 1048576 | tf_op jit(solution)/shard_map/slice | solution.py:252

commit v7 on v6

--- a/solution.py
+++ b/solution.py
@@ -58,8 +58,9 @@
     nrm, dlt = n_ref[0], d_ref[0]
     lo, hi = lo_ref[...], hi_ref[...]
     dq_ref[...] = jnp.zeros_like(dq_ref)
-    for c in range(span // CH):
-        ks = slice(c * CH, (c + 1) * CH)
+
+    def chunk(c, carry):
+        ks = pl.ds(pl.multiple_of(c * CH, CH), CH)
 
         @pl.when(need_ref[c] > 0)
         def _():
@@ -87,6 +88,9 @@
         def _():
             dkv_ref[ks, :] = jnp.zeros((CH, 2 * HD), f32)
 
+        return carry
+
+    lax.fori_loop(0, span // CH, chunk, 0)
 
 def tile_kernel(q, do, keys, values, norms, delta, lo, hi):
     tokens, lq = q.shape
@@ -202,16 +206,23 @@
 
         kv = got[:, 2 * lq :]
         kv_prior = shifted(kv, names, sizes, 1)
+        t = jnp.arange(tokens, dtype=jnp.int32).reshape(1, tokens)
+        ls = local_start.reshape(1, tokens).astype(jnp.int32)
         dq, dkv = tile_kernel(
+            got[:, :lq], got[:, lq : 2 * lq], kv[:, :lk], kv[:, lk:], norms, delta, ls, t
+        )
+        dq_b, dkv_b = tile_kernel(
             got[:, :lq],
             got[:, lq : 2 * lq],
-            jnp.concatenate([kv_prior[:, :lk], kv[:, :lk]], axis=0),
-            jnp.concatenate([kv_prior[:, lk:], kv[:, lk:]], axis=0),
+            kv_prior[:, :lk],
+            kv_prior[:, lk:],
             norms,
             delta,
-            (local_start + tokens).reshape(1, tokens).astype(jnp.int32),
-            (jnp.arange(tokens, dtype=jnp.int32) + tokens).reshape(1, tokens),
-        )
+            ls + tokens,
+            jnp.full((1, tokens), tokens - 1, jnp.int32),
+        )
+        back = shifted(dkv_b.astype(bf16), names, sizes, -1)
+        dq = dq + dq_b
 
         pkv, _ = lax.optimization_barrier(
             (jnp.concatenate([prefix_keys, prefix_values], axis=1), got)
@@ -245,8 +256,7 @@
         ).sum(axis=0)
         pgrad = pgrad.reshape(-1, kvh, 2, HD)
 
-        back = shifted(dkv[:tokens].astype(bf16), names, sizes, -1)
-        kv_grad = (dkv[tokens:] + back.astype(f32)).reshape(tokens, kvh, 2, HD)
+        kv_grad = (dkv + back.astype(f32)).reshape(tokens, kvh, 2, HD)
         return (
             ((dq + dq_p) * scale).astype(bf16),
             (kv_grad[:, :, 0] * scale).astype(bf16).reshape(tokens, lk),

time: 239 us -> 231 us (0.967)
  waiting for transfers between devices: 112 us -> 91 us
  other arithmetic: 13.2 us -> 19.2 us
  local copies, waits for them, and re-layouts: 22.4 us -> 28.2 us
  starting transfers between devices: 41.1 us -> 37.8 us
  Pallas kernels: 49.6 us -> 52.7 us
    ppermute x2, waiting for transfers between devices: 79.6 us -> 57.9 us  [shifted(): return lax.ppermute(array, axes, pairs)]
    add x4, other arithmetic: 1.97 us -> 5.78 us  [the longest x1 2.83 us: shards(): dq = dq + dq_b]
    all_to_all x1, starting transfers between devices: 13.4 us -> 9.88 us  [shards(): lax.all_to_all(pgrad.reshape(nctx, -1, pgrad.shape[1]), names, split_axis...]
    pallas_call x2 -> x3, Pallas kernels: 49.6 us -> 52.7 us  [tile_kernel(): pl.pallas_call(tile_body, grid_spec=grid_spec, out_shape=[jax.ShapeDtypeS...]
    unnamed x24 -> x26, local copies, waits for them, and re-layouts: 6.24 us -> 7.5 us
  transfers between devices with their start and end apart: 6 -> 6, of which waited for: 4 -> 4; matrix products, arithmetic and copies ran while one was open for 11% -> 16% of each run, Pallas kernels for 14% -> 16%
where the time goes in v7:
time: 231 us; the launch traced here: 230 us
  waiting for transfers between devices  91 us (39%)
  Pallas kernels  52.7 us (23%)
  starting transfers between devices  37.8 us (16%)
  local copies, waits for them, and re-layouts  28.2 us (12%)
  other arithmetic  19.2 us (8%)
    ppermute x2, waiting for transfers between devices, shifted(): return lax.ppermute(array, axes, pairs)  57.9 us
    pallas_call x3, Pallas kernels, tile_kernel(): pl.pallas_call(tile_body, grid_spec=grid_spec, out_shape=[jax.ShapeDtypeS...  52.7 us
    all_to_all x1, waiting for transfers between devices, shards(): lax.all_to_all(packed, 'head', split_axis=1, concat_axis=0, tiled=True)  31.6 us
    all_to_all x1, starting transfers between devices, shards(): lax.all_to_all(jnp.broadcast_to(pkv[None], (nctx,) + pkv.shape), names, s...  14.6 us
    all_to_all x1, starting transfers between devices, shards(): lax.all_to_all(pgrad.reshape(nctx, -1, pgrad.shape[1]), names, split_axis...  9.88 us
    unnamed x26, local copies, waits for them, and re-layouts  7.5 us
    ppermute x2, starting transfers between devices, shifted(): return lax.ppermute(array, axes, pairs)  6.31 us
  transfers between devices with their start and end apart: 6, of which 4 were waited for; matrix products, arithmetic and copies ran while one was open for 16% of the time, Pallas kernels for 16%

profile of v7, /device:TPU:22, one launch (start us, length us, event | category | flops | bytes accessed | tf_op | source)
XLA Modules:
  0.0 229.9 jit_solution(14169479758227452593)
XLA Ops:
  0.6 1.1 copy_bitcast_fusion.2
  1.7 1.9 copy_bitcast_fusion
  3.6 1.9 pad_maximum_fusion
  5.5 3.8 %all-to-all-start = ((bf16[128,4,3072]{2,0,1:T(8,128)(2,1)}), bf16[128,4,3072]{2,0,1:T(8,128)(2,1)S(1)}, u32[]{:S(2)}, u32[]{:S(2)}) async-start(bf16[128,4,3072]{2,0,1:T(8,128)(2,1)} %pad_maximum_fusion), calls=%async_computation | async-start | bytes 6291456 | tf_op jit(solution)/shard_map/all_to_all | solution.py:179
  9.3 0.1 eq.31
  9.4 0.1 copy.43
  9.5 0.2 reduce-window.9
  9.7 0.1 reduce.1
  9.9 0.2 fusion.5
  10.0 0.1 select_reduce_fusion
  10.2 0.2 select_reduce_fusion.1
  10.4 0.1 broadcast_in_dim.64
  10.4 0.1 mul.97
  10.6 0.1 sub.65
  10.7 1.7 copy.62
  12.4 0.3 copy.61
  12.7 0.8 fusion
  13.5 0.6 reshape.205
  14.2 0.2 and_reduce_fusion
  14.4 0.2 and_reduce_fusion.1
  14.6 31.6 %all-to-all-done = bf16[128,4,3072]{2,0,1:T(8,128)(2,1)S(1)} async-done(((bf16[128,4,3072]{2,0,1:T(8,128)(2,1)}), bf16[128,4,3072]{2,0,1:T(8,128)(2,1)S(1)}, u32[]{:S(2)}, u32[]{:S(2)}) %all-to-all-start) | async-done | bytes 3145760 | tf_op jit(solution)/shard_map/all_to_all | solution.py:179
  46.2 3.3 %all-to-all-start.2 = ((f32[128,4,10]{0,2,1:T(8,128)}), f32[128,4,10]{0,2,1:T(8,128)S(1)}, u32[]{:S(2)}, u32[]{:S(2)}) async-start(f32[128,4,10]{0,2,1:T(8,128)} %reshape.205), calls=%async_computation.2 | async-start | bytes 65536 | tf_op jit(solution)/shard_map/all_to_all | solution.py:180
  49.5 0.1 mul.99.lo_ref
  49.6 0.1 sub.68.lo_ref
  49.7 0.6 reshape.202.n_ref
  50.3 0.6 convert_element_type.48.need_ref
  50.8 0.5 convert_element_type.46.need_ref
  51.4 0.5 convert_element_type.45.need_ref
  51.9 1.5 all-to-all-done.2
  53.4 1.1 broadcast_in_dim.36
  54.5 14.6 %all-to-all-start.1 = ((bf16[64,16,512]{2,1,0:T(8,128)(2,1)}), bf16[64,16,512]{2,1,0:T(8,128)(2,1)}, u32[]{:S(2)}, u32[]{:S(2)}) async-start(bf16[64,16,512]{2,1,0:T(8,128)(2,1)} %broadcast_in_dim.36), calls=%async_computation.1 | async-start | bytes 2097152 | tf_op jit(solution)/shard_map/all_to_all | solution.py:231
  69.0 0.6 broadcast_add_fusion.hi_ref
  69.6 0.6 broadcast_add_fusion.2.lo_ref
  70.3 0.6 reshape.207.d_ref
  70.9 0.8 slice.64
  71.7 3.4 %collective-permute-start = (bf16[512,512]{1,0:T(8,128)(2,1)}, bf16[512,512]{1,0:T(8,128)(2,1)}, u32[]{:S(2)}, u32[]{:S(2)}) collective-permute-start(bf16[512,512]{1,0:T(8,128)(2,1)} %slice.64), channel_id=1, source_target_pairs={{0,4},{4,8},{8,12},{12,16},{16,20},{20,24},{24,28},{28,32},{32,36}... | collective-permute-start | bytes 1572872 | tf_op jit(solution)/shard_map/ppermute | solution.py:29
  75.1 1.7 fusion.9
  76.8 0.8 fusion.8
  77.6 0.6 iota.46.hi_ref
  78.2 18.6 %shard_map.137 = (f32[512,1280]{1,0:T(8,128)}, f32[512,512]{1,0:T(8,128)}) custom-call(s32[4]{0:T(128)} %convert_element_type.45.need_ref, bf16[512,1280]{1,0:T(8,128)(2,1)} %get-tuple-element.47.q_ref, bf16[512,1280]{1,0:T(8,128)(2,1)} %get-tuple-element.46.do_ref, bf16[512,256]{1,0:T(8,128)(2,1)} %get-tuple-element.45.k_ref, ...), custom_call_target="tpu_custom_call" | custom-call | flops 3355443200 | bytes 6815744 | tf_op jit(solution)/shard_map/pallas_call | solution.py:125
  96.8 5.3 %collective-permute-done = bf16[512,512]{1,0:T(8,128)(2,1)} collective-permute-done((bf16[512,512]{1,0:T(8,128)(2,1)}, bf16[512,512]{1,0:T(8,128)(2,1)}, u32[]{:S(2)}, u32[]{:S(2)}) %collective-permute-start) | collective-permute-done | bytes 524320 | tf_op jit(solution)/shard_map/ppermute | solution.py:29
  102.1 1.9 fusion.11
  103.9 0.6 broadcast_in_dim.60.hi_ref
  104.5 18.6 %shard_map.138 = (f32[512,1280]{1,0:T(8,128)}, f32[512,512]{1,0:T(8,128)}) custom-call(s32[4]{0:T(128)} %convert_element_type.46.need_ref, bf16[512,1280]{1,0:T(8,128)(2,1)} %get-tuple-element.47.q_ref, bf16[512,1280]{1,0:T(8,128)(2,1)} %get-tuple-element.46.do_ref, bf16[512,256]{1,0:T(8,128)(2,1)} %get-tuple-element.51.k_ref, ...), custom_call_target="tpu_custom_call" | custom-call | flops 3355443200 | bytes 6815744 | tf_op jit(solution)/shard_map/pallas_call | solution.py:125
  123.2 2.8 %add.89 = f32[512,1280]{1,0:T(8,128)S(1)} add(f32[512,1280]{1,0:T(8,128)} %get-tuple-element.15, f32[512,1280]{1,0:T(8,128)} %get-tuple-element.16) | non-fusion elementwise | flops 655360 | bytes 7864320 | tf_op jit(solution)/shard_map/add | solution.py:225
  126.0 2.2 fusion.10
  128.2 15.5 %shard_map.139 = (f32[512,1280]{1,0:T(8,128)}, f32[1024,512]{1,0:T(8,128)}) custom-call(s32[8]{0:T(128)} %convert_element_type.48.need_ref, bf16[512,1280]{1,0:T(8,128)(2,1)} %get-tuple-element.47.q_ref, bf16[512,1280]{1,0:T(8,128)(2,1)} %get-tuple-element.46.do_ref, bf16[1024,256]{1,0:T(8,128)(2,1)} %get-tuple-element.49.k_ref, ...), custom_call_target="tpu_custom_call" | custom-call | flops 6710886400 | bytes 8388608 | tf_op jit(solution)/shard_map/pallas_call | solution.py:125
  143.7 9.9 %all-to-all-start.3 = ((f32[64,16,512]{2,1,0:T(8,128)}), f32[64,16,512]{2,1,0:T(8,128)}, u32[]{:S(2)}, u32[]{:S(2)}) async-start(f32[64,16,512]{2,1,0:T(8,128)} %bitcast.56), calls=%async_computation.3 | async-start | bytes 4194304 | tf_op jit(solution)/shard_map/all_to_all | solution.py:250
  153.6 1.3 convert_element_type.50
  154.9 2.9 %collective-permute-start.1 = (bf16[512,512]{1,0:T(8,128)(2,1)S(1)}, bf16[512,512]{1,0:T(8,128)(2,1)S(1)}, u32[]{:S(2)}, u32[]{:S(2)}) collective-permute-start(bf16[512,512]{1,0:T(8,128)(2,1)S(1)} %convert_element_type.50), channel_id=1, source_target_pairs={{4,0},{8,4},{12,8},{16,12},{20,16},{24,20},{28,24},{32,28},{36,32}... | collective-permute-start | bytes 1572872 | tf_op jit(solution)/shard_map/ppermute | solution.py:29
  157.8 52.6 %collective-permute-done.1 = bf16[512,512]{1,0:T(8,128)(2,1)S(1)} collective-permute-done((bf16[512,512]{1,0:T(8,128)(2,1)S(1)}, bf16[512,512]{1,0:T(8,128)(2,1)S(1)}, u32[]{:S(2)}, u32[]{:S(2)}) %collective-permute-start.1) | collective-permute-done | bytes 524320 | tf_op jit(solution)/shard_map/ppermute | solution.py:29
  210.5 2.4 %convert_add_fusion = f32[512,512]{1,0:T(8,128)} fusion(f32[512,512]{1,0:T(8,128)} %get-tuple-element.20, bf16[512,512]{1,0:T(8,128)(2,1)S(1)} %collective-permute-done.1), kind=kLoop, calls=%fused_computation.6 | loop fusion | flops 524288 | bytes 2621440 | tf_op jit(solution)/shard_map/add | solution.py:259
  212.8 2.9 %reshape.208 = f32[512,2,2,128]{3,2,1,0:T(2,128)} reshape(f32[512,512]{1,0:T(8,128)} %convert_add_fusion) | data formatting | bytes 2097152 | tf_op jit(solution)/shard_map/reshape | solution.py:259
  215.7 2.6 %slice.68 = bf16[512,2,1,128]{3,2,1,0:T(2,128)(2,1)} slice(f32[512,2,2,128]{3,2,1,0:T(2,128)} %reshape.208), slice={[0:512], [0:2], [1:2], [0:128]} | slice | bytes 524288 | tf_op jit(solution)/shard_map/slice | solution.py:263
  218.3 1.2 copy.56
  219.5 0.8 copy.48
  220.4 1.4 copy.55
  221.8 1.1 multiply_convert_fusion.1
  222.8 0.8 copy.47
  223.7 3.1 %multiply_convert_fusion = bf16[512,1280]{1,0:T(8,128)(2,1)} fusion(f32[512,1280]{1,0:T(8,128)S(1)} %add.89, f32[512,1280]{1,0:T(8,128)} %get-tuple-element.19), kind=kLoop, calls=%fused_computation.3 | loop fusion | flops 1966080 | bytes 6553600 | tf_op jit(solution)/shard_map/convert_element_type | solution.py:261
  226.8 1.7 reduce_sum.39
  228.6 0.1 fusion.1
  228.7 0.6 copy.74
  229.3 0.6 copy.75
  (37 shorter events, 0.3 us)
Async XLA Ops:
  5.5 3.9 %copy-start.6 = (s32[8,16]{1,0:T(8,128)S(1)}, s32[8,16]{1,0:T(8,128)}, u32[]{:S(2)}) copy-start(s32[8,16]{1,0:T(8,128)} %param.19) | copy-start | bytes 1540
  5.5 3.9 %copy-start.7 = (s32[128]{0:T(128)S(1)}, s32[128]{0:T(128)}, u32[]{:S(2)}) copy-start(s32[128]{0:T(128)} %param.18) | copy-start | bytes 1540
  5.5 40.7 %all-to-all-start = ((bf16[128,4,3072]{2,0,1:T(8,128)(2,1)}), bf16[128,4,3072]{2,0,1:T(8,128)(2,1)S(1)}, u32[]{:S(2)}, u32[]{:S(2)}) async-start(bf16[128,4,3072]{2,0,1:T(8,128)(2,1)} %pad_maximum_fusion), calls=%async_computation | async-start | bytes 6291456 | tf_op jit(solution)/shard_map/all_to_all | solution.py:179
  10.7 1.7 copy-start
  12.4 37.1 %copy-start.4 = (bf16[16,256]{1,0:T(8,128)(2,1)S(1)}, bf16[16,256]{1,0:T(8,128)(2,1)}, u32[]{:S(2)}) copy-start(bf16[16,256]{1,0:T(8,128)(2,1)} %param.17) | copy-start | bytes 24580
  12.4 37.1 %copy-start.5 = (bf16[16,256]{1,0:T(8,128)(2,1)S(1)}, bf16[16,256]{1,0:T(8,128)(2,1)}, u32[]{:S(2)}) copy-start(bf16[16,256]{1,0:T(8,128)(2,1)} %param.16) | copy-start | bytes 24580
  12.4 37.3 %copy-start.1 = (f32[10,512]{1,0:T(8,128)S(1)}, f32[10,512]{1,0:T(8,128)}, u32[]{:S(2)}) copy-start(f32[10,512]{1,0:T(8,128)} %param.15) | copy-start | bytes 61444
  46.2 7.2 %all-to-all-start.2 = ((f32[128,4,10]{0,2,1:T(8,128)}), f32[128,4,10]{0,2,1:T(8,128)S(1)}, u32[]{:S(2)}, u32[]{:S(2)}) async-start(f32[128,4,10]{0,2,1:T(8,128)} %reshape.205), calls=%async_computation.2 | async-start | bytes 65536 | tf_op jit(solution)/shard_map/all_to_all | solution.py:180
  49.6 27.2 %copy-start.2 = (s32[1,512]{1,0:T(1,128)}, s32[1,512]{1,0:T(1,128)S(1)}, u32[]{:S(2)}) copy-start(s32[1,512]{1,0:T(1,128)S(1)} %mul.99.lo_ref) | copy-start | bytes 6148
  49.7 27.1 %copy-start.3 = (s32[1,512]{1,0:T(1,128)}, s32[1,512]{1,0:T(1,128)S(1)}, u32[]{:S(2)}) copy-start(s32[1,512]{1,0:T(1,128)S(1)} %sub.68.lo_ref) | copy-start | bytes 6148
  54.5 71.5 %all-to-all-start.1 = ((bf16[64,16,512]{2,1,0:T(8,128)(2,1)}), bf16[64,16,512]{2,1,0:T(8,128)(2,1)}, u32[]{:S(2)}, u32[]{:S(2)}) async-start(bf16[64,16,512]{2,1,0:T(8,128)(2,1)} %broadcast_in_dim.36), calls=%async_computation.1 | async-start | bytes 2097152 | tf_op jit(solution)/shard_map/all_to_all | solution.py:231
  71.7 30.4 %collective-permute-start = (bf16[512,512]{1,0:T(8,128)(2,1)}, bf16[512,512]{1,0:T(8,128)(2,1)}, u32[]{:S(2)}, u32[]{:S(2)}) collective-permute-start(bf16[512,512]{1,0:T(8,128)(2,1)} %slice.64), channel_id=1, source_target_pairs={{0,4},{4,8},{8,12},{12,16},{16,20},{20,24},{24,28},{28,32},{32,36}... | collective-permute-start | bytes 1572872 | tf_op jit(solution)/shard_map/ppermute | solution.py:29
  143.7 83.1 %all-to-all-start.3 = ((f32[64,16,512]{2,1,0:T(8,128)}), f32[64,16,512]{2,1,0:T(8,128)}, u32[]{:S(2)}, u32[]{:S(2)}) async-start(f32[64,16,512]{2,1,0:T(8,128)} %bitcast.56), calls=%async_computation.3 | async-start | bytes 4194304 | tf_op jit(solution)/shard_map/all_to_all | solution.py:250
  154.9 55.6 %collective-permute-start.1 = (bf16[512,512]{1,0:T(8,128)(2,1)S(1)}, bf16[512,512]{1,0:T(8,128)(2,1)S(1)}, u32[]{:S(2)}, u32[]{:S(2)}) collective-permute-start(bf16[512,512]{1,0:T(8,128)(2,1)S(1)} %convert_element_type.50), channel_id=1, source_target_pairs={{4,0},{8,4},{12,8},{16,12},{20,16},{24,20},{28,24},{32,28},{36,32}... | collective-permute-start | bytes 1572872 | tf_op jit(solution)/shard_map/ppermute | solution.py:29
  215.7 4.7 %slice-start = ((f32[512,2,2,128]{3,2,1,0:T(2,128)}), f32[512,2,1,128]{3,2,1,0:T(1,128)S(1)}, s32[]{:S(2)}) async-start(f32[512,2,2,128]{3,2,1,0:T(2,128)} %reshape.208), calls=%async_computation.4 | async-start | bytes 1048576 | tf_op jit(solution)/shard_map/slice | solution.py:262

commit v8 on v7

--- a/solution.py
+++ b/solution.py
@@ -247,6 +247,7 @@
             prompt_lo.reshape(1, tokens),
             (prompt_lo + PL - 1).reshape(1, tokens),
         )
+        pgrad, back = lax.optimization_barrier((pgrad, back))
         pgrad = lax.all_to_all(
             pgrad.reshape(nctx, -1, pgrad.shape[1]),
             names,

time: 231 us -> 215 us (0.931)
  waiting for transfers between devices: 91 us -> 72.7 us
  starting transfers between devices: 37.8 us -> 46.2 us
  Pallas kernels: 52.7 us -> 45.3 us
    ppermute x2, waiting for transfers between devices: 57.9 us -> 6.18 us  [shifted(): return lax.ppermute(array, axes, pairs)]
    all_to_all x1, waiting for transfers between devices: 0.01 us -> 33.5 us  [shards(): lax.all_to_all(pgrad.reshape(nctx, -1, pgrad.shape[1]), names, split_axis...]
    all_to_all x1, starting transfers between devices: 9.88 us -> 19.3 us  [shards(): lax.all_to_all(pgrad.reshape(nctx, -1, pgrad.shape[1]), names, split_axis...]
    pallas_call x3, Pallas kernels: 52.7 us -> 45.3 us  [tile_kernel(): pl.pallas_call(tile_body, grid_spec=grid_spec, out_shape=[jax.ShapeDtypeS...]
  transfers between devices with their start and end apart: 6 -> 6, of which waited for: 4 -> 5; matrix products, arithmetic and copies ran while one was open for 16% -> 18% of each run, Pallas kernels for 16% -> 21%
where the time goes in v8:
time: 215 us; the launch traced here: 214 us
  waiting for transfers between devices  72.7 us (34%)
  starting transfers between devices  46.2 us (21%)
  Pallas kernels  45.3 us (21%)
  local copies, waits for them, and re-layouts  28.3 us (13%)
  other arithmetic  20.1 us (9%)
    pallas_call x3, Pallas kernels, tile_kernel(): pl.pallas_call(tile_body, grid_spec=grid_spec, out_shape=[jax.ShapeDtypeS...  45.3 us
    all_to_all x1, waiting for transfers between devices, shards(): lax.all_to_all(pgrad.reshape(nctx, -1, pgrad.shape[1]), names, split_axis...  33.5 us
    all_to_all x1, waiting for transfers between devices, shards(): lax.all_to_all(packed, 'head', split_axis=1, concat_axis=0, tiled=True)  31.6 us
    all_to_all x1, starting transfers between devices, shards(): lax.all_to_all(pgrad.reshape(nctx, -1, pgrad.shape[1]), names, split_axis...  19.3 us
    all_to_all x1, starting transfers between devices, shards(): lax.all_to_all(jnp.broadcast_to(pkv[None], (nctx,) + pkv.shape), names, s...  14.6 us
    unnamed x26, local copies, waits for them, and re-layouts  7.5 us
    ppermute x2, waiting for transfers between devices, shifted(): return lax.ppermute(array, axes, pairs)  6.18 us
    ppermute x2, starting transfers between devices, shifted(): return lax.ppermute(array, axes, pairs)  5.27 us
  transfers between devices with their start and end apart: 6, of which 5 were waited for; matrix products, arithmetic and copies ran while one was open for 18% of the time, Pallas kernels for 21%

profile of v8, /device:TPU:22, one launch (start us, length us, event | category | flops | bytes accessed | tf_op | source)
XLA Modules:
  0.0 213.5 jit_solution(15512293119564515021)
XLA Ops:
  0.6 1.1 copy_bitcast_fusion.2
  1.7 1.9 copy_bitcast_fusion
  3.6 1.9 pad_maximum_fusion
  5.5 3.8 %all-to-all-start = ((bf16[128,4,3072]{2,0,1:T(8,128)(2,1)}), bf16[128,4,3072]{2,0,1:T(8,128)(2,1)S(1)}, u32[]{:S(2)}, u32[]{:S(2)}) async-start(bf16[128,4,3072]{2,0,1:T(8,128)(2,1)} %pad_maximum_fusion), calls=%async_computation | async-start | bytes 6291456 | tf_op jit(solution)/shard_map/all_to_all | solution.py:179
  9.3 0.1 eq.31
  9.4 0.1 copy.43
  9.5 0.2 reduce-window.9
  9.7 0.1 reduce.1
  9.9 0.2 fusion.5
  10.0 0.1 select_reduce_fusion
  10.2 0.2 select_reduce_fusion.1
  10.4 0.1 mul.97
  10.6 0.1 sub.65
  10.7 1.7 copy.62
  12.4 0.3 copy.61
  12.7 0.8 fusion
  13.5 0.6 reshape.205
  14.2 0.2 and_reduce_fusion
  14.4 0.2 and_reduce_fusion.1
  14.6 31.6 %all-to-all-done = bf16[128,4,3072]{2,0,1:T(8,128)(2,1)S(1)} async-done(((bf16[128,4,3072]{2,0,1:T(8,128)(2,1)}), bf16[128,4,3072]{2,0,1:T(8,128)(2,1)S(1)}, u32[]{:S(2)}, u32[]{:S(2)}) %all-to-all-start) | async-done | bytes 3145760 | tf_op jit(solution)/shard_map/all_to_all | solution.py:179
  46.2 3.3 %all-to-all-start.2 = ((f32[128,4,10]{0,2,1:T(8,128)}), f32[128,4,10]{0,2,1:T(8,128)S(1)}, u32[]{:S(2)}, u32[]{:S(2)}) async-start(f32[128,4,10]{0,2,1:T(8,128)} %reshape.205), calls=%async_computation.2 | async-start | bytes 65536 | tf_op jit(solution)/shard_map/all_to_all | solution.py:180
  49.5 0.1 mul.99.lo_ref
  49.6 0.1 sub.68.lo_ref
  49.7 0.6 reshape.202.n_ref
  50.3 0.6 convert_element_type.48.need_ref
  50.8 0.6 convert_element_type.46.need_ref
  51.4 0.6 convert_element_type.45.need_ref
  52.0 1.4 all-to-all-done.2
  53.4 1.1 broadcast_in_dim.36
  54.5 14.6 %all-to-all-start.1 = ((bf16[64,16,512]{2,1,0:T(8,128)(2,1)}), bf16[64,16,512]{2,1,0:T(8,128)(2,1)}, u32[]{:S(2)}, u32[]{:S(2)}) async-start(bf16[64,16,512]{2,1,0:T(8,128)(2,1)} %broadcast_in_dim.36), calls=%async_computation.1 | async-start | bytes 2097152 | tf_op jit(solution)/shard_map/all_to_all | solution.py:231
  69.0 0.6 broadcast_add_fusion.hi_ref
  69.6 0.6 broadcast_add_fusion.2.lo_ref
  70.3 0.6 reshape.207.d_ref
  70.9 0.8 slice.64
  71.7 3.4 %collective-permute-start = (bf16[512,512]{1,0:T(8,128)(2,1)}, bf16[512,512]{1,0:T(8,128)(2,1)}, u32[]{:S(2)}, u32[]{:S(2)}) collective-permute-start(bf16[512,512]{1,0:T(8,128)(2,1)} %slice.64), channel_id=1, source_target_pairs={{0,4},{4,8},{8,12},{12,16},{16,20},{20,24},{24,28},{28,32},{32,36}... | collective-permute-start | bytes 1572872 | tf_op jit(solution)/shard_map/ppermute | solution.py:29
  75.1 1.7 fusion.9
  76.8 0.8 fusion.8
  77.6 0.6 iota.46.hi_ref
  78.2 18.7 %shard_map.137 = (f32[512,1280]{1,0:T(8,128)}, f32[512,512]{1,0:T(8,128)}) custom-call(s32[4]{0:T(128)} %convert_element_type.45.need_ref, bf16[512,1280]{1,0:T(8,128)(2,1)} %get-tuple-element.51.q_ref, bf16[512,1280]{1,0:T(8,128)(2,1)} %get-tuple-element.50.do_ref, bf16[512,256]{1,0:T(8,128)(2,1)} %get-tuple-element.49.k_ref, ...), custom_call_target="tpu_custom_call" | custom-call | flops 3355443200 | bytes 6815744 | tf_op jit(solution)/shard_map/pallas_call | solution.py:125
  96.9 5.2 %collective-permute-done = bf16[512,512]{1,0:T(8,128)(2,1)} collective-permute-done((bf16[512,512]{1,0:T(8,128)(2,1)}, bf16[512,512]{1,0:T(8,128)(2,1)}, u32[]{:S(2)}, u32[]{:S(2)}) %collective-permute-start) | collective-permute-done | bytes 524320 | tf_op jit(solution)/shard_map/ppermute | solution.py:29
  102.1 1.9 fusion.11
  103.9 0.6 broadcast_in_dim.60.hi_ref
  104.5 11.2 %shard_map.138 = (f32[512,1280]{1,0:T(8,128)}, f32[512,512]{1,0:T(8,128)}) custom-call(s32[4]{0:T(128)} %convert_element_type.46.need_ref, bf16[512,1280]{1,0:T(8,128)(2,1)} %get-tuple-element.51.q_ref, bf16[512,1280]{1,0:T(8,128)(2,1)} %get-tuple-element.50.do_ref, bf16[512,256]{1,0:T(8,128)(2,1)} %get-tuple-element.55.k_ref, ...), custom_call_target="tpu_custom_call" | custom-call | flops 3355443200 | bytes 6815744 | tf_op jit(solution)/shard_map/pallas_call | solution.py:125
  115.7 2.1 convert_element_type.50
  117.8 1.9 collective-permute-start.1
  119.7 2.8 %add.89 = f32[512,1280]{1,0:T(8,128)S(1)} add(f32[512,1280]{1,0:T(8,128)} %get-tuple-element.17, f32[512,1280]{1,0:T(8,128)} %get-tuple-element.18) | non-fusion elementwise | flops 655360 | bytes 7864320 | tf_op jit(solution)/shard_map/add | solution.py:225
  122.6 2.3 %fusion.10 = (bf16[1024,256]{1,0:T(8,128)(2,1)}, bf16[1024,256]{1,0:T(8,128)(2,1)}) fusion(bf16[1024,512]{1,0:T(8,128)(2,1)} %bitcast.3), kind=kLoop, calls=%fused_computation.51 | loop fusion | bytes 2097152 | tf_op jit(solution)/shard_map/slice | solution.py:244
  124.9 15.4 %shard_map.139 = (f32[512,1280]{1,0:T(8,128)}, f32[1024,512]{1,0:T(8,128)}) custom-call(s32[8]{0:T(128)} %convert_element_type.48.need_ref, bf16[512,1280]{1,0:T(8,128)(2,1)} %get-tuple-element.51.q_ref, bf16[512,1280]{1,0:T(8,128)(2,1)} %get-tuple-element.50.do_ref, bf16[1024,256]{1,0:T(8,128)(2,1)} %get-tuple-element.53.k_ref, ...), custom_call_target="tpu_custom_call" | custom-call | flops 6710886400 | bytes 8388608 | tf_op jit(solution)/shard_map/pallas_call | solution.py:125
  140.3 1.0 collective-permute-done.1
  141.3 19.3 %all-to-all-start.3 = ((f32[64,16,512]{2,1,0:T(8,128)}), f32[64,16,512]{2,1,0:T(8,128)}, u32[]{:S(2)}, u32[]{:S(2)}) async-start(f32[64,16,512]{2,1,0:T(8,128)} %bitcast.56), calls=%async_computation.3 | async-start | bytes 4194304 | tf_op jit(solution)/shard_map/all_to_all | solution.py:251
  160.6 2.4 %convert_add_fusion = f32[512,512]{1,0:T(8,128)} fusion(f32[512,512]{1,0:T(8,128)} %get-tuple-element.22, bf16[512,512]{1,0:T(8,128)(2,1)S(1)} %collective-permute-done.1), kind=kLoop, calls=%fused_computation.6 | loop fusion | flops 524288 | bytes 2621440 | tf_op jit(solution)/shard_map/add | solution.py:260
  162.9 2.9 %reshape.208 = f32[512,2,2,128]{3,2,1,0:T(2,128)} reshape(f32[512,512]{1,0:T(8,128)} %convert_add_fusion) | data formatting | bytes 2097152 | tf_op jit(solution)/shard_map/reshape | solution.py:260
  165.8 2.6 %slice.68 = bf16[512,2,1,128]{3,2,1,0:T(2,128)(2,1)} slice(f32[512,2,2,128]{3,2,1,0:T(2,128)} %reshape.208), slice={[0:512], [0:2], [1:2], [0:128]} | slice | bytes 524288 | tf_op jit(solution)/shard_map/slice | solution.py:264
  168.4 1.2 copy.56
  169.7 0.8 copy.48
  170.5 1.4 copy.55
  171.9 1.1 multiply_convert_fusion.1
  173.0 0.8 copy.47
  173.8 3.1 %multiply_convert_fusion = bf16[512,1280]{1,0:T(8,128)(2,1)} fusion(f32[512,1280]{1,0:T(8,128)S(1)} %add.89, f32[512,1280]{1,0:T(8,128)} %get-tuple-element.21), kind=kLoop, calls=%fused_computation.3 | loop fusion | flops 1966080 | bytes 6553600 | tf_op jit(solution)/shard_map/convert_element_type | solution.py:262
  176.9 33.5 %all-to-all-done.3 = f32[64,16,512]{2,1,0:T(8,128)} async-done(((f32[64,16,512]{2,1,0:T(8,128)}), f32[64,16,512]{2,1,0:T(8,128)}, u32[]{:S(2)}, u32[]{:S(2)}) %all-to-all-start.3) | async-done | bytes 2097184 | tf_op jit(solution)/shard_map/all_to_all | solution.py:251
  210.4 1.7 reduce_sum.39
  212.2 0.1 fusion.1
  212.3 0.6 copy.74
  212.9 0.6 copy.75
  (37 shorter events, 0.4 us)
Async XLA Ops:
  5.5 3.9 %copy-start.6 = (s32[8,16]{1,0:T(8,128)S(1)}, s32[8,16]{1,0:T(8,128)}, u32[]{:S(2)}) copy-start(s32[8,16]{1,0:T(8,128)} %param.19) | copy-start | bytes 1540
  5.5 3.9 %copy-start.7 = (s32[128]{0:T(128)S(1)}, s32[128]{0:T(128)}, u32[]{:S(2)}) copy-start(s32[128]{0:T(128)} %param.18) | copy-start | bytes 1540
  5.5 40.7 %all-to-all-start = ((bf16[128,4,3072]{2,0,1:T(8,128)(2,1)}), bf16[128,4,3072]{2,0,1:T(8,128)(2,1)S(1)}, u32[]{:S(2)}, u32[]{:S(2)}) async-start(bf16[128,4,3072]{2,0,1:T(8,128)(2,1)} %pad_maximum_fusion), calls=%async_computation | async-start | bytes 6291456 | tf_op jit(solution)/shard_map/all_to_all | solution.py:179
  10.7 1.7 copy-start
  12.4 37.1 %copy-start.4 = (bf16[16,256]{1,0:T(8,128)(2,1)S(1)}, bf16[16,256]{1,0:T(8,128)(2,1)}, u32[]{:S(2)}) copy-start(bf16[16,256]{1,0:T(8,128)(2,1)} %param.17) | copy-start | bytes 24580
  12.4 37.1 %copy-start.5 = (bf16[16,256]{1,0:T(8,128)(2,1)S(1)}, bf16[16,256]{1,0:T(8,128)(2,1)}, u32[]{:S(2)}) copy-start(bf16[16,256]{1,0:T(8,128)(2,1)} %param.16) | copy-start | bytes 24580
  12.4 37.3 %copy-start.1 = (f32[10,512]{1,0:T(8,128)S(1)}, f32[10,512]{1,0:T(8,128)}, u32[]{:S(2)}) copy-start(f32[10,512]{1,0:T(8,128)} %param.15) | copy-start | bytes 61444
  46.2 7.2 %all-to-all-start.2 = ((f32[128,4,10]{0,2,1:T(8,128)}), f32[128,4,10]{0,2,1:T(8,128)S(1)}, u32[]{:S(2)}, u32[]{:S(2)}) async-start(f32[128,4,10]{0,2,1:T(8,128)} %reshape.205), calls=%async_computation.2 | async-start | bytes 65536 | tf_op jit(solution)/shard_map/all_to_all | solution.py:180
  49.6 27.2 %copy-start.2 = (s32[1,512]{1,0:T(1,128)}, s32[1,512]{1,0:T(1,128)S(1)}, u32[]{:S(2)}) copy-start(s32[1,512]{1,0:T(1,128)S(1)} %mul.99.lo_ref) | copy-start | bytes 6148
  49.7 27.1 %copy-start.3 = (s32[1,512]{1,0:T(1,128)}, s32[1,512]{1,0:T(1,128)S(1)}, u32[]{:S(2)}) copy-start(s32[1,512]{1,0:T(1,128)S(1)} %sub.68.lo_ref) | copy-start | bytes 6148
  54.5 68.1 %all-to-all-start.1 = ((bf16[64,16,512]{2,1,0:T(8,128)(2,1)}), bf16[64,16,512]{2,1,0:T(8,128)(2,1)}, u32[]{:S(2)}, u32[]{:S(2)}) async-start(bf16[64,16,512]{2,1,0:T(8,128)(2,1)} %broadcast_in_dim.36), calls=%async_computation.1 | async-start | bytes 2097152 | tf_op jit(solution)/shard_map/all_to_all | solution.py:231
  71.7 30.4 %collective-permute-start = (bf16[512,512]{1,0:T(8,128)(2,1)}, bf16[512,512]{1,0:T(8,128)(2,1)}, u32[]{:S(2)}, u32[]{:S(2)}) collective-permute-start(bf16[512,512]{1,0:T(8,128)(2,1)} %slice.64), channel_id=1, source_target_pairs={{0,4},{4,8},{8,12},{12,16},{16,20},{20,24},{24,28},{28,32},{32,36}... | collective-permute-start | bytes 1572872 | tf_op jit(solution)/shard_map/ppermute | solution.py:29
  117.8 23.5 %collective-permute-start.1 = (bf16[512,512]{1,0:T(8,128)(2,1)}, bf16[512,512]{1,0:T(8,128)(2,1)S(1)}, u32[]{:S(2)}, u32[]{:S(2)}) collective-permute-start(bf16[512,512]{1,0:T(8,128)(2,1)} %convert_element_type.50), channel_id=1, source_target_pairs={{4,0},{8,4},{12,8},{16,12},{20,16},{24,20},{28,24},{32,28},{36,32}... | collective-permute-start | bytes 1572872 | tf_op jit(solution)/shard_map/ppermute | solution.py:29
  141.3 69.2 %all-to-all-start.3 = ((f32[64,16,512]{2,1,0:T(8,128)}), f32[64,16,512]{2,1,0:T(8,128)}, u32[]{:S(2)}, u32[]{:S(2)}) async-start(f32[64,16,512]{2,1,0:T(8,128)} %bitcast.56), calls=%async_computation.3 | async-start | bytes 4194304 | tf_op jit(solution)/shard_map/all_to_all | solution.py:251
  165.8 4.7 %slice-start = ((f32[512,2,2,128]{3,2,1,0:T(2,128)}), f32[512,2,1,128]{3,2,1,0:T(1,128)S(1)}, s32[]{:S(2)}) async-start(f32[512,2,2,128]{3,2,1,0:T(2,128)} %reshape.208), calls=%async_computation.4 | async-start | bytes 1048576 | tf_op jit(solution)/shard_map/slice | solution.py:263

commit v9 on v8

--- a/solution.py
+++ b/solution.py
@@ -249,12 +249,12 @@
         )
         pgrad, back = lax.optimization_barrier((pgrad, back))
         pgrad = lax.all_to_all(
-            pgrad.reshape(nctx, -1, pgrad.shape[1]),
+            pgrad.astype(bf16).reshape(nctx, -1, pgrad.shape[1]),
             names,
             split_axis=0,
             concat_axis=0,
             tiled=True,
-        ).sum(axis=0)
+        ).astype(f32).sum(axis=0)
         pgrad = pgrad.reshape(-1, kvh, 2, HD)
 
         kv_grad = (dkv + back.astype(f32)).reshape(tokens, kvh, 2, HD)

time: 215 us -> 194 us (0.902)
  waiting for transfers between devices: 72.7 us -> 48.8 us
  starting transfers between devices: 46.2 us -> 41.9 us
  Pallas kernels: 45.3 us -> 48.9 us
  other arithmetic: 20.1 us -> 22.4 us
    all_to_all x1, waiting for transfers between devices: 33.5 us -> 10.5 us  [shards(): lax.all_to_all(pgrad.astype(bf16).reshape(nctx, -1, pgrad.shape[1]), name...]
    all_to_all x1, starting transfers between devices: 19.3 us -> 15 us  [shards(): lax.all_to_all(pgrad.astype(bf16).reshape(nctx, -1, pgrad.shape[1]), name...]
    pallas_call x3, Pallas kernels: 45.3 us -> 48.9 us  [tile_kernel(): pl.pallas_call(tile_body, grid_spec=grid_spec, out_shape=[jax.ShapeDtypeS...]
    convert_element_type x0 -> x1, other arithmetic: none -> 2.74 us  [shards(): pgrad.astype(bf16).reshape(nctx, -1, pgrad.shape[1])]
  transfers between devices with their start and end apart: 6 -> 6, of which waited for: 5 -> 4; matrix products, arithmetic and copies ran while one was open for 18% -> 21% of each run, Pallas kernels for 21% -> 26%
where the time goes in v9:
time: 194 us; the launch traced here: 191 us
  Pallas kernels  48.9 us (25%)
  waiting for transfers between devices  48.8 us (25%)
  starting transfers between devices  41.9 us (22%)
  local copies, waits for them, and re-layouts  28.4 us (15%)
  other arithmetic  22.4 us (12%)
    pallas_call x3, Pallas kernels, tile_kernel(): pl.pallas_call(tile_body, grid_spec=grid_spec, out_shape=[jax.ShapeDtypeS...  48.9 us
    all_to_all x1, waiting for transfers between devices, shards(): lax.all_to_all(packed, 'head', split_axis=1, concat_axis=0, tiled=True)  31.6 us
    all_to_all x1, starting transfers between devices, shards(): lax.all_to_all(pgrad.astype(bf16).reshape(nctx, -1, pgrad.shape[1]), name...  15 us
    all_to_all x1, starting transfers between devices, shards(): lax.all_to_all(jnp.broadcast_to(pkv[None], (nctx,) + pkv.shape), names, s...  14.6 us
    all_to_all x1, waiting for transfers between devices, shards(): lax.all_to_all(pgrad.astype(bf16).reshape(nctx, -1, pgrad.shape[1]), name...  10.5 us
    unnamed x26, local copies, waits for them, and re-layouts  7.5 us
    ppermute x2, starting transfers between devices, shifted(): return lax.ppermute(array, axes, pairs)  5.27 us
    ppermute x2, waiting for transfers between devices, shifted(): return lax.ppermute(array, axes, pairs)  5.24 us
  transfers between devices with their start and end apart: 6, of which 4 were waited for; matrix products, arithmetic and copies ran while one was open for 21% of the time, Pallas kernels for 26%

profile of v9, /device:TPU:22, one launch (start us, length us, event | category | flops | bytes accessed | tf_op | source)
XLA Modules:
  0.0 191.4 jit_solution(10146544268535758520)
XLA Ops:
  0.6 1.1 copy_bitcast_fusion.2
  1.7 1.9 copy_bitcast_fusion
  3.6 1.9 pad_maximum_fusion
  5.5 3.8 %all-to-all-start = ((bf16[128,4,3072]{2,0,1:T(8,128)(2,1)}), bf16[128,4,3072]{2,0,1:T(8,128)(2,1)S(1)}, u32[]{:S(2)}, u32[]{:S(2)}) async-start(bf16[128,4,3072]{2,0,1:T(8,128)(2,1)} %pad_maximum_fusion), calls=%async_computation | async-start | bytes 6291456 | tf_op jit(solution)/shard_map/all_to_all | solution.py:179
  9.3 0.1 eq.31
  9.4 0.1 copy.43
  9.5 0.2 reduce-window.9
  9.7 0.1 reduce.1
  9.9 0.2 fusion.5
  10.0 0.1 select_reduce_fusion
  10.2 0.2 select_reduce_fusion.1
  10.4 0.1 mul.97
  10.6 0.1 sub.65
  10.7 1.7 copy.62
  12.4 0.3 copy.61
  12.7 0.8 fusion
  13.5 0.6 reshape.205
  14.2 0.2 and_reduce_fusion
  14.4 0.2 and_reduce_fusion.1
  14.6 31.6 %all-to-all-done = bf16[128,4,3072]{2,0,1:T(8,128)(2,1)S(1)} async-done(((bf16[128,4,3072]{2,0,1:T(8,128)(2,1)}), bf16[128,4,3072]{2,0,1:T(8,128)(2,1)S(1)}, u32[]{:S(2)}, u32[]{:S(2)}) %all-to-all-start) | async-done | bytes 3145760 | tf_op jit(solution)/shard_map/all_to_all | solution.py:179
  46.2 3.3 %all-to-all-start.2 = ((f32[128,4,10]{0,2,1:T(8,128)}), f32[128,4,10]{0,2,1:T(8,128)S(1)}, u32[]{:S(2)}, u32[]{:S(2)}) async-start(f32[128,4,10]{0,2,1:T(8,128)} %reshape.205), calls=%async_computation.2 | async-start | bytes 65536 | tf_op jit(solution)/shard_map/all_to_all | solution.py:180
  49.5 0.1 mul.99.lo_ref
  49.6 0.1 sub.68.lo_ref
  49.7 0.6 reshape.202.n_ref
  50.3 0.5 convert_element_type.54.need_ref
  50.8 0.6 convert_element_type.52.need_ref
  51.4 0.5 convert_element_type.51.need_ref
  51.9 1.5 all-to-all-done.2
  53.4 1.2 broadcast_in_dim.36
  54.6 14.6 %all-to-all-start.1 = ((bf16[64,16,512]{2,1,0:T(8,128)(2,1)}), bf16[64,16,512]{2,1,0:T(8,128)(2,1)}, u32[]{:S(2)}, u32[]{:S(2)}) async-start(bf16[64,16,512]{2,1,0:T(8,128)(2,1)} %broadcast_in_dim.36), calls=%async_computation.1 | async-start | bytes 2097152 | tf_op jit(solution)/shard_map/all_to_all | solution.py:231
  69.1 0.6 broadcast_add_fusion.hi_ref
  69.7 0.6 broadcast_add_fusion.2.lo_ref
  70.3 0.6 reshape.207.d_ref
  70.9 0.8 slice.64
  71.8 3.4 %collective-permute-start = (bf16[512,512]{1,0:T(8,128)(2,1)}, bf16[512,512]{1,0:T(8,128)(2,1)}, u32[]{:S(2)}, u32[]{:S(2)}) collective-permute-start(bf16[512,512]{1,0:T(8,128)(2,1)} %slice.64), channel_id=1, source_target_pairs={{0,4},{4,8},{8,12},{12,16},{16,20},{20,24},{24,28},{28,32},{32,36}... | collective-permute-start | bytes 1572872 | tf_op jit(solution)/shard_map/ppermute | solution.py:29
  75.2 1.7 fusion.9
  76.9 0.8 fusion.8
  77.7 0.6 iota.46.hi_ref
  78.3 18.6 %shard_map.137 = (f32[512,1280]{1,0:T(8,128)}, f32[512,512]{1,0:T(8,128)}) custom-call(s32[4]{0:T(128)} %convert_element_type.51.need_ref, bf16[512,1280]{1,0:T(8,128)(2,1)} %get-tuple-element.51.q_ref, bf16[512,1280]{1,0:T(8,128)(2,1)} %get-tuple-element.50.do_ref, bf16[512,256]{1,0:T(8,128)(2,1)} %get-tuple-element.49.k_ref, ...), custom_call_target="tpu_custom_call" | custom-call | flops 3355443200 | bytes 6815744 | tf_op jit(solution)/shard_map/pallas_call | solution.py:125
  96.9 5.2 %collective-permute-done = bf16[512,512]{1,0:T(8,128)(2,1)} collective-permute-done((bf16[512,512]{1,0:T(8,128)(2,1)}, bf16[512,512]{1,0:T(8,128)(2,1)}, u32[]{:S(2)}, u32[]{:S(2)}) %collective-permute-start) | collective-permute-done | bytes 524320 | tf_op jit(solution)/shard_map/ppermute | solution.py:29
  102.2 1.9 fusion.11
  104.0 0.6 broadcast_in_dim.60.hi_ref
  104.6 14.9 %shard_map.138 = (f32[512,1280]{1,0:T(8,128)}, f32[512,512]{1,0:T(8,128)}) custom-call(s32[4]{0:T(128)} %convert_element_type.52.need_ref, bf16[512,1280]{1,0:T(8,128)(2,1)} %get-tuple-element.51.q_ref, bf16[512,1280]{1,0:T(8,128)(2,1)} %get-tuple-element.50.do_ref, bf16[512,256]{1,0:T(8,128)(2,1)} %get-tuple-element.55.k_ref, ...), custom_call_target="tpu_custom_call" | custom-call | flops 3355443200 | bytes 6815744 | tf_op jit(solution)/shard_map/pallas_call | solution.py:125
  119.5 2.1 %convert_element_type.56 = bf16[512,512]{1,0:T(8,128)(2,1)} convert(f32[512,512]{1,0:T(8,128)} %get-tuple-element.24) | non-fusion elementwise | flops 262144 | bytes 1572864 | tf_op jit(solution)/shard_map/convert_element_type | solution.py:224
  121.5 1.9 collective-permute-start.1
  123.5 2.8 %add.89 = f32[512,1280]{1,0:T(8,128)S(1)} add(f32[512,1280]{1,0:T(8,128)} %get-tuple-element.17, f32[512,1280]{1,0:T(8,128)} %get-tuple-element.18) | non-fusion elementwise | flops 655360 | bytes 7864320 | tf_op jit(solution)/shard_map/add | solution.py:225
  126.3 2.3 %fusion.10 = (bf16[1024,256]{1,0:T(8,128)(2,1)}, bf16[1024,256]{1,0:T(8,128)(2,1)}) fusion(bf16[1024,512]{1,0:T(8,128)(2,1)} %bitcast.3), kind=kLoop, calls=%fused_computation.52 | loop fusion | bytes 2097152 | tf_op jit(solution)/shard_map/slice | solution.py:244
  128.6 15.4 %shard_map.139 = (f32[512,1280]{1,0:T(8,128)}, f32[1024,512]{1,0:T(8,128)}) custom-call(s32[8]{0:T(128)} %convert_element_type.54.need_ref, bf16[512,1280]{1,0:T(8,128)(2,1)} %get-tuple-element.51.q_ref, bf16[512,1280]{1,0:T(8,128)(2,1)} %get-tuple-element.50.do_ref, bf16[1024,256]{1,0:T(8,128)(2,1)} %get-tuple-element.53.k_ref, ...), custom_call_target="tpu_custom_call" | custom-call | flops 6710886400 | bytes 8388608 | tf_op jit(solution)/shard_map/pallas_call | solution.py:125
  144.1 2.7 %convert_element_type.61 = bf16[1024,512]{1,0:T(8,128)(2,1)} convert(f32[1024,512]{1,0:T(8,128)} %get-tuple-element.26) | non-fusion elementwise | flops 524288 | bytes 3145728 | tf_op jit(solution)/shard_map/convert_element_type | solution.py:252
  146.8 15.0 %all-to-all-start.3 = ((bf16[64,16,512]{2,1,0:T(8,128)(2,1)}), bf16[64,16,512]{2,1,0:T(8,128)(2,1)}, u32[]{:S(2)}, u32[]{:S(2)}) async-start(bf16[64,16,512]{2,1,0:T(8,128)(2,1)} %bitcast.56), calls=%async_computation.3 | async-start | bytes 2097152 | tf_op jit(solution)/shard_map/all_to_all | solution.py:251
  161.8 2.4 %convert_add_fusion = f32[512,512]{1,0:T(8,128)} fusion(f32[512,512]{1,0:T(8,128)} %get-tuple-element.22, bf16[512,512]{1,0:T(8,128)(2,1)S(1)} %collective-permute-done.1), kind=kLoop, calls=%fused_computation.7 | loop fusion | flops 524288 | bytes 2621440 | tf_op jit(solution)/shard_map/add | solution.py:260
  164.2 2.8 %reshape.208 = f32[512,2,2,128]{3,2,1,0:T(2,128)} reshape(f32[512,512]{1,0:T(8,128)} %convert_add_fusion) | data formatting | bytes 2097152 | tf_op jit(solution)/shard_map/reshape | solution.py:260
  167.0 2.6 %slice.68 = bf16[512,2,1,128]{3,2,1,0:T(2,128)(2,1)} slice(f32[512,2,2,128]{3,2,1,0:T(2,128)} %reshape.208), slice={[0:512], [0:2], [1:2], [0:128]} | slice | bytes 524288 | tf_op jit(solution)/shard_map/slice | solution.py:264
  169.7 1.2 copy.56
  170.9 0.8 copy.48
  171.8 1.4 copy.55
  173.1 1.1 multiply_convert_fusion.1
  174.2 0.8 copy.47
  175.0 3.1 %multiply_convert_fusion = bf16[512,1280]{1,0:T(8,128)(2,1)} fusion(f32[512,1280]{1,0:T(8,128)S(1)} %add.89, f32[512,1280]{1,0:T(8,128)} %get-tuple-element.21), kind=kLoop, calls=%fused_computation.3 | loop fusion | flops 1966080 | bytes 6553600 | tf_op jit(solution)/shard_map/convert_element_type | solution.py:262
  178.2 10.5 %all-to-all-done.3 = bf16[64,16,512]{2,1,0:T(8,128)(2,1)} async-done(((bf16[64,16,512]{2,1,0:T(8,128)(2,1)}), bf16[64,16,512]{2,1,0:T(8,128)(2,1)}, u32[]{:S(2)}, u32[]{:S(2)}) %all-to-all-start.3) | async-done | bytes 1048608 | tf_op jit(solution)/shard_map/all_to_all | solution.py:251
  188.7 1.4 convert_reduce_fusion
  190.1 0.1 fusion.1
  190.2 0.6 copy.74
  190.8 0.6 copy.75
  (38 shorter events, 0.4 us)
Async XLA Ops:
  5.5 3.9 %copy-start.6 = (s32[8,16]{1,0:T(8,128)S(1)}, s32[8,16]{1,0:T(8,128)}, u32[]{:S(2)}) copy-start(s32[8,16]{1,0:T(8,128)} %param.19) | copy-start | bytes 1540
  5.5 3.9 %copy-start.7 = (s32[128]{0:T(128)S(1)}, s32[128]{0:T(128)}, u32[]{:S(2)}) copy-start(s32[128]{0:T(128)} %param.18) | copy-start | bytes 1540
  5.5 40.7 %all-to-all-start = ((bf16[128,4,3072]{2,0,1:T(8,128)(2,1)}), bf16[128,4,3072]{2,0,1:T(8,128)(2,1)S(1)}, u32[]{:S(2)}, u32[]{:S(2)}) async-start(bf16[128,4,3072]{2,0,1:T(8,128)(2,1)} %pad_maximum_fusion), calls=%async_computation | async-start | bytes 6291456 | tf_op jit(solution)/shard_map/all_to_all | solution.py:179
  10.7 1.7 copy-start
  12.4 37.1 %copy-start.4 = (bf16[16,256]{1,0:T(8,128)(2,1)S(1)}, bf16[16,256]{1,0:T(8,128)(2,1)}, u32[]{:S(2)}) copy-start(bf16[16,256]{1,0:T(8,128)(2,1)} %param.17) | copy-start | bytes 24580
  12.4 37.1 %copy-start.5 = (bf16[16,256]{1,0:T(8,128)(2,1)S(1)}, bf16[16,256]{1,0:T(8,128)(2,1)}, u32[]{:S(2)}) copy-start(bf16[16,256]{1,0:T(8,128)(2,1)} %param.16) | copy-start | bytes 24580
  12.4 37.3 %copy-start.1 = (f32[10,512]{1,0:T(8,128)S(1)}, f32[10,512]{1,0:T(8,128)}, u32[]{:S(2)}) copy-start(f32[10,512]{1,0:T(8,128)} %param.15) | copy-start | bytes 61444
  46.2 7.2 %all-to-all-start.2 = ((f32[128,4,10]{0,2,1:T(8,128)}), f32[128,4,10]{0,2,1:T(8,128)S(1)}, u32[]{:S(2)}, u32[]{:S(2)}) async-start(f32[128,4,10]{0,2,1:T(8,128)} %reshape.205), calls=%async_computation.2 | async-start | bytes 65536 | tf_op jit(solution)/shard_map/all_to_all | solution.py:180
  49.6 27.3 %copy-start.2 = (s32[1,512]{1,0:T(1,128)}, s32[1,512]{1,0:T(1,128)S(1)}, u32[]{:S(2)}) copy-start(s32[1,512]{1,0:T(1,128)S(1)} %mul.99.lo_ref) | copy-start | bytes 6148
  49.7 27.2 %copy-start.3 = (s32[1,512]{1,0:T(1,128)}, s32[1,512]{1,0:T(1,128)S(1)}, u32[]{:S(2)}) copy-start(s32[1,512]{1,0:T(1,128)S(1)} %sub.68.lo_ref) | copy-start | bytes 6148
  54.6 71.7 %all-to-all-start.1 = ((bf16[64,16,512]{2,1,0:T(8,128)(2,1)}), bf16[64,16,512]{2,1,0:T(8,128)(2,1)}, u32[]{:S(2)}, u32[]{:S(2)}) async-start(bf16[64,16,512]{2,1,0:T(8,128)(2,1)} %broadcast_in_dim.36), calls=%async_computation.1 | async-start | bytes 2097152 | tf_op jit(solution)/shard_map/all_to_all | solution.py:231
  71.8 30.4 %collective-permute-start = (bf16[512,512]{1,0:T(8,128)(2,1)}, bf16[512,512]{1,0:T(8,128)(2,1)}, u32[]{:S(2)}, u32[]{:S(2)}) collective-permute-start(bf16[512,512]{1,0:T(8,128)(2,1)} %slice.64), channel_id=1, source_target_pairs={{0,4},{4,8},{8,12},{12,16},{16,20},{20,24},{24,28},{28,32},{32,36}... | collective-permute-start | bytes 1572872 | tf_op jit(solution)/shard_map/ppermute | solution.py:29
  121.5 22.5 %collective-permute-start.1 = (bf16[512,512]{1,0:T(8,128)(2,1)}, bf16[512,512]{1,0:T(8,128)(2,1)S(1)}, u32[]{:S(2)}, u32[]{:S(2)}) collective-permute-start(bf16[512,512]{1,0:T(8,128)(2,1)} %convert_element_type.56), channel_id=1, source_target_pairs={{4,0},{8,4},{12,8},{16,12},{20,16},{24,20},{28,24},{32,28},{36,32}... | collective-permute-start | bytes 1572872 | tf_op jit(solution)/shard_map/ppermute | solution.py:29
  146.8 41.9 %all-to-all-start.3 = ((bf16[64,16,512]{2,1,0:T(8,128)(2,1)}), bf16[64,16,512]{2,1,0:T(8,128)(2,1)}, u32[]{:S(2)}, u32[]{:S(2)}) async-start(bf16[64,16,512]{2,1,0:T(8,128)(2,1)} %bitcast.56), calls=%async_computation.3 | async-start | bytes 2097152 | tf_op jit(solution)/shard_map/all_to_all | solution.py:251
  167.0 4.7 %slice-start = ((f32[512,2,2,128]{3,2,1,0:T(2,128)}), f32[512,2,1,128]{3,2,1,0:T(1,128)S(1)}, s32[]{:S(2)}) async-start(f32[512,2,2,128]{3,2,1,0:T(2,128)} %reshape.208), calls=%async_computation.4 | async-start | bytes 1048576 | tf_op jit(solution)/shard_map/slice | solution.py:263
